TPU v7x, 256 devices: a whole 4x4x8 slice. The times are simulated.
256 devices in a mesh: req: 32 (over x, z), tp: 8 (over y, core).
Axes of the slice: x: 4, y: 4, z: 8, core: 2. Of those that a mesh axis runs over, the one named last changes fastest.
Arguments:
- hidden: bfloat16 [4096, 2048], P('req', 'tp'), may hold values from -3 to 3
- lengths: int32 [4096], P('req'), may hold values from 1 to 1921, as said below
- routes: int32 [4096, 6], P('req'), may hold values from 0 to 63, all different within a row; in each aligned block of 128 rows (0 to 127, 128 to 255, ...) at most 32 rows name the same one
- latent_cache: bfloat16 [65536, 576], P('req'), may hold values from -400 to 400
- attention_gain: bfloat16 [2048], replicated, may hold values from 0.099609375 to 1.8984375
- query_weight: bfloat16 [2048, 3072], P(None, 'tp'), may hold values from -0.125 to 0.125
- latent_weight: bfloat16 [2048, 576], P(None, 'tp'), may hold values from -0.125 to 0.125
- latent_gain: bfloat16 [512], replicated, may hold values from 0.099609375 to 1.8984375
- key_absorb: bfloat16 [16, 128, 512], P('tp'), may hold values from -0.5 to 0.5
- value_absorb: bfloat16 [16, 512, 128], P('tp'), may hold values from -0.5 to 0.5
- output_weight: bfloat16 [2048, 2048], P('tp'), may hold values from -0.75 to 0.75
- feedforward_gain: bfloat16 [2048], replicated, may hold values from 0.099609375 to 1.8984375
- router_weight: bfloat16 [2048, 64], replicated, may hold values from -0.0625 to 0.0625
- expert_gate: bfloat16 [64, 2048, 1408], P('req', None, 'tp'), may hold values from -0.25 to 0.25
- expert_up: bfloat16 [64, 2048, 1408], P('req', None, 'tp'), may hold values from -0.25 to 0.25
- expert_down: bfloat16 [64, 1408, 2048], P('req', 'tp'), may hold values from -0.4375 to 0.4375
- shared_gate: bfloat16 [2048, 1408], P(None, 'tp'), may hold values from -0.25 to 0.25
- shared_up: bfloat16 [2048, 1408], P(None, 'tp'), may hold values from -0.25 to 0.25
- shared_down: bfloat16 [1408, 2048], P('tp'), may hold values from -0.21875 to 0.21875
Outputs:
- next_hidden: bfloat16 [4096, 2048], P('req', 'tp')
- new_rows: bfloat16 [4096, 576], P('req')
Inputs may be any that keep to these rules, and one draw needn't show every extreme that they name: The lengths of the 128 requests of one index of req (aligned blocks of 128) sum to at most 2048, and to exactly 2048 on some index, where one request holds 1921. `routes`: among the rows of one index of req, no expert is named by more than 32 rows, a bound that some block reaches.
All inputs are finite; a program needn't handle non-finite values.
Results may differ from a plain program's by a relative error of at most 0.023.
The roundings to bfloat16 on the way count: a program that leaves them out, or rounds other values in their place, can miss the bound.
Values may be sent and summed in bfloat16 or wider, within the bound.
No kernel may reach another device: no remote copies, remote signals or barrier semaphores. Data moves between devices by JAX's collectives and lax.ppermute only.
A program may use at most 128 MiB of HBM per device.

v0:
```python
import jax
import jax.numpy as jnp
from jax import lax
from jax.sharding import PartitionSpec as P

rope_base = 50000.0
route_scale = 2.446
norm_eps = 1e-06


def rms_norm(values, gains):
    widened = values.astype(jnp.float32)
    factor = lax.rsqrt(jnp.mean(widened * widened, axis=-1, keepdims=True) + norm_eps)
    return widened * factor * gains.astype(jnp.float32)


def rotate(values, positions):
    half_width = values.shape[-1] // 2
    exponent = jnp.arange(half_width, dtype=jnp.float32) * (2.0 / values.shape[-1])
    angles = positions[..., None] * jnp.power(rope_base, -exponent)
    cosine = jnp.cos(angles)
    sine_part = jnp.sin(angles)
    first_half = values[..., :half_width]
    second_half = values[..., half_width:]
    return jnp.concatenate(
        [
            first_half * cosine - second_half * sine_part,
            first_half * sine_part + second_half * cosine,
        ],
        axis=-1,
    )


def attend(queries, cache_rows, lengths, new_rows, score_scale, latent_width):
    starts = jnp.cumsum(lengths) - lengths
    places = jnp.arange(cache_rows.shape[0], dtype=jnp.int32)
    inside = (places[None, :] >= starts[:, None]) & (places[None, :] < (starts + lengths)[:, None])
    scores = (
        jnp.einsum("rhk,jk->rhj", queries, cache_rows, preferred_element_type=jnp.float32)
        * score_scale
    )
    own_score = (
        jnp.einsum("rhk,rk->rh", queries, new_rows, preferred_element_type=jnp.float32)
        * score_scale
    )
    highest = jnp.maximum(
        jnp.max(jnp.where(inside[:, None, :], scores, -jnp.inf), axis=-1), own_score
    )
    weights = jnp.where(inside[:, None, :], jnp.exp(scores - highest[..., None]), 0.0)
    own_weight = jnp.exp(own_score - highest)
    totals = jnp.sum(weights, axis=-1) + own_weight
    probabilities = (weights / totals[..., None]).astype(jnp.bfloat16)
    own_prob = (own_weight / totals).astype(jnp.bfloat16)
    summed = jnp.einsum(
        "rhj,jl->rhl",
        probabilities,
        cache_rows[:, :latent_width],
        preferred_element_type=jnp.float32,
    )
    summed = summed + own_prob.astype(jnp.float32)[..., None] * new_rows[
        :, None, :latent_width
    ].astype(jnp.float32)
    return summed.astype(jnp.bfloat16)


def shards(
    hidden,
    lengths,
    routes,
    latent_cache,
    attention_gain,
    query_weight,
    latent_weight,
    latent_gain,
    key_absorb,
    value_absorb,
    output_weight,
    feedforward_gain,
    router_weight,
    expert_gate,
    expert_up,
    expert_down,
    shared_gate,
    shared_up,
    shared_down,
):
    token_count = hidden.shape[0]
    owner_count = lax.axis_size("req")
    column_width = hidden.shape[1]
    column_start = lax.axis_index("tp") * column_width
    heads_here = key_absorb.shape[0]
    nope_width = key_absorb.shape[1]
    latent_width = key_absorb.shape[2]
    whole = lax.all_gather(hidden, "tp", axis=1, tiled=True)
    normed = rms_norm(whole, attention_gain).astype(jnp.bfloat16)
    projected = jnp.dot(normed, query_weight, preferred_element_type=jnp.float32).reshape(
        token_count, heads_here, -1
    )
    rope_width = projected.shape[2] - nope_width
    positions = lengths.astype(jnp.float32)
    query_nope = projected[..., :nope_width].astype(jnp.bfloat16)
    query_rope = rotate(projected[..., nope_width:], positions[:, None]).astype(jnp.bfloat16)
    query_latent = jnp.einsum(
        "thn,hnl->thl", query_nope, key_absorb, preferred_element_type=jnp.float32
    ).astype(jnp.bfloat16)
    latent_part = jnp.dot(normed, latent_weight, preferred_element_type=jnp.float32).astype(
        jnp.bfloat16
    )
    latent_raw = lax.all_gather(latent_part, "tp", axis=1, tiled=True)
    latent_new = rms_norm(latent_raw[:, :latent_width], latent_gain)
    key_new = rotate(latent_raw[:, latent_width:].astype(jnp.float32), positions)
    new_rows = jnp.concatenate([latent_new, key_new], axis=-1).astype(jnp.bfloat16)
    queries = jnp.concatenate([query_latent, query_rope], axis=-1)
    attended = attend(
        queries, latent_cache, lengths, new_rows, (nope_width + rope_width) ** (-0.5), latent_width
    )
    head_values = jnp.einsum(
        "thl,hlv->thv", attended, value_absorb, preferred_element_type=jnp.float32
    ).astype(jnp.bfloat16)
    attention = jnp.dot(
        head_values.reshape(token_count, -1), output_weight, preferred_element_type=jnp.float32
    )
    total_attention = lax.psum(attention, "tp")
    mixed = (whole.astype(jnp.float32) + total_attention).astype(jnp.bfloat16)
    mixed_columns = lax.dynamic_slice_in_dim(mixed, column_start, column_width, 1)
    expert_in = rms_norm(mixed, feedforward_gain).astype(jnp.bfloat16)
    logits = jnp.dot(expert_in, router_weight, preferred_element_type=jnp.float32)
    expert_count = router_weight.shape[1]
    top_count = routes.shape[1]
    per_owner = expert_count // owner_count
    slot_count = max(2, 8 * token_count * top_count // (3 * expert_count))
    chosen = jnp.take_along_axis(jax.nn.sigmoid(logits), routes, axis=1)
    route_weights = chosen / jnp.sum(chosen, axis=1, keepdims=True) * route_scale
    expert_ids = routes.reshape(-1)
    onehot = (expert_ids[:, None] == jnp.arange(expert_count, dtype=jnp.int32)[None, :]).astype(
        jnp.int32
    )
    earlier = jnp.cumsum(onehot, axis=0) - onehot
    slot_index = jnp.sum(earlier * onehot, axis=1)
    slot_places = (expert_ids * slot_count + slot_index).reshape(token_count, top_count)
    slot_total = expert_count * slot_count
    placed = slot_places[None, :, :] == jnp.arange(slot_total, dtype=jnp.int32)[:, None, None]
    gather_matrix = jnp.any(placed, axis=2).astype(jnp.bfloat16)
    combine_matrix = jnp.sum(jnp.where(placed, route_weights[None, :, :], 0.0), axis=2).T
    outgoing = jnp.dot(gather_matrix, expert_in, preferred_element_type=jnp.float32).astype(
        jnp.bfloat16
    )
    outgoing = outgoing.reshape(owner_count, per_owner, slot_count, expert_in.shape[1])
    slab = lax.all_to_all(outgoing, "req", split_axis=0, concat_axis=0, tiled=True)
    gate_part = jnp.einsum("oesd,edf->oesf", slab, expert_gate, preferred_element_type=jnp.float32)
    up_part = jnp.einsum("oesd,edf->oesf", slab, expert_up, preferred_element_type=jnp.float32)
    inner_units = (jax.nn.silu(gate_part) * up_part).astype(jnp.bfloat16)
    partial_out = jnp.einsum(
        "oesf,efd->oesd", inner_units, expert_down, preferred_element_type=jnp.float32
    )
    results = lax.psum_scatter(partial_out, "tp", scatter_dimension=3, tiled=True)
    shared_inner = (
        jax.nn.silu(jnp.dot(expert_in, shared_gate, preferred_element_type=jnp.float32))
        * jnp.dot(expert_in, shared_up, preferred_element_type=jnp.float32)
    ).astype(jnp.bfloat16)
    shared_part = jnp.dot(shared_inner, shared_down, preferred_element_type=jnp.float32)
    returned = lax.all_to_all(results, "req", split_axis=0, concat_axis=0, tiled=True)
    routed = jnp.dot(
        combine_matrix, returned.reshape(slot_total, column_width), precision=lax.Precision.HIGHEST
    )
    shared_columns = lax.psum_scatter(shared_part, "tp", scatter_dimension=1, tiled=True)
    next_hidden = (mixed_columns.astype(jnp.float32) + routed + shared_columns).astype(jnp.bfloat16)
    return (next_hidden, new_rows)


def solution(mesh):
    in_specs = (
        P("req", "tp"),
        P("req"),
        P("req", None),
        P("req", None),
        P(),
        P(None, "tp"),
        P(None, "tp"),
        P(),
        P("tp", None, None),
        P("tp", None, None),
        P("tp", None),
        P(),
        P(),
        P("req", None, "tp"),
        P("req", None, "tp"),
        P("req", "tp", None),
        P(None, "tp"),
        P(None, "tp"),
        P("tp", None),
    )
    out_specs = (P("req", "tp"), P("req", None))
    return jax.shard_map(shards, mesh=mesh, in_specs=in_specs, out_specs=out_specs, check_vma=False)
```

profile of v0, /device:TPU:32, one launch (start us, length us, event | category | flops | bytes accessed | tf_op | source)
XLA Modules:
  0.0 508.9 jit_solution(7842593407011253523)
XLA Ops:
  7.2 14.0 %all_gather.6 = bf16[128,2048]{1,0:T(8,128)(2,1)S(1)} all-gather(bf16[128,256]{1,0:T(8,128)(2,1)} %param.19), channel_id=1, replica_groups=mesh['req'=32,'tp'=8] {'tp'}, dimensions={1}, use_global_device_ids=true | all-gather | bytes 589824 | tf_op jit(solution)/shard_map/all_gather | solution.py:94
  21.2 0.2 fusion.45
  21.4 0.7 convert_element_type.92
  22.1 1.3 convolution_convert_fusion.2
  23.4 12.8 %all_gather.7 = bf16[128,576]{0,1:T(8,128)(2,1)S(1)} all-gather(bf16[128,72]{0,1:T(8,128)(2,1)S(1)} %convolution_convert_fusion.2), channel_id=1, replica_groups=mesh['req'=32,'tp'=8] {'tp'}, dimensions={1}, use_global_device_ids=true | all-gather | bytes 165888 | tf_op jit(solution)/shard_map/all_gather | solution.py:109
  36.5 0.2 reduce-window.18
  36.8 0.5 copy-done.8
  37.3 0.5 fusion.94
  37.8 0.1 fusion.62
  38.0 0.8 copy.114
  38.8 0.1 subtract_convert_fusion.1
  39.0 0.1 copy.140
  39.1 0.7 copy.109
  39.9 0.7 copy.111
  40.6 0.8 fusion.70
  41.6 0.3 fusion.31
  41.9 1.1 fusion.56
  43.0 0.9 subtract_convert_fusion
  43.9 0.2 multiply_reduce_fusion
  44.1 2.9 select_reduce_fusion.1
  47.0 1.3 copy-done.2
  48.3 0.6 fusion.13
  48.9 3.5 fusion.34
  52.5 1.4 fusion.95
  54.0 0.1 eq.42
  54.3 1.8 reduce-window.19
  56.1 0.3 slice_reduce_fusion
  56.4 0.1 fusion.67
  56.8 1.1 fusion.4
  57.9 65.9 %all-reduce.2.cloned.1.call-done = f32[128,2048]{1,0:T(8,128)} async-done(((f32[128,2048]{1,0:T(8,128)}), f32[128,2048]{1,0:T(8,128)}) %all-reduce.2.cloned.1.call-update) | async-done | bytes 1048592 | tf_op jit(solution)/shard_map/psum | solution.py:123
  123.8 1.5 fusion.42
  125.3 2.4 convolution_convert_fusion
  127.7 194.0 %all_to_all.10 = bf16[32,2,32,2048]{3,2,1,0:T(8,128)(2,1)S(1)} all-to-all(bf16[32,2,32,2048]{3,2,1,0:T(8,128)(2,1)S(1)} %bitcast.104), channel_id=1, replica_groups=mesh['req'=32,'tp'=8] {'req'}, dimensions={0} | all-to-all | bytes 16777216 | tf_op jit(solution)/shard_map/all_to_all | solution.py:149
  321.7 3.2 copy-done.1
  324.9 3.7 fusion.2
  328.7 15.2 %convolution_bitcast_fusion = f32[32,2,32,2048]{3,2,0,1:T(8,128)} fusion(f32[2,32,32,176]{3,2,1,0:T(8,128)} %fusion.2, bf16[32,2,32,2048]{3,2,1,0:T(8,128)(2,1)} %copy-done.1, bf16[2,176,2048]{2,1,0:T(8,128)(2,1)} %param.34, bf16[2,2048,176]{1,2,0:T(8,128)(2,1)} %param.33), kind=kOutput, calls=%fused_computation.6 | convolution fusion | flops 2954952704 | bytes 29491200 | tf_op jit(solution)/shard_map/oesf,efd->oesd/dot_general | solution.py:153
  343.9 91.3 %reduce-scatter.3.cloned.1.call-done = f32[32,2,32,256]{3,2,0,1:T(8,128)} async-done(((f32[32,2,32,2048]{3,2,0,1:T(8,128)}), f32[32,2,32,256]{3,2,0,1:T(8,128)}) %reduce-scatter.3.cloned.1.call-update) | async-done | bytes 2097168 | tf_op jit(solution)/shard_map/reduce_scatter | solution.py:156
  435.2 3.2 copy.124
  438.4 10.2 %all-to-all-start.1 = ((f32[32,2,32,256]{3,2,1,0:T(8,128)}), f32[32,2,32,256]{3,2,1,0:T(8,128)}, u32[]{:S(2)}, u32[]{:S(2)}) async-start(f32[32,2,32,256]{3,2,1,0:T(8,128)} %copy.124), calls=%async_computation.2 | async-start | bytes 4194304 | tf_op jit(solution)/shard_map/all_to_all | solution.py:162
  448.7 1.5 fusion.88
  450.3 3.2 fusion.38
  453.6 0.1 reshape.227
  453.7 0.4 fusion.41
  454.1 5.1 %gather_fusion = f32[768]{0:T(1024)S(1)} fusion(f32[128,64]{0,1:T(8,128)S(1)} %fusion.41, s32[768]{0:T(1024)S(1)} %reshape.227), kind=kCustom, calls=%fused_computation | custom fusion | bytes 12288 | tf_op jit(solution)/shard_map/jit(take_along_axis)/gather | solution.py:132
  459.5 1.8 select_reduce_fusion
  461.3 26.9 %reduce-scatter.5.cloned.1.call-done = f32[128,256]{1,0:T(8,128)} async-done(((f32[128,2048]{1,0:T(8,128)}), f32[128,256]{1,0:T(8,128)}) %reduce-scatter.5.cloned.1.call-update) | async-done | bytes 131088 | tf_op jit(solution)/shard_map/reduce_scatter | solution.py:166
  488.1 9.9 %all-to-all-done.1 = f32[32,2,32,256]{3,2,1,0:T(8,128)} async-done(((f32[32,2,32,256]{3,2,1,0:T(8,128)}), f32[32,2,32,256]{3,2,1,0:T(8,128)}, u32[]{:S(2)}, u32[]{:S(2)}) %all-to-all-start.1) | async-done | bytes 2097184 | tf_op jit(solution)/shard_map/all_to_all | solution.py:162
  498.0 4.3 fusion.33
  (60 shorter events, 1.7 us)
Async XLA Ops:
  7.2 33.4 %copy-start = (bf16[2048,384]{1,0:T(8,128)(2,1)S(1)}, bf16[2048,384]{1,0:T(8,128)(2,1)}, u32[]{:S(2)}) copy-start(bf16[2048,384]{1,0:T(8,128)(2,1)} %param.24) | copy-start | bytes 4718596
  7.2 29.2 %copy-start.11 = (bf16[512]{0:T(512)(128)(2,1)S(1)}, bf16[512]{0:T(512)(128)(2,1)}, u32[]{:S(2)}) copy-start(bf16[512]{0:T(512)(128)(2,1)} %param.26) | copy-start | bytes 3076
  7.2 29.2 %copy-start.10 = (s32[128]{0:T(128)S(1)}, s32[128]{0:T(128)}, u32[]{:S(2)}) copy-start(s32[128]{0:T(128)} %param.20) | copy-start | bytes 1540
  7.2 116.6 %all-reduce.2.cloned.1.call-start = ((), (), s32[]{:S(2)}) async-start(), calls=%async_computation.4 | async-start | bytes 2097152 | tf_op jit(solution)/shard_map/psum | solution.py:123
  36.8 0.6 copy-start.8
  38.0 3.6 copy-start.6
  39.0 4.0 copy-start.5
  47.0 1.4 copy-start.2
  48.9 3.5 copy-start.3
  52.4 1.5 copy-start.7
  52.5 4.3 copy-start.9
  53.9 381.4 %reduce-scatter.3.cloned.1.call-start = ((), (), s32[]{:S(2)}) async-start(), calls=%async_computation.5 | async-start | bytes 18874368 | tf_op jit(solution)/shard_map/reduce_scatter | solution.py:156
  127.7 197.2 %copy-start.12 = (bf16[2,2048,176]{1,2,0:T(8,128)(2,1)S(1)}, bf16[2,2048,176]{1,2,0:T(8,128)(2,1)}, u32[]{:S(2)}) copy-start(bf16[2,2048,176]{1,2,0:T(8,128)(2,1)} %param.32) | copy-start | bytes 4325380
  321.7 3.2 copy-start.1
  438.4 11.8 %copy-start.4 = (bf16[176,2048]{1,0:T(8,128)(2,1)S(1)}, bf16[176,2048]{1,0:T(8,128)(2,1)}, u32[]{:S(2)}) copy-start(bf16[176,2048]{1,0:T(8,128)(2,1)} %param.37) | copy-start | bytes 2162692
  438.4 59.6 %all-to-all-start.1 = ((f32[32,2,32,256]{3,2,1,0:T(8,128)}), f32[32,2,32,256]{3,2,1,0:T(8,128)}, u32[]{:S(2)}, u32[]{:S(2)}) async-start(f32[32,2,32,256]{3,2,1,0:T(8,128)} %copy.124), calls=%async_computation.2 | async-start | bytes 4194304 | tf_op jit(solution)/shard_map/all_to_all | solution.py:162
  448.7 39.5 %reduce-scatter.5.cloned.1.call-start = ((), (), s32[]{:S(2)}) async-start(), calls=%async_computation.6 | async-start | bytes 1179648 | tf_op jit(solution)/shard_map/reduce_scatter | solution.py:166
  450.3 3.5 copy-start.13
Sparse Core Ops, SparseCore 0:
  54.0 69.7 all-reduce.1
  344.0 91.1 reduce-scatter.2
  453.6 34.5 reduce-scatter.4
where the time goes:
time: 510 us; the launch traced here: 509 us
  blocking collectives  221 us (43%)
  waiting for transfers between devices  194 us (38%)
  matrix products  40.9 us (8%)
  local copies, waits for them, and re-layouts  17.5 us (3%)
  between operations  14.1 us (3%)
  other arithmetic  11.2 us (2%)
  starting transfers between devices  10.4 us (2%)
    all_to_all x1, blocking collectives, shards(): lax.all_to_all(outgoing, 'req', split_axis=0, concat_axis=0, tiled=True)  194 us
    reduce_scatter x1, waiting for transfers between devices, shards(): lax.psum_scatter(partial_out, 'tp', scatter_dimension=3, tiled=True)  91.3 us
    psum x1, waiting for transfers between devices, shards(): total_attention = lax.psum(attention, 'tp')  65.9 us
    reduce_scatter x1, waiting for transfers between devices, shards(): lax.psum_scatter(shared_part, 'tp', scatter_dimension=1, tiled=True)  26.9 us
    dot_general x1, matrix products, shards(): jnp.einsum('oesf,efd->oesd', inner_units, expert_down, preferred_element_...  15.2 us
    all_gather x1, blocking collectives, shards(): whole = lax.all_gather(hidden, 'tp', axis=1, tiled=True)  14 us
    all_gather x1, blocking collectives, shards(): latent_raw = lax.all_gather(latent_part, 'tp', axis=1, tiled=True)  12.8 us
    all_to_all x1, starting transfers between devices, shards(): lax.all_to_all(results, 'req', split_axis=0, concat_axis=0, tiled=True)  10.2 us
  transfers between devices with their start and end apart: 4, of which 4 were waited for; matrix products, arithmetic and copies ran while one was open for 3% of the time, Pallas kernels for 0%

commit v1 on v0

--- a/solution.py
+++ b/solution.py
@@ -120,9 +120,9 @@
     attention = jnp.dot(
         head_values.reshape(token_count, -1), output_weight, preferred_element_type=jnp.float32
     )
-    total_attention = lax.psum(attention, "tp")
-    mixed = (whole.astype(jnp.float32) + total_attention).astype(jnp.bfloat16)
-    mixed_columns = lax.dynamic_slice_in_dim(mixed, column_start, column_width, 1)
+    attention_columns = lax.psum_scatter(attention, "tp", scatter_dimension=1, tiled=True)
+    mixed_columns = (hidden.astype(jnp.float32) + attention_columns).astype(jnp.bfloat16)
+    mixed = lax.all_gather(mixed_columns, "tp", axis=1, tiled=True)
     expert_in = rms_norm(mixed, feedforward_gain).astype(jnp.bfloat16)
     logits = jnp.dot(expert_in, router_weight, preferred_element_type=jnp.float32)
     expert_count = router_weight.shape[1]
@@ -142,13 +142,20 @@
     placed = slot_places[None, :, :] == jnp.arange(slot_total, dtype=jnp.int32)[:, None, None]
     gather_matrix = jnp.any(placed, axis=2).astype(jnp.bfloat16)
     combine_matrix = jnp.sum(jnp.where(placed, route_weights[None, :, :], 0.0), axis=2).T
-    outgoing = jnp.dot(gather_matrix, expert_in, preferred_element_type=jnp.float32).astype(
+    expert_columns = lax.dynamic_slice_in_dim(expert_in, column_start, column_width, 1)
+    outgoing = jnp.dot(gather_matrix, expert_columns, preferred_element_type=jnp.float32).astype(
         jnp.bfloat16
     )
-    outgoing = outgoing.reshape(owner_count, per_owner, slot_count, expert_in.shape[1])
-    slab = lax.all_to_all(outgoing, "req", split_axis=0, concat_axis=0, tiled=True)
-    gate_part = jnp.einsum("oesd,edf->oesf", slab, expert_gate, preferred_element_type=jnp.float32)
-    up_part = jnp.einsum("oesd,edf->oesf", slab, expert_up, preferred_element_type=jnp.float32)
+    outgoing = outgoing.reshape(owner_count, per_owner, slot_count, column_width)
+    slab_columns = lax.all_to_all(outgoing, "req", split_axis=0, concat_axis=0, tiled=True)
+    slab = lax.all_gather(slab_columns, "tp", axis=0, tiled=False)
+    tp_count = slab.shape[0]
+    gate_blocks = expert_gate.reshape(per_owner, tp_count, column_width, -1)
+    up_blocks = expert_up.reshape(per_owner, tp_count, column_width, -1)
+    gate_part = jnp.einsum(
+        "toesc,etcf->oesf", slab, gate_blocks, preferred_element_type=jnp.float32
+    )
+    up_part = jnp.einsum("toesc,etcf->oesf", slab, up_blocks, preferred_element_type=jnp.float32)
     inner_units = (jax.nn.silu(gate_part) * up_part).astype(jnp.bfloat16)
     partial_out = jnp.einsum(
         "oesf,efd->oesd", inner_units, expert_down, preferred_element_type=jnp.float32

time: 510 us -> 373 us (0.73)
  blocking collectives: 221 us -> 78.5 us
  waiting for transfers between devices: 194 us -> 211 us
  matrix products: 40.9 us -> 35.6 us
    all_to_all x1, blocking collectives: 194 us -> 38.7 us  [shards(): lax.all_to_all(outgoing, 'req', split_axis=0, concat_axis=0, tiled=True)]
    psum x1 -> x0, waiting for transfers between devices: 65.9 us -> none  [shards(): total_attention = lax.psum(attention, 'tp')]
    all_gather x0 -> x1, waiting for transfers between devices: none -> 45.3 us  [shards(): slab = lax.all_gather(slab_columns, 'tp', axis=0, tiled=False)]
    reduce_scatter x0 -> x1, waiting for transfers between devices: none -> 32 us  [shards(): lax.psum_scatter(attention, 'tp', scatter_dimension=1, tiled=True)]
    all_gather x0 -> x1, blocking collectives: none -> 13.1 us  [shards(): mixed = lax.all_gather(mixed_columns, 'tp', axis=1, tiled=True)]
    dot_general x1, matrix products: 15.2 us -> 8.08 us  [shards(): jnp.einsum('oesf,efd->oesd', inner_units, expert_down, preferred_element_...]
  transfers between devices with their start and end apart: 4 -> 5, of which waited for: 4 -> 5; matrix products, arithmetic and copies ran while one was open for 3% -> 5% of each run, Pallas kernels for 0% -> 0%
where the time goes in v1:
time: 373 us
  waiting for transfers between devices  211 us (57%)
  blocking collectives  78.5 us (21%)
  matrix products  35.6 us (10%)
  local copies, waits for them, and re-layouts  14.3 us (4%)
  between operations  14.3 us (4%)
  starting transfers between devices  10.6 us (3%)
  other arithmetic  8.92 us (2%)
    reduce_scatter x1, waiting for transfers between devices, shards(): lax.psum_scatter(partial_out, 'tp', scatter_dimension=3, tiled=True)  94.7 us
    all_gather x1, waiting for transfers between devices, shards(): slab = lax.all_gather(slab_columns, 'tp', axis=0, tiled=False)  45.3 us
    all_to_all x1, blocking collectives, shards(): lax.all_to_all(outgoing, 'req', split_axis=0, concat_axis=0, tiled=True)  38.7 us
    reduce_scatter x1, waiting for transfers between devices, shards(): lax.psum_scatter(attention, 'tp', scatter_dimension=1, tiled=True)  32 us
    reduce_scatter x1, waiting for transfers between devices, shards(): lax.psum_scatter(shared_part, 'tp', scatter_dimension=1, tiled=True)  27.9 us
    all_gather x1, blocking collectives, shards(): whole = lax.all_gather(hidden, 'tp', axis=1, tiled=True)  14 us
    all_gather x1, blocking collectives, shards(): mixed = lax.all_gather(mixed_columns, 'tp', axis=1, tiled=True)  13.1 us
    all_gather x1, blocking collectives, shards(): latent_raw = lax.all_gather(latent_part, 'tp', axis=1, tiled=True)  12.8 us
  transfers between devices with their start and end apart: 5, of which 5 were waited for; matrix products, arithmetic and copies ran while one was open for 5% of the time, Pallas kernels for 0%

profile of v1, /device:TPU:32, one launch (start us, length us, event | category | flops | bytes accessed | tf_op | source)
XLA Modules:
  0.0 372.7 jit_solution(6910081507702166990)
XLA Ops:
  7.2 14.0 %all_gather.15 = bf16[128,2048]{1,0:T(8,128)(2,1)S(1)} all-gather(bf16[128,256]{1,0:T(8,128)(2,1)} %param.19), channel_id=1, replica_groups=mesh['req'=32,'tp'=8] {'tp'}, dimensions={1}, use_global_device_ids=true | all-gather | bytes 589824 | tf_op jit(solution)/shard_map/all_gather | solution.py:94
  21.2 0.2 fusion.37
  21.4 0.7 convert_element_type.95
  22.1 1.3 convolution_convert_fusion.2
  23.4 12.8 %all_gather.16 = bf16[128,576]{0,1:T(8,128)(2,1)S(1)} all-gather(bf16[128,72]{0,1:T(8,128)(2,1)S(1)} %convolution_convert_fusion.2), channel_id=1, replica_groups=mesh['req'=32,'tp'=8] {'tp'}, dimensions={1}, use_global_device_ids=true | all-gather | bytes 165888 | tf_op jit(solution)/shard_map/all_gather | solution.py:109
  36.5 0.2 reduce-window.18
  36.8 0.1 fusion.56
  37.0 0.1 subtract_convert_fusion.1
  37.2 0.1 copy.152
  37.5 0.4 copy-done.9
  38.0 0.8 fusion.64
  39.0 0.3 fusion.26
  39.3 0.5 fusion.50
  39.8 0.2 multiply_reduce_fusion
  40.0 2.9 select_reduce_fusion.1
  42.9 1.3 copy-done.1
  44.2 0.6 fusion.13
  44.8 3.5 fusion.29
  48.3 1.3 fusion.83
  50.2 1.8 reduce-window.19
  52.0 0.3 slice_reduce_fusion
  52.3 0.1 fusion.61
  52.6 1.9 fusion.4
  54.5 32.0 %reduce-scatter.4.cloned.1.call-done = f32[128,256]{1,0:T(8,128)} async-done(((f32[128,2048]{1,0:T(8,128)}), f32[128,256]{1,0:T(8,128)}) %reduce-scatter.4.cloned.1.call-update) | async-done | bytes 131088 | tf_op jit(solution)/shard_map/reduce_scatter | solution.py:123
  86.5 1.0 add_convert_fusion
  87.5 13.1 %all_gather.17 = bf16[128,2048]{1,0:T(8,128)(2,1)S(1)} all-gather(bf16[128,256]{1,0:T(8,128)(2,1)S(1)} %add_convert_fusion), channel_id=1, replica_groups=mesh['req'=32,'tp'=8] {'tp'}, dimensions={1}, use_global_device_ids=true | all-gather | bytes 589824 | tf_op jit(solution)/shard_map/all_gather | solution.py:125
  100.6 0.2 fusion.40
  100.8 0.2 fusion.42
  101.0 0.4 convolution_convert_fusion
  101.5 38.7 %all_to_all.10 = bf16[32,2,32,256]{3,2,1,0:T(8,128)(2,1)} all-to-all(bf16[32,2,32,256]{3,2,1,0:T(8,128)(2,1)S(1)} %bitcast.117), channel_id=1, replica_groups=mesh['req'=32,'tp'=8] {'req'}, dimensions={0} | all-to-all | bytes 2097152 | tf_op jit(solution)/shard_map/all_to_all | solution.py:150
  140.1 0.2 reduce-scatter.6.cloned.1.call-start
  140.4 1.6 copy.155
  142.0 0.4 copy.154
  142.5 45.3 %all-gather.3.cloned.1.call-done = bf16[256,2,32,256]{3,2,1,0:T(8,128)(2,1)} async-done(((bf16[32,2,32,256]{3,2,1,0:T(8,128)(2,1)}), bf16[256,2,32,256]{3,2,1,0:T(8,128)(2,1)}) %all-gather.3.cloned.1.call-update) | async-done | bytes 8388624 | tf_op jit(solution)/shard_map/all_gather | solution.py:151
  187.8 6.2 %fusion = f32[2,32,32,176,1]{3,2,1,0,4:T(8,128)S(1)} fusion(bf16[8,32,2,32,256]{4,3,2,1,0:T(8,128)(2,1)} %bitcast.127, bf16[2,8,256,176,1]{2,1,3,0,4:T(8,128)(2,1)} %bitcast.121), kind=kOutput, calls=%fused_computation.1 | convolution fusion | flops 1476395008 | bytes 11272192 | tf_op jit(solution)/shard_map/toesc,etcf->oesf/dot_general | solution.py:158
  194.1 2.3 fusion.2
  196.4 8.1 %convolution_bitcast_fusion = f32[32,2,32,2048]{3,2,0,1:T(8,128)} fusion(bf16[2,176,2048]{2,1,0:T(8,128)(2,1)S(1)} %copy-done.4, f32[2,32,32,176,1]{3,2,1,0,4:T(8,128)S(1)} %fusion, f32[2,32,32,176,1]{3,2,1,0,4:T(8,128)S(1)} %fusion.2), kind=kOutput, calls=%fused_computation.5 | convolution fusion | flops 1478557696 | bytes 21102592 | tf_op jit(solution)/shard_map/oesf,efd->oesd/dot_general | solution.py:160
  204.5 94.7 %reduce-scatter.6.cloned.1.call-done = f32[32,2,32,256]{3,2,0,1:T(8,128)} async-done(((f32[32,2,32,2048]{3,2,0,1:T(8,128)}), f32[32,2,32,256]{3,2,0,1:T(8,128)}) %reduce-scatter.6.cloned.1.call-update) | async-done | bytes 2097168 | tf_op jit(solution)/shard_map/reduce_scatter | solution.py:163
  299.2 3.2 copy.129
  302.4 10.2 %all-to-all-start.1 = ((f32[32,2,32,256]{3,2,1,0:T(8,128)}), f32[32,2,32,256]{3,2,1,0:T(8,128)}, u32[]{:S(2)}, u32[]{:S(2)}) async-start(f32[32,2,32,256]{3,2,1,0:T(8,128)} %copy.129), calls=%async_computation.3 | async-start | bytes 4194304 | tf_op jit(solution)/shard_map/all_to_all | solution.py:169
  312.7 1.0 fusion.84
  313.7 3.0 fusion.33
  317.1 0.3 fusion.36
  317.4 5.1 %gather_fusion = f32[768]{0:T(1024)S(1)} fusion(f32[128,64]{0,1:T(8,128)S(1)} %fusion.36, s32[768]{0:T(1024)S(1)} %reshape.235), kind=kCustom, calls=%fused_computation | custom fusion | bytes 12288 | tf_op jit(solution)/shard_map/jit(take_along_axis)/gather | solution.py:132
  322.8 0.8 select_reduce_fusion
  323.6 27.9 %reduce-scatter.8.cloned.1.call-done = f32[128,256]{1,0:T(8,128)} async-done(((f32[128,2048]{1,0:T(8,128)}), f32[128,256]{1,0:T(8,128)}) %reduce-scatter.8.cloned.1.call-update) | async-done | bytes 131088 | tf_op jit(solution)/shard_map/reduce_scatter | solution.py:173
  351.5 10.5 %all-to-all-done.1 = f32[32,2,32,256]{3,2,1,0:T(8,128)} async-done(((f32[32,2,32,256]{3,2,1,0:T(8,128)}), f32[32,2,32,256]{3,2,1,0:T(8,128)}, u32[]{:S(2)}, u32[]{:S(2)}) %all-to-all-start.1) | async-done | bytes 2097184 | tf_op jit(solution)/shard_map/all_to_all | solution.py:169
  362.1 4.1 %fusion.28 = bf16[128,256]{1,0:T(8,128)(2,1)} fusion(f32[128,256]{1,0:T(8,128)} %reduce-scatter.8.cloned.1.call-done, f32[2048,128]{1,0:T(8,128)S(1)} %select_reduce_fusion, f32[2048,256]{1,0:T(8,128)} %bitcast.22, bf16[128,256]{1,0:T(8,128)(2,1)S(1)} %copy-done.11), kind=kOutput, calls=%fused_computation.40 | convolution fusion | flops 805437440 | bytes 3407872 | tf_op jit(solution)/shard_map/dot_general | solution.py:170
  (83 shorter events, 2.3 us)
Async XLA Ops:
  7.2 30.8 %copy-start = (bf16[2048,384]{1,0:T(8,128)(2,1)S(1)}, bf16[2048,384]{1,0:T(8,128)(2,1)}, u32[]{:S(2)}) copy-start(bf16[2048,384]{1,0:T(8,128)(2,1)} %param.24) | copy-start | bytes 4718596
  7.2 29.2 %copy-start.18 = (bf16[512]{0:T(512)(128)(2,1)S(1)}, bf16[512]{0:T(512)(128)(2,1)}, u32[]{:S(2)}) copy-start(bf16[512]{0:T(512)(128)(2,1)} %param.26) | copy-start | bytes 3076
  7.2 29.2 %copy-start.17 = (s32[128]{0:T(128)S(1)}, s32[128]{0:T(128)}, u32[]{:S(2)}) copy-start(s32[128]{0:T(128)} %param.20) | copy-start | bytes 1540
  7.2 79.3 %reduce-scatter.4.cloned.1.call-start = ((), (), s32[]{:S(2)}) async-start(), calls=%async_computation.5 | async-start | bytes 1179648 | tf_op jit(solution)/shard_map/reduce_scatter | solution.py:123
  36.9 2.1 copy-start.13
  37.2 0.7 copy-start.9
  42.9 1.4 copy-start.1
  42.9 1.9 copy-start.20
  44.8 3.5 copy-start.6
  48.3 1.4 copy-start.15
  48.3 1.8 copy-start.16
  48.3 38.2 %copy-start.14 = (bf16[128,256]{1,0:T(8,128)(2,1)S(1)}, bf16[128,256]{1,0:T(8,128)(2,1)}, u32[]{:S(2)}) copy-start(bf16[128,256]{1,0:T(8,128)(2,1)} %param.19) | copy-start | bytes 196612
  49.7 138.2 %all-gather.3.cloned.1.call-start = ((), (), s32[]{:S(2)}) async-start(), calls=%async_computation.8 | async-start | bytes 9437184 | tf_op jit(solution)/shard_map/all_gather | solution.py:151
  86.5 14.5 %copy-start.5 = (pred[2048,128]{1,0:T(8,128)(4,1)S(1)}, pred[2048,128]{1,0:T(8,128)(4,1)}, u32[]{:S(2)}) copy-start(pred[2048,128]{1,0:T(8,128)(4,1)} %fusion.4) | copy-start | bytes 786436
  87.5 13.3 %copy-start.10 = (bf16[128,256]{1,0:T(8,128)(2,1)}, bf16[128,256]{1,0:T(8,128)(2,1)S(1)}, u32[]{:S(2)}) copy-start(bf16[128,256]{1,0:T(8,128)(2,1)S(1)} %add_convert_fusion) | copy-start | bytes 196612
  101.0 39.4 %copy-start.2 = (bf16[2,2048,176]{1,2,0:T(8,128)(2,1)S(1)}, bf16[2,2048,176]{1,2,0:T(8,128)(2,1)}, u32[]{:S(2)}) copy-start(bf16[2,2048,176]{1,2,0:T(8,128)(2,1)} %param.33) | copy-start | bytes 4325380
  140.1 159.1 %reduce-scatter.6.cloned.1.call-start = ((), (), s32[]{:S(2)}) async-start(), calls=%async_computation.6 | async-start | bytes 18874368 | tf_op jit(solution)/shard_map/reduce_scatter | solution.py:163
  140.4 1.7 copy-start.3
  187.8 6.3 %copy-start.19 = (bf16[256,2,32,256]{3,2,1,0:T(8,128)(2,1)S(1)}, bf16[256,2,32,256]{3,2,1,0:T(8,128)(2,1)}, u32[]{:S(2)}) copy-start(bf16[256,2,32,256]{3,2,1,0:T(8,128)(2,1)} %all-gather.3.cloned.1.call-done) | copy-start | bytes 25165828
  194.1 2.4 copy-start.4
  302.4 10.3 %copy-start.7 = (bf16[2048,176]{0,1:T(8,128)(2,1)S(1)}, bf16[2048,176]{0,1:T(8,128)(2,1)}, u32[]{:S(2)}) copy-start(bf16[2048,176]{0,1:T(8,128)(2,1)} %param.35) | copy-start | bytes 2162692
  302.4 11.3 %copy-start.8 = (bf16[176,2048]{1,0:T(8,128)(2,1)S(1)}, bf16[176,2048]{1,0:T(8,128)(2,1)}, u32[]{:S(2)}) copy-start(bf16[176,2048]{1,0:T(8,128)(2,1)} %param.37) | copy-start | bytes 2162692
  302.4 59.6 %all-to-all-start.1 = ((f32[32,2,32,256]{3,2,1,0:T(8,128)}), f32[32,2,32,256]{3,2,1,0:T(8,128)}, u32[]{:S(2)}, u32[]{:S(2)}) async-start(f32[32,2,32,256]{3,2,1,0:T(8,128)} %copy.129), calls=%async_computation.3 | async-start | bytes 4194304 | tf_op jit(solution)/shard_map/all_to_all | solution.py:169
  312.7 38.8 %reduce-scatter.8.cloned.1.call-start = ((), (), s32[]{:S(2)}) async-start(), calls=%async_computation.7 | async-start | bytes 1179648 | tf_op jit(solution)/shard_map/reduce_scatter | solution.py:173
  313.7 3.3 copy-start.12
  317.4 44.6 %copy-start.11 = (bf16[128,256]{1,0:T(8,128)(2,1)S(1)}, bf16[128,256]{1,0:T(8,128)(2,1)}, u32[]{:S(2)}) copy-start(bf16[128,256]{1,0:T(8,128)(2,1)} %copy-done.10) | copy-start | bytes 196612
Sparse Core Ops, SparseCore 0:
  49.8 36.6 reduce-scatter.3
  140.3 47.4 all-gather.2
  204.7 94.5 reduce-scatter.5
  316.9 34.5 reduce-scatter.7

commit v2 on v1

--- a/solution.py
+++ b/solution.py
@@ -160,17 +160,23 @@
     partial_out = jnp.einsum(
         "oesf,efd->oesd", inner_units, expert_down, preferred_element_type=jnp.float32
     )
-    results = lax.psum_scatter(partial_out, "tp", scatter_dimension=3, tiled=True)
     shared_inner = (
         jax.nn.silu(jnp.dot(expert_in, shared_gate, preferred_element_type=jnp.float32))
         * jnp.dot(expert_in, shared_up, preferred_element_type=jnp.float32)
     ).astype(jnp.bfloat16)
     shared_part = jnp.dot(shared_inner, shared_down, preferred_element_type=jnp.float32)
+    both_parts = jnp.concatenate(
+        [partial_out.reshape(slot_total, -1), shared_part], axis=0
+    ).astype(jnp.bfloat16)
+    both_columns = lax.psum_scatter(both_parts, "tp", scatter_dimension=1, tiled=True)
+    results = both_columns[:slot_total].reshape(owner_count, per_owner, slot_count, column_width)
+    shared_columns = both_columns[slot_total:].astype(jnp.float32)
     returned = lax.all_to_all(results, "req", split_axis=0, concat_axis=0, tiled=True)
     routed = jnp.dot(
-        combine_matrix, returned.reshape(slot_total, column_width), precision=lax.Precision.HIGHEST
-    )
-    shared_columns = lax.psum_scatter(shared_part, "tp", scatter_dimension=1, tiled=True)
+        combine_matrix,
+        returned.reshape(slot_total, column_width).astype(jnp.float32),
+        precision=lax.Precision.HIGHEST,
+    )
     next_hidden = (mixed_columns.astype(jnp.float32) + routed + shared_columns).astype(jnp.bfloat16)
     return (next_hidden, new_rows)
 

time: 373 us -> 325 us (0.87)
  waiting for transfers between devices: 211 us -> 152 us
  local copies, waits for them, and re-layouts: 14.3 us -> 22.7 us
  other arithmetic: 8.92 us -> 16.4 us
  matrix products: 35.6 us -> 30.4 us
    reduce_scatter x2 -> x1, waiting for transfers between devices: 123 us -> 57.9 us  [shards(): lax.psum_scatter(both_parts, 'tp', scatter_dimension=1, tiled=True)]
    all_to_all x1, waiting for transfers between devices: 10.5 us -> 20.2 us  [shards(): lax.all_to_all(results, 'req', split_axis=0, concat_axis=0, tiled=True)]
    transpose x0 -> x1, local copies, waits for them, and re-layouts: none -> 8.27 us  [shards(): jnp.einsum('oesf,efd->oesd', inner_units, expert_down, preferred_element_...]
    concatenate x0 -> x1, other arithmetic: none -> 7.36 us  [shards(): jnp.concatenate([partial_out.reshape(slot_total, -1), shared_part], axis=0)]
    all_gather x1, waiting for transfers between devices: 45.3 us -> 41.3 us  [shards(): slab = lax.all_gather(slab_columns, 'tp', axis=0, tiled=False)]
  transfers between devices with their start and end apart: 5 -> 4, of which waited for: 5 -> 4; matrix products, arithmetic and copies ran while one was open for 5% -> 5% of each run, Pallas kernels for 0% -> 0%
where the time goes in v2:
time: 325 us
  waiting for transfers between devices  152 us (47%)
  blocking collectives  78.4 us (24%)
  matrix products  30.4 us (9%)
  local copies, waits for them, and re-layouts  22.7 us (7%)
  other arithmetic  16.4 us (5%)
  between operations  14.3 us (4%)
  starting transfers between devices  10.4 us (3%)
    reduce_scatter x1, waiting for transfers between devices, shards(): lax.psum_scatter(both_parts, 'tp', scatter_dimension=1, tiled=True)  57.9 us
    all_gather x1, waiting for transfers between devices, shards(): slab = lax.all_gather(slab_columns, 'tp', axis=0, tiled=False)  41.3 us
    all_to_all x1, blocking collectives, shards(): lax.all_to_all(outgoing, 'req', split_axis=0, concat_axis=0, tiled=True)  38.6 us
    reduce_scatter x1, waiting for transfers between devices, shards(): lax.psum_scatter(attention, 'tp', scatter_dimension=1, tiled=True)  32.8 us
    all_to_all x1, waiting for transfers between devices, shards(): lax.all_to_all(results, 'req', split_axis=0, concat_axis=0, tiled=True)  20.2 us
    all_gather x1, blocking collectives, shards(): whole = lax.all_gather(hidden, 'tp', axis=1, tiled=True)  14 us
    all_gather x1, blocking collectives, shards(): mixed = lax.all_gather(mixed_columns, 'tp', axis=1, tiled=True)  13.1 us
    all_gather x1, blocking collectives, shards(): latent_raw = lax.all_gather(latent_part, 'tp', axis=1, tiled=True)  12.8 us
  transfers between devices with their start and end apart: 4, of which 4 were waited for; matrix products, arithmetic and copies ran while one was open for 5% of the time, Pallas kernels for 0%

profile of v2, /device:TPU:32, one launch (start us, length us, event | category | flops | bytes accessed | tf_op | source)
XLA Modules:
  0.0 324.7 jit_solution(2594306848680994148)
XLA Ops:
  7.2 14.0 %all_gather.15 = bf16[128,2048]{1,0:T(8,128)(2,1)S(1)} all-gather(bf16[128,256]{1,0:T(8,128)(2,1)} %param.19), channel_id=1, replica_groups=mesh['req'=32,'tp'=8] {'tp'}, dimensions={1}, use_global_device_ids=true | all-gather | bytes 589824 | tf_op jit(solution)/shard_map/all_gather | solution.py:94
  21.2 0.2 fusion.36
  21.4 0.7 convert_element_type.100
  22.1 1.3 convolution_convert_fusion.3
  23.4 12.8 %all_gather.16 = bf16[128,576]{0,1:T(8,128)(2,1)S(1)} all-gather(bf16[128,72]{0,1:T(8,128)(2,1)S(1)} %convolution_convert_fusion.3), channel_id=1, replica_groups=mesh['req'=32,'tp'=8] {'tp'}, dimensions={1}, use_global_device_ids=true | all-gather | bytes 165888 | tf_op jit(solution)/shard_map/all_gather | solution.py:109
  36.5 0.2 reduce-window.18
  36.8 0.1 fusion.55
  37.0 0.1 subtract_convert_fusion.1
  37.2 0.1 copy.153
  37.6 0.8 fusion.63
  38.6 0.3 fusion.26
  38.9 0.5 fusion.49
  39.4 0.2 multiply_reduce_fusion
  39.6 2.9 select_reduce_fusion.1
  42.5 1.3 copy-done.2
  43.8 0.6 fusion.13
  44.4 3.5 %fusion.29 = bf16[2,128,128]{1,2,0:T(8,128)(2,1)S(1)} fusion(bf16[2,512,128]{2,1,0:T(8,128)(2,1)S(1)} %copy-done.16, bf16[2048,576]{0,1:T(8,128)(2,1)} %param.22, f32[128,2,2048]{2,0,1:T(8,128)} %copy-done.2, f32[128,2]{0,1:T(2,128)S(1)} %get-tuple-element.9, f32[128,2]{0,1:T(2,128)S(1)} %multiply_maximum_fusion, pred[128,2048]{1,0:T(8,128)(4,1)S(1)} %fusion.49, ...), kind=kOutput, calls=%fused_computation.43 | convolution fusion | flops 572948480 | bytes 5049344 | tf_op jit(solution)/shard_map/thl,hlv->thv/dot_general | solution.py:117
  47.9 1.3 fusion.82
  49.8 1.8 reduce-window.19
  51.6 0.3 slice_reduce_fusion
  51.9 0.1 fusion.60
  52.2 1.1 fusion.4
  53.3 32.8 %reduce-scatter.3.cloned.1.call-done = f32[128,256]{1,0:T(8,128)} async-done(((f32[128,2048]{1,0:T(8,128)}), f32[128,256]{1,0:T(8,128)}) %reduce-scatter.3.cloned.1.call-update) | async-done | bytes 131088 | tf_op jit(solution)/shard_map/reduce_scatter | solution.py:123
  86.1 0.9 add_convert_fusion
  87.0 13.1 %all_gather.17 = bf16[128,2048]{1,0:T(8,128)(2,1)S(1)} all-gather(bf16[128,256]{1,0:T(8,128)(2,1)S(1)} %add_convert_fusion), channel_id=1, replica_groups=mesh['req'=32,'tp'=8] {'tp'}, dimensions={1}, use_global_device_ids=true | all-gather | bytes 589824 | tf_op jit(solution)/shard_map/all_gather | solution.py:125
  100.1 0.2 fusion.39
  100.3 0.2 fusion.41
  100.5 0.4 convolution_convert_fusion
  101.0 38.6 %all_to_all.10 = bf16[32,2,32,256]{3,2,1,0:T(8,128)(2,1)} all-to-all(bf16[32,2,32,256]{3,2,1,0:T(8,128)(2,1)S(1)} %bitcast.121), channel_id=1, replica_groups=mesh['req'=32,'tp'=8] {'req'}, dimensions={0} | all-to-all | bytes 2097152 | tf_op jit(solution)/shard_map/all_to_all | solution.py:150
  139.6 0.2 reduce-scatter.5.cloned.1.call-start
  139.8 1.6 copy.156
  141.5 1.9 copy.155
  143.4 0.4 fusion.83
  143.7 2.2 convolution_convert_fusion.1
  146.0 41.3 %all-gather.3.cloned.1.call-done = bf16[256,2,32,256]{3,2,1,0:T(8,128)(2,1)} async-done(((bf16[32,2,32,256]{3,2,1,0:T(8,128)(2,1)}), bf16[256,2,32,256]{3,2,1,0:T(8,128)(2,1)}) %all-gather.3.cloned.1.call-update) | async-done | bytes 8388624 | tf_op jit(solution)/shard_map/all_gather | solution.py:151
  187.3 6.2 %fusion = f32[2,32,32,176,1]{3,2,1,0,4:T(8,128)S(1)} fusion(bf16[8,32,2,32,256]{4,3,2,1,0:T(8,128)(2,1)} %bitcast.131, bf16[2,8,256,176,1]{2,1,3,0,4:T(8,128)(2,1)} %bitcast.125), kind=kOutput, calls=%fused_computation.3 | convolution fusion | flops 1476395008 | bytes 11272192 | tf_op jit(solution)/shard_map/toesc,etcf->oesf/dot_general | solution.py:158
  193.5 2.3 fusion.2
  195.9 5.6 %convert_bitcast_fusion = bf16[32,2,32,2048]{3,2,0,1:T(8,128)(2,1)} fusion(bf16[2,176,2048]{2,1,0:T(8,128)(2,1)S(1)} %copy-done.15, f32[2,32,32,176,1]{3,2,1,0,4:T(8,128)S(1)} %fusion, f32[2,32,32,176,1]{3,2,1,0,4:T(8,128)S(1)} %fusion.2), kind=kOutput, calls=%fused_computation.2 | convolution fusion | flops 1482752000 | bytes 12713984 | tf_op jit(solution)/shard_map/oesf,efd->oesd/dot_general | solution.py:160
  201.5 8.3 %copy.130 = bf16[32,2,32,2048]{3,2,1,0:T(8,128)(2,1)} copy(bf16[32,2,32,2048]{3,2,0,1:T(8,128)(2,1)} %convert_bitcast_fusion) | data formatting | bytes 16777216 | tf_op jit(solution)/shard_map/oesf,efd->oesd/transpose | solution.py:160
  209.8 7.4 %pad_maximum_fusion = bf16[2176,2048]{1,0:T(8,128)(2,1)} fusion(bf16[128,2048]{1,0:T(8,128)(2,1)S(1)} %convolution_convert_fusion.1, bf16[2048,2048]{1,0:T(8,128)(2,1)} %bitcast.119), kind=kLoop, calls=%fused_computation.1 | loop fusion | flops 17825792 | bytes 17825792 | tf_op jit(solution)/shard_map/concatenate | solution.py:168
  217.2 57.9 %reduce-scatter.5.cloned.1.call-done = bf16[2176,256]{1,0:T(8,128)(2,1)} async-done(((bf16[2176,2048]{1,0:T(8,128)(2,1)}), bf16[2176,256]{1,0:T(8,128)(2,1)}) %reduce-scatter.5.cloned.1.call-update) | async-done | bytes 1114128 | tf_op jit(solution)/shard_map/reduce_scatter | solution.py:171
  275.0 2.3 slice.66
  277.3 10.1 %all-to-all-start.1 = ((bf16[32,2,32,256]{3,2,1,0:T(8,128)(2,1)}), bf16[32,2,32,256]{3,2,1,0:T(8,128)(2,1)S(1)}, u32[]{:S(2)}, u32[]{:S(2)}) async-start(bf16[32,2,32,256]{3,2,1,0:T(8,128)(2,1)} %bitcast.23), calls=%async_computation.3 | async-start | bytes 2097152 | tf_op jit(solution)/shard_map/all_to_all | solution.py:174
  287.7 0.3 fusion.35
  288.0 5.1 %gather_fusion = f32[768]{0:T(1024)S(1)} fusion(f32[128,64]{0,1:T(8,128)S(1)} %fusion.35, s32[768]{0:T(1024)S(1)} %reshape.244), kind=kCustom, calls=%fused_computation | custom fusion | bytes 12288 | tf_op jit(solution)/shard_map/jit(take_along_axis)/gather | solution.py:132
  293.4 1.8 select_reduce_fusion
  295.2 20.2 %all-to-all-done.1 = bf16[32,2,32,256]{3,2,1,0:T(8,128)(2,1)S(1)} async-done(((bf16[32,2,32,256]{3,2,1,0:T(8,128)(2,1)}), bf16[32,2,32,256]{3,2,1,0:T(8,128)(2,1)S(1)}, u32[]{:S(2)}, u32[]{:S(2)}) %all-to-all-start.1) | async-done | bytes 1048608 | tf_op jit(solution)/shard_map/all_to_all | solution.py:174
  315.4 2.9 fusion.28
  (74 shorter events, 2.3 us)
Async XLA Ops:
  7.2 30.4 %copy-start = (bf16[2048,384]{1,0:T(8,128)(2,1)S(1)}, bf16[2048,384]{1,0:T(8,128)(2,1)}, u32[]{:S(2)}) copy-start(bf16[2048,384]{1,0:T(8,128)(2,1)} %param.24) | copy-start | bytes 4718596
  7.2 29.2 %copy-start.13 = (bf16[512]{0:T(512)(128)(2,1)S(1)}, bf16[512]{0:T(512)(128)(2,1)}, u32[]{:S(2)}) copy-start(bf16[512]{0:T(512)(128)(2,1)} %param.26) | copy-start | bytes 3076
  7.2 29.2 %copy-start.12 = (s32[128]{0:T(128)S(1)}, s32[128]{0:T(128)}, u32[]{:S(2)}) copy-start(s32[128]{0:T(128)} %param.20) | copy-start | bytes 1540
  7.2 78.9 %reduce-scatter.3.cloned.1.call-start = ((), (), s32[]{:S(2)}) async-start(), calls=%async_computation.4 | async-start | bytes 1179648 | tf_op jit(solution)/shard_map/reduce_scatter | solution.py:123
  36.9 1.7 copy-start.8
  37.2 2.1 copy-start.6
  42.4 1.4 copy-start.2
  42.5 1.9 copy-start.16
  44.4 3.5 %copy-start.4 = (bf16[256,2048]{1,0:T(8,128)(2,1)S(1)}, bf16[256,2048]{1,0:T(8,128)(2,1)}, u32[]{:S(2)}) copy-start(bf16[256,2048]{1,0:T(8,128)(2,1)} %param.29) | copy-start | bytes 3145732
  47.9 1.4 copy-start.10
  47.9 1.8 copy-start.11
  47.9 38.2 %copy-start.9 = (bf16[128,256]{1,0:T(8,128)(2,1)S(1)}, bf16[128,256]{1,0:T(8,128)(2,1)}, u32[]{:S(2)}) copy-start(bf16[128,256]{1,0:T(8,128)(2,1)} %param.19) | copy-start | bytes 196612
  49.3 138.0 %all-gather.3.cloned.1.call-start = ((), (), s32[]{:S(2)}) async-start(), calls=%async_computation.6 | async-start | bytes 9437184 | tf_op jit(solution)/shard_map/all_gather | solution.py:151
  100.5 39.3 %copy-start.3 = (bf16[2,2048,176]{1,2,0:T(8,128)(2,1)S(1)}, bf16[2,2048,176]{1,2,0:T(8,128)(2,1)}, u32[]{:S(2)}) copy-start(bf16[2,2048,176]{1,2,0:T(8,128)(2,1)} %param.33) | copy-start | bytes 4325380
  139.6 135.4 %reduce-scatter.5.cloned.1.call-start = ((), (), s32[]{:S(2)}) async-start(), calls=%async_computation.5 | async-start | bytes 10027008 | tf_op jit(solution)/shard_map/reduce_scatter | solution.py:171
  141.5 1.9 copy-start.5
  187.3 6.3 %copy-start.14 = (bf16[256,2,32,256]{3,2,1,0:T(8,128)(2,1)S(1)}, bf16[256,2,32,256]{3,2,1,0:T(8,128)(2,1)}, u32[]{:S(2)}) copy-start(bf16[256,2,32,256]{3,2,1,0:T(8,128)(2,1)} %all-gather.3.cloned.1.call-done) | copy-start | bytes 25165828
  193.5 2.4 copy-start.15
  217.1 70.5 %copy-start.7 = (bf16[2048,64]{0,1:T(8,128)(2,1)S(1)}, bf16[2048,64]{0,1:T(8,128)(2,1)}, u32[]{:S(2)}) copy-start(bf16[2048,64]{0,1:T(8,128)(2,1)} %param.31) | copy-start | bytes 786436
  277.3 38.0 %all-to-all-start.1 = ((bf16[32,2,32,256]{3,2,1,0:T(8,128)(2,1)}), bf16[32,2,32,256]{3,2,1,0:T(8,128)(2,1)S(1)}, u32[]{:S(2)}, u32[]{:S(2)}) async-start(bf16[32,2,32,256]{3,2,1,0:T(8,128)(2,1)} %bitcast.23), calls=%async_computation.3 | async-start | bytes 2097152 | tf_op jit(solution)/shard_map/all_to_all | solution.py:174
  288.0 30.2 %copy-start.1 = (bf16[2048,384]{1,0:T(8,128)(2,1)S(1)}, bf16[2048,384]{1,0:T(8,128)(2,1)}, u32[]{:S(2)}) copy-start(bf16[2048,384]{1,0:T(8,128)(2,1)} %param.24) | copy-start | bytes 4718596
Sparse Core Ops, SparseCore 0:
  49.4 36.6 reduce-scatter.2
  139.7 47.4 all-gather.2
  217.3 57.7 reduce-scatter.4

commit v3 on v2

--- a/solution.py
+++ b/solution.py
@@ -120,7 +120,10 @@
     attention = jnp.dot(
         head_values.reshape(token_count, -1), output_weight, preferred_element_type=jnp.float32
     )
-    attention_columns = lax.psum_scatter(attention, "tp", scatter_dimension=1, tiled=True)
+    tp_count = lax.axis_size("tp")
+    attention_blocks = attention.reshape(token_count, tp_count, column_width).transpose(1, 0, 2)
+    attention_blocks = lax.all_to_all(attention_blocks, "tp", split_axis=0, concat_axis=0, tiled=True)
+    attention_columns = jnp.sum(attention_blocks, axis=0)
     mixed_columns = (hidden.astype(jnp.float32) + attention_columns).astype(jnp.bfloat16)
     mixed = lax.all_gather(mixed_columns, "tp", axis=1, tiled=True)
     expert_in = rms_norm(mixed, feedforward_gain).astype(jnp.bfloat16)
@@ -149,16 +152,15 @@
     outgoing = outgoing.reshape(owner_count, per_owner, slot_count, column_width)
     slab_columns = lax.all_to_all(outgoing, "req", split_axis=0, concat_axis=0, tiled=True)
     slab = lax.all_gather(slab_columns, "tp", axis=0, tiled=False)
-    tp_count = slab.shape[0]
     gate_blocks = expert_gate.reshape(per_owner, tp_count, column_width, -1)
     up_blocks = expert_up.reshape(per_owner, tp_count, column_width, -1)
     gate_part = jnp.einsum(
-        "toesc,etcf->oesf", slab, gate_blocks, preferred_element_type=jnp.float32
-    )
-    up_part = jnp.einsum("toesc,etcf->oesf", slab, up_blocks, preferred_element_type=jnp.float32)
+        "toesc,etcf->eosf", slab, gate_blocks, preferred_element_type=jnp.float32
+    )
+    up_part = jnp.einsum("toesc,etcf->eosf", slab, up_blocks, preferred_element_type=jnp.float32)
     inner_units = (jax.nn.silu(gate_part) * up_part).astype(jnp.bfloat16)
     partial_out = jnp.einsum(
-        "oesf,efd->oesd", inner_units, expert_down, preferred_element_type=jnp.float32
+        "eosf,efd->eosd", inner_units, expert_down, preferred_element_type=jnp.float32
     )
     shared_inner = (
         jax.nn.silu(jnp.dot(expert_in, shared_gate, preferred_element_type=jnp.float32))
@@ -169,8 +171,12 @@
         [partial_out.reshape(slot_total, -1), shared_part], axis=0
     ).astype(jnp.bfloat16)
     both_columns = lax.psum_scatter(both_parts, "tp", scatter_dimension=1, tiled=True)
-    results = both_columns[:slot_total].reshape(owner_count, per_owner, slot_count, column_width)
-    shared_columns = both_columns[slot_total:].astype(jnp.float32)
+    expert_sums = both_columns[:slot_total]
+    shared_sums = both_columns[slot_total:]
+    results = expert_sums.reshape(per_owner, owner_count, slot_count, column_width).transpose(
+        1, 0, 2, 3
+    )
+    shared_columns = shared_sums.astype(jnp.float32)
     returned = lax.all_to_all(results, "req", split_axis=0, concat_axis=0, tiled=True)
     routed = jnp.dot(
         combine_matrix,

time: 325 us -> 296 us (0.911)
  waiting for transfers between devices: 152 us -> 131 us
  local copies, waits for them, and re-layouts: 22.7 us -> 15.8 us
  starting transfers between devices: 10.4 us -> 14.2 us
  matrix products: 30.4 us -> 27 us
    reduce_scatter x1 -> x0, waiting for transfers between devices: 32.8 us -> none  [shards(): lax.psum_scatter(attention, 'tp', scatter_dimension=1, tiled=True)]
    all_to_all x0 -> x1, waiting for transfers between devices: none -> 11.1 us  [shards(): lax.all_to_all(attention_blocks, 'tp', split_axis=0, concat_axis=0, tiled...]
    transpose x1 -> x0, local copies, waits for them, and re-layouts: 8.27 us -> none  [shards(): jnp.einsum('oesf,efd->oesd', inner_units, expert_down, preferred_element_...]
    all_to_all x0 -> x1, starting transfers between devices: none -> 3.89 us  [shards(): lax.all_to_all(attention_blocks, 'tp', split_axis=0, concat_axis=0, tiled...]
  transfers between devices with their start and end apart: 4 -> 4, of which waited for: 4 -> 4; matrix products, arithmetic and copies ran while one was open for 5% -> 6% of each run, Pallas kernels for 0% -> 0%
where the time goes in v3:
time: 296 us
  waiting for transfers between devices  131 us (44%)
  blocking collectives  79.7 us (27%)
  matrix products  27 us (9%)
  local copies, waits for them, and re-layouts  15.8 us (5%)
  between operations  14.6 us (5%)
  starting transfers between devices  14.2 us (5%)
  other arithmetic  13.3 us (4%)
    reduce_scatter x1, waiting for transfers between devices, shards(): lax.psum_scatter(both_parts, 'tp', scatter_dimension=1, tiled=True)  57.8 us
    all_gather x1, waiting for transfers between devices, shards(): slab = lax.all_gather(slab_columns, 'tp', axis=0, tiled=False)  41.8 us
    all_to_all x1, blocking collectives, shards(): lax.all_to_all(outgoing, 'req', split_axis=0, concat_axis=0, tiled=True)  39.7 us
    all_to_all x1, waiting for transfers between devices, shards(): lax.all_to_all(results, 'req', split_axis=0, concat_axis=0, tiled=True)  20.2 us
    all_gather x1, blocking collectives, shards(): whole = lax.all_gather(hidden, 'tp', axis=1, tiled=True)  14 us
    all_gather x1, blocking collectives, shards(): mixed = lax.all_gather(mixed_columns, 'tp', axis=1, tiled=True)  13.2 us
    all_gather x1, blocking collectives, shards(): latent_raw = lax.all_gather(latent_part, 'tp', axis=1, tiled=True)  12.8 us
    all_to_all x1, waiting for transfers between devices, shards(): lax.all_to_all(attention_blocks, 'tp', split_axis=0, concat_axis=0, tiled...  11.1 us
  transfers between devices with their start and end apart: 4, of which 4 were waited for; matrix products, arithmetic and copies ran while one was open for 6% of the time, Pallas kernels for 0%

profile of v3, /device:TPU:32, one launch (start us, length us, event | category | flops | bytes accessed | tf_op | source)
XLA Modules:
  0.0 295.6 jit_solution(18424972539516100525)
XLA Ops:
  7.2 14.0 %all_gather.15 = bf16[128,2048]{1,0:T(8,128)(2,1)S(1)} all-gather(bf16[128,256]{1,0:T(8,128)(2,1)} %param.19), channel_id=1, replica_groups=mesh['req'=32,'tp'=8] {'tp'}, dimensions={1}, use_global_device_ids=true | all-gather | bytes 589824 | tf_op jit(solution)/shard_map/all_gather | solution.py:94
  21.2 0.2 fusion.36
  21.4 0.7 convert_element_type.100
  22.1 1.3 convolution_convert_fusion.4
  23.4 12.8 %all_gather.16 = bf16[128,576]{0,1:T(8,128)(2,1)S(1)} all-gather(bf16[128,72]{0,1:T(8,128)(2,1)S(1)} %convolution_convert_fusion.4), channel_id=1, replica_groups=mesh['req'=32,'tp'=8] {'tp'}, dimensions={1}, use_global_device_ids=true | all-gather | bytes 165888 | tf_op jit(solution)/shard_map/all_gather | solution.py:109
  36.4 0.2 reduce-window.18
  37.0 0.1 subtract_convert_fusion.1
  37.4 0.4 copy-done.10
  37.9 0.8 fusion.63
  38.9 0.3 fusion.26
  39.2 0.5 fusion.49
  39.7 0.2 multiply_reduce_fusion
  39.9 2.9 select_reduce_fusion.1
  42.8 0.6 fusion.13
  43.4 0.8 copy-done.1
  44.2 1.5 copy.157
  45.7 3.3 %fusion.29 = bf16[2,128,128]{1,2,0:T(8,128)(2,1)S(1)} fusion(bf16[2,512,128]{2,1,0:T(8,128)(2,1)S(1)} %copy-done.20, bf16[2048,576]{0,1:T(8,128)(2,1)} %param.22, f32[128,2,2048]{2,0,1:T(8,128)} %copy-done.1, f32[128,2]{0,1:T(2,128)S(1)} %get-tuple-element.9, f32[128,2]{0,1:T(2,128)S(1)} %multiply_maximum_fusion, pred[128,2048]{1,0:T(8,128)(4,1)S(1)} %fusion.49, ...), kind=kOutput, calls=%fused_computation.44 | convolution fusion | flops 572948480 | bytes 5049344 | tf_op jit(solution)/shard_map/thl,hlv->thv/dot_general | solution.py:117
  49.0 1.5 convolution_bitcast_fusion
  50.5 3.9 %all-to-all-start = ((f32[8,128,256]{2,1,0:T(8,128)}), f32[8,128,256]{2,1,0:T(8,128)S(1)}, u32[]{:S(2)}, u32[]{:S(2)}) async-start(f32[8,128,256]{2,1,0:T(8,128)} %convolution_bitcast_fusion), calls=%async_computation | async-start | bytes 2097152 | tf_op jit(solution)/shard_map/all_to_all | solution.py:125
  54.9 1.8 reduce-window.19
  56.7 0.3 slice_reduce_fusion
  57.3 1.9 fusion.4
  59.2 11.1 %all-to-all-done = f32[8,128,256]{2,1,0:T(8,128)S(1)} async-done(((f32[8,128,256]{2,1,0:T(8,128)}), f32[8,128,256]{2,1,0:T(8,128)S(1)}, u32[]{:S(2)}, u32[]{:S(2)}) %all-to-all-start) | async-done | bytes 1048608 | tf_op jit(solution)/shard_map/all_to_all | solution.py:125
  70.5 13.2 %all_gather.17 = bf16[128,2048]{1,0:T(8,128)(2,1)S(1)} all-gather(bf16[128,256]{1,0:T(8,128)(2,1)S(1)} %add_convert_fusion), channel_id=1, replica_groups=mesh['req'=32,'tp'=8] {'tp'}, dimensions={1}, use_global_device_ids=true | all-gather | bytes 589824 | tf_op jit(solution)/shard_map/all_gather | solution.py:128
  83.7 0.2 fusion.39
  83.9 0.2 fusion.41
  84.1 0.4 convolution_convert_fusion.1
  84.6 39.7 %all_to_all.15 = bf16[32,2,32,256]{3,2,1,0:T(8,128)(2,1)} all-to-all(bf16[32,2,32,256]{3,2,1,0:T(8,128)(2,1)S(1)} %bitcast.126), channel_id=1, replica_groups=mesh['req'=32,'tp'=8] {'req'}, dimensions={0} | all-to-all | bytes 2097152 | tf_op jit(solution)/shard_map/all_to_all | solution.py:153
  124.3 0.2 reduce-scatter.2.cloned.1.call-start
  124.6 1.6 copy.168
  126.2 1.5 copy.167
  127.7 0.4 fusion.82
  128.1 2.0 convolution_convert_fusion.2
  130.2 41.8 %all-gather.3.cloned.1.call-done = bf16[256,2,32,256]{3,2,1,0:T(8,128)(2,1)} async-done(((bf16[32,2,32,256]{3,2,1,0:T(8,128)(2,1)}), bf16[256,2,32,256]{3,2,1,0:T(8,128)(2,1)}) %all-gather.3.cloned.1.call-update) | async-done | bytes 8388624 | tf_op jit(solution)/shard_map/all_gather | solution.py:154
  172.0 6.2 %fusion = f32[2,32,32,176,1]{3,2,1,0,4:T(8,128)S(1)} fusion(bf16[8,32,2,32,256]{4,3,2,1,0:T(8,128)(2,1)} %bitcast.138, bf16[2,8,256,176,1]{2,1,3,0,4:T(8,128)(2,1)} %bitcast.131), kind=kOutput, calls=%fused_computation.2 | convolution fusion | flops 1476395008 | bytes 11272192 | tf_op jit(solution)/shard_map/toesc,etcf->eosf/dot_general | solution.py:160
  178.2 0.4 copy-done.18
  178.6 2.3 fusion.2
  181.0 2.4 convolution_convert_fusion
  183.4 4.3 %pad_maximum_fusion = bf16[2176,2048]{1,0:T(8,128)(2,1)} fusion(bf16[128,2048]{1,0:T(8,128)(2,1)S(1)} %convolution_convert_fusion.2, bf16[2048,2048]{1,0:T(8,128)(2,1)S(1)} %bitcast.122), kind=kLoop, calls=%fused_computation.1 | loop fusion | flops 17825792 | bytes 17825792 | tf_op jit(solution)/shard_map/concatenate | solution.py:170
  187.7 57.8 %reduce-scatter.2.cloned.1.call-done = bf16[2176,256]{1,0:T(8,128)(2,1)} async-done(((bf16[2176,2048]{1,0:T(8,128)(2,1)}), bf16[2176,256]{1,0:T(8,128)(2,1)}) %reduce-scatter.2.cloned.1.call-update) | async-done | bytes 1114128 | tf_op jit(solution)/shard_map/reduce_scatter | solution.py:173
  245.5 1.2 slice-done
  246.8 1.1 copy.187
  247.9 10.1 %all-to-all-start.2 = ((bf16[32,2,32,256]{3,2,1,0:T(8,128)(2,1)}), bf16[32,2,32,256]{3,2,1,0:T(8,128)(2,1)S(1)}, u32[]{:S(2)}, u32[]{:S(2)}) async-start(bf16[32,2,32,256]{3,2,1,0:T(8,128)(2,1)} %bitcast.124), calls=%async_computation.3 | async-start | bytes 2097152 | tf_op jit(solution)/shard_map/all_to_all | solution.py:180
  258.2 0.3 fusion.35
  258.6 5.1 %gather_fusion = f32[768]{0:T(1024)S(1)} fusion(f32[128,64]{0,1:T(8,128)S(1)} %fusion.35, s32[768]{0:T(1024)S(1)} %reshape.246), kind=kCustom, calls=%fused_computation | custom fusion | bytes 12288 | tf_op jit(solution)/shard_map/jit(take_along_axis)/gather | solution.py:135
  263.9 1.8 select_reduce_fusion
  265.7 20.2 %all-to-all-done.2 = bf16[32,2,32,256]{3,2,1,0:T(8,128)(2,1)S(1)} async-done(((bf16[32,2,32,256]{3,2,1,0:T(8,128)(2,1)}), bf16[32,2,32,256]{3,2,1,0:T(8,128)(2,1)S(1)}, u32[]{:S(2)}, u32[]{:S(2)}) %all-to-all-start.2) | async-done | bytes 1048608 | tf_op jit(solution)/shard_map/all_to_all | solution.py:180
  285.9 2.9 fusion.28
  (84 shorter events, 2.7 us)
Async XLA Ops:
  7.2 30.8 %copy-start = (bf16[2048,384]{1,0:T(8,128)(2,1)S(1)}, bf16[2048,384]{1,0:T(8,128)(2,1)}, u32[]{:S(2)}) copy-start(bf16[2048,384]{1,0:T(8,128)(2,1)} %param.24) | copy-start | bytes 4718596
  7.2 29.1 %copy-start.17 = (bf16[512]{0:T(512)(128)(2,1)S(1)}, bf16[512]{0:T(512)(128)(2,1)}, u32[]{:S(2)}) copy-start(bf16[512]{0:T(512)(128)(2,1)} %param.26) | copy-start | bytes 3076
  7.2 29.1 %copy-start.16 = (s32[128]{0:T(128)S(1)}, s32[128]{0:T(128)}, u32[]{:S(2)}) copy-start(s32[128]{0:T(128)} %param.20) | copy-start | bytes 1540
  36.9 2.1 copy-start.12
  37.2 0.7 copy-start.10
  42.8 1.4 copy-start.1
  42.8 2.8 copy-start.20
  49.0 5.4 %copy-start.14 = (s32[128,6]{0,1:T(8,128)S(1)}, s32[128,6]{0,1:T(8,128)}, u32[]{:S(2)}) copy-start(s32[128,6]{0,1:T(8,128)} %param.21) | copy-start | bytes 9220
  49.0 5.8 %copy-start.15 = (bf16[2048]{0:T(1024)(128)(2,1)S(1)}, bf16[2048]{0:T(1024)(128)(2,1)}, u32[]{:S(2)}) copy-start(bf16[2048]{0:T(1024)(128)(2,1)} %param.30) | copy-start | bytes 12292
  50.5 19.9 %copy-start.13 = (bf16[128,256]{1,0:T(8,128)(2,1)S(1)}, bf16[128,256]{1,0:T(8,128)(2,1)}, u32[]{:S(2)}) copy-start(bf16[128,256]{1,0:T(8,128)(2,1)} %param.19) | copy-start | bytes 196612
  50.5 19.8 %all-to-all-start = ((f32[8,128,256]{2,1,0:T(8,128)}), f32[8,128,256]{2,1,0:T(8,128)S(1)}, u32[]{:S(2)}, u32[]{:S(2)}) async-start(f32[8,128,256]{2,1,0:T(8,128)} %convolution_bitcast_fusion), calls=%async_computation | async-start | bytes 2097152 | tf_op jit(solution)/shard_map/all_to_all | solution.py:125
  54.4 117.6 %all-gather.3.cloned.1.call-start = ((), (), s32[]{:S(2)}) async-start(), calls=%async_computation.5 | async-start | bytes 9437184 | tf_op jit(solution)/shard_map/all_gather | solution.py:154
  70.4 13.7 %copy-start.5 = (pred[2048,128]{1,0:T(8,128)(4,1)S(1)}, pred[2048,128]{1,0:T(8,128)(4,1)}, u32[]{:S(2)}) copy-start(pred[2048,128]{1,0:T(8,128)(4,1)} %fusion.4) | copy-start | bytes 786436
  70.4 13.5 %copy-start.8 = (bf16[128,256]{1,0:T(8,128)(2,1)}, bf16[128,256]{1,0:T(8,128)(2,1)S(1)}, u32[]{:S(2)}) copy-start(bf16[128,256]{1,0:T(8,128)(2,1)S(1)} %add_convert_fusion) | copy-start | bytes 196612
  84.1 40.4 %copy-start.2 = (bf16[2,2048,176]{1,2,0:T(8,128)(2,1)S(1)}, bf16[2,2048,176]{1,2,0:T(8,128)(2,1)}, u32[]{:S(2)}) copy-start(bf16[2,2048,176]{1,2,0:T(8,128)(2,1)} %param.33) | copy-start | bytes 4325380
  124.3 121.2 %reduce-scatter.2.cloned.1.call-start = ((), (), s32[]{:S(2)}) async-start(), calls=%async_computation.4 | async-start | bytes 10027008 | tf_op jit(solution)/shard_map/reduce_scatter | solution.py:173
  124.5 1.7 copy-start.3
  126.2 1.5 copy-start.6
  126.2 1.9 copy-start.7
  172.0 6.3 %copy-start.4 = (bf16[44,8,8,256]{3,2,1,0:T(8,128)(2,1)S(1)}, bf16[44,8,8,256]{3,2,1,0:T(8,128)(2,1)}, u32[]{:S(2)}) copy-start(bf16[44,8,8,256]{3,2,1,0:T(8,128)(2,1)} %copy.167) | copy-start | bytes 4325380
  172.0 6.6 %copy-start.18 = (bf16[256,2,32,256]{3,2,1,0:T(8,128)(2,1)S(1)}, bf16[256,2,32,256]{3,2,1,0:T(8,128)(2,1)}, u32[]{:S(2)}) copy-start(bf16[256,2,32,256]{3,2,1,0:T(8,128)(2,1)} %all-gather.3.cloned.1.call-done) | copy-start | bytes 25165828
  178.6 2.4 copy-start.19
  245.5 1.2 slice-start
  246.8 11.5 %copy-start.11 = (bf16[2048,64]{0,1:T(8,128)(2,1)S(1)}, bf16[2048,64]{0,1:T(8,128)(2,1)}, u32[]{:S(2)}) copy-start(bf16[2048,64]{0,1:T(8,128)(2,1)} %param.31) | copy-start | bytes 786436
  247.9 38.0 %all-to-all-start.2 = ((bf16[32,2,32,256]{3,2,1,0:T(8,128)(2,1)}), bf16[32,2,32,256]{3,2,1,0:T(8,128)(2,1)S(1)}, u32[]{:S(2)}, u32[]{:S(2)}) async-start(bf16[32,2,32,256]{3,2,1,0:T(8,128)(2,1)} %bitcast.124), calls=%async_computation.3 | async-start | bytes 2097152 | tf_op jit(solution)/shard_map/all_to_all | solution.py:180
  258.6 27.3 %copy-start.9 = (bf16[128,256]{1,0:T(8,128)(2,1)S(1)}, bf16[128,256]{1,0:T(8,128)(2,1)}, u32[]{:S(2)}) copy-start(bf16[128,256]{1,0:T(8,128)(2,1)} %copy-done.8) | copy-start | bytes 196612
Sparse Core Ops, SparseCore 0:
  124.4 47.4 all-gather.2
  187.8 57.6 reduce-scatter.1

commit v4 on v3

--- a/solution.py
+++ b/solution.py
@@ -1,7 +1,7 @@
 import jax
 import jax.numpy as jnp
 from jax import lax
-from jax.sharding import PartitionSpec as P
+from jax.sharding import Mesh, PartitionSpec as P
 
 rope_base = 50000.0
 route_scale = 2.446
@@ -61,6 +61,27 @@
         :, None, :latent_width
     ].astype(jnp.float32)
     return summed.astype(jnp.bfloat16)
+
+
+REQ_AXES = ("req_hi", "req_lo")
+
+
+def req_all_to_all(values):
+    high = lax.axis_size(REQ_AXES[0])
+    low = lax.axis_size(REQ_AXES[1])
+    staged = values.reshape(high, low, *values.shape[1:])
+    staged = lax.all_to_all(staged, REQ_AXES[1], split_axis=1, concat_axis=1, tiled=True)
+    staged = lax.all_to_all(staged, REQ_AXES[0], split_axis=0, concat_axis=0, tiled=True)
+    return staged.reshape(values.shape)
+
+
+def split_mesh(mesh):
+    column = mesh.devices[:, 0]
+    low = len({device.coords[2] for device in column})
+    if low < 1 or column.size % low:
+        low = 1
+    devices = mesh.devices.reshape(column.size // low, low, mesh.devices.shape[1])
+    return Mesh(devices, REQ_AXES + ("tp",))
 
 
 def shards(
@@ -85,7 +106,7 @@
     shared_down,
 ):
     token_count = hidden.shape[0]
-    owner_count = lax.axis_size("req")
+    owner_count = lax.axis_size(REQ_AXES)
     column_width = hidden.shape[1]
     column_start = lax.axis_index("tp") * column_width
     heads_here = key_absorb.shape[0]
@@ -150,7 +171,7 @@
         jnp.bfloat16
     )
     outgoing = outgoing.reshape(owner_count, per_owner, slot_count, column_width)
-    slab_columns = lax.all_to_all(outgoing, "req", split_axis=0, concat_axis=0, tiled=True)
+    slab_columns = req_all_to_all(outgoing)
     slab = lax.all_gather(slab_columns, "tp", axis=0, tiled=False)
     gate_blocks = expert_gate.reshape(per_owner, tp_count, column_width, -1)
     up_blocks = expert_up.reshape(per_owner, tp_count, column_width, -1)
@@ -177,7 +198,7 @@
         1, 0, 2, 3
     )
     shared_columns = shared_sums.astype(jnp.float32)
-    returned = lax.all_to_all(results, "req", split_axis=0, concat_axis=0, tiled=True)
+    returned = req_all_to_all(results)
     routed = jnp.dot(
         combine_matrix,
         returned.reshape(slot_total, column_width).astype(jnp.float32),
@@ -188,11 +209,12 @@
 
 
 def solution(mesh):
+    req = REQ_AXES
     in_specs = (
-        P("req", "tp"),
-        P("req"),
-        P("req", None),
-        P("req", None),
+        P(req, "tp"),
+        P(req),
+        P(req, None),
+        P(req, None),
         P(),
         P(None, "tp"),
         P(None, "tp"),
@@ -202,12 +224,14 @@
         P("tp", None),
         P(),
         P(),
-        P("req", None, "tp"),
-        P("req", None, "tp"),
-        P("req", "tp", None),
+        P(req, None, "tp"),
+        P(req, None, "tp"),
+        P(req, "tp", None),
         P(None, "tp"),
         P(None, "tp"),
         P("tp", None),
     )
-    out_specs = (P("req", "tp"), P("req", None))
-    return jax.shard_map(shards, mesh=mesh, in_specs=in_specs, out_specs=out_specs, check_vma=False)
+    out_specs = (P(req, "tp"), P(req, None))
+    return jax.shard_map(
+        shards, mesh=split_mesh(mesh), in_specs=in_specs, out_specs=out_specs, check_vma=False
+    )

time: 296 us -> 338 us (1.14); the launches traced: 296 us -> 333 us
  blocking collectives: 79.7 us -> 93.6 us
  waiting for transfers between devices: 131 us -> 142 us
  matrix products: 27 us -> 33.6 us
    all_to_all x1 -> x2, blocking collectives: 39.7 us -> 53.7 us  [the longest x1 36.2 us: req_all_to_all(): lax.all_to_all(staged, REQ_AXES[1], split_axis=1, concat_axis=1, tiled=True)]
    all_to_all x1 -> x2, waiting for transfers between devices: 20.2 us -> 30.8 us  [the longest x1 26.4 us: req_all_to_all(): lax.all_to_all(staged, REQ_AXES[1], split_axis=1, concat_axis=1, tiled=True)]
    dot_general x1, matrix products: 2.39 us -> 9.89 us  [shards(): jnp.einsum('eosf,efd->eosd', inner_units, expert_down, preferred_element_...]
    dot_general x1 -> x0, matrix products: 6.24 us -> none  [shards(): jnp.einsum('toesc,etcf->eosf', slab, up_blocks, preferred_element_type=jn...]
    dot_general x1, matrix products: 2.34 us -> 7.43 us  [shards(): jnp.einsum('toesc,etcf->eosf', slab, gate_blocks, preferred_element_type=...]
    all_to_all x1 -> x2, starting transfers between devices: 10.1 us -> 11.7 us  [the longest x1 7.48 us: req_all_to_all(): lax.all_to_all(staged, REQ_AXES[1], split_axis=1, concat_axis=1, tiled=True)]
  transfers between devices with their start and end apart: 4 -> 5, of which waited for: 4 -> 5; matrix products, arithmetic and copies ran while one was open for 6% -> 5% of each run, Pallas kernels for 0% -> 0%
where the time goes in v4:
time: 338 us; the launch traced here: 333 us
  waiting for transfers between devices  142 us (42%)
  blocking collectives  93.6 us (28%)
  matrix products  33.6 us (10%)
  local copies, waits for them, and re-layouts  17.7 us (5%)
  starting transfers between devices  15.9 us (5%)
  other arithmetic  15.6 us (5%)
  between operations  14.5 us (4%)
    reduce_scatter x1, waiting for transfers between devices, shards(): lax.psum_scatter(both_parts, 'tp', scatter_dimension=1, tiled=True)  57.9 us
    all_gather x1, waiting for transfers between devices, shards(): slab = lax.all_gather(slab_columns, 'tp', axis=0, tiled=False)  41.1 us
    all_to_all x1, blocking collectives, req_all_to_all(): lax.all_to_all(staged, REQ_AXES[1], split_axis=1, concat_axis=1, tiled=True)  36.2 us
    all_to_all x1, waiting for transfers between devices, req_all_to_all(): lax.all_to_all(staged, REQ_AXES[1], split_axis=1, concat_axis=1, tiled=True)  26.4 us
    all_to_all x1, blocking collectives, req_all_to_all(): lax.all_to_all(staged, REQ_AXES[0], split_axis=0, concat_axis=0, tiled=True)  17.6 us
    all_gather x1, blocking collectives, shards(): whole = lax.all_gather(hidden, 'tp', axis=1, tiled=True)  14 us
    all_gather x1, blocking collectives, shards(): mixed = lax.all_gather(mixed_columns, 'tp', axis=1, tiled=True)  13.1 us
    all_gather x1, blocking collectives, shards(): latent_raw = lax.all_gather(latent_part, 'tp', axis=1, tiled=True)  12.8 us
  transfers between devices with their start and end apart: 5, of which 5 were waited for; matrix products, arithmetic and copies ran while one was open for 5% of the time, Pallas kernels for 0%

profile of v4, /device:TPU:32, one launch (start us, length us, event | category | flops | bytes accessed | tf_op | source)
XLA Modules:
  0.0 332.6 jit_solution(9559697454544116745)
XLA Ops:
  7.2 14.0 %all_gather.12 = bf16[128,2048]{1,0:T(8,128)(2,1)S(1)} all-gather(bf16[128,256]{1,0:T(8,128)(2,1)} %param.19), channel_id=1, replica_groups=mesh['req_hi'=4,'req_lo'=8,'tp'=8] {'tp'}, dimensions={1}, use_global_device_ids=true | all-gather | bytes 589824 | tf_op jit(solution)/shard_map/all_gather | solution.py:115
  21.2 0.2 fusion.34
  21.4 0.7 convert_element_type.100
  22.1 1.3 convolution_convert_fusion.4
  23.4 12.8 %all_gather.13 = bf16[128,576]{0,1:T(8,128)(2,1)S(1)} all-gather(bf16[128,72]{0,1:T(8,128)(2,1)S(1)} %convolution_convert_fusion.4), channel_id=1, replica_groups=mesh['req_hi'=4,'req_lo'=8,'tp'=8] {'tp'}, dimensions={1}, use_global_device_ids=true | all-gather | bytes 165888 | tf_op jit(solution)/shard_map/all_gather | solution.py:130
  37.5 0.8 fusion.61
  38.5 0.3 fusion.24
  38.8 0.5 fusion.47
  39.5 2.9 select_reduce_fusion.1
  42.4 0.6 fusion.9
  43.0 0.7 copy-done.2
  43.8 0.6 copy-done.4
  44.4 0.5 copy.226
  44.9 3.3 %fusion.27 = bf16[2,128,128]{1,2,0:T(8,128)(2,1)S(1)} fusion(bf16[2,512,128]{2,1,0:T(8,128)(2,1)S(1)} %copy-done.14, bf16[2048,576]{0,1:T(8,128)(2,1)} %param.22, f32[128,2,2048]{2,0,1:T(8,128)} %copy-done.2, f32[128,2]{0,1:T(2,128)S(1)} %get-tuple-element.9, f32[128,2]{0,1:T(2,128)S(1)} %multiply_maximum_fusion, pred[128,2048]{1,0:T(8,128)(4,1)S(1)} %fusion.47, ...), kind=kOutput, calls=%fused_computation.41 | convolution fusion | flops 572948480 | bytes 5049344 | tf_op jit(solution)/shard_map/thl,hlv->thv/dot_general | solution.py:138
  48.3 1.5 convolution_bitcast_fusion
  49.8 3.9 %all-to-all-start = ((f32[8,128,256]{2,1,0:T(8,128)}), f32[8,128,256]{2,1,0:T(8,128)S(1)}, u32[]{:S(2)}, u32[]{:S(2)}) async-start(f32[8,128,256]{2,1,0:T(8,128)} %convolution_bitcast_fusion), calls=%async_computation | async-start | bytes 2097152 | tf_op jit(solution)/shard_map/all_to_all | solution.py:146
  54.2 1.8 reduce-window.19
  56.0 0.3 slice_reduce_fusion
  56.6 1.1 fusion
  57.7 11.9 %all-to-all-done = f32[8,128,256]{2,1,0:T(8,128)S(1)} async-done(((f32[8,128,256]{2,1,0:T(8,128)}), f32[8,128,256]{2,1,0:T(8,128)S(1)}, u32[]{:S(2)}, u32[]{:S(2)}) %all-to-all-start) | async-done | bytes 1048608 | tf_op jit(solution)/shard_map/all_to_all | solution.py:146
  69.7 13.1 %all_gather.14 = bf16[128,2048]{1,0:T(8,128)(2,1)S(1)} all-gather(bf16[128,256]{1,0:T(8,128)(2,1)S(1)} %add_convert_fusion), channel_id=1, replica_groups=mesh['req_hi'=4,'req_lo'=8,'tp'=8] {'tp'}, dimensions={1}, use_global_device_ids=true | all-gather | bytes 589824 | tf_op jit(solution)/shard_map/all_gather | solution.py:149
  83.0 0.2 fusion.39
  83.2 0.4 convolution_convert_fusion.1
  83.7 36.2 %all_to_all.25 = bf16[4,8,2,32,256]{4,3,2,0,1:T(8,128)(2,1)S(1)} all-to-all(bf16[4,8,2,32,256]{4,3,2,0,1:T(8,128)(2,1)S(1)} %copy.202), channel_id=1, replica_groups=mesh['req_hi'=4,'req_lo'=8,'tp'=8] {'req_lo'}, dimensions={1} | all-to-all | bytes 2097152 | tf_op jit(solution)/shard_map/all_to_all | solution.py:73
  120.0 17.6 %all_to_all.26 = bf16[4,8,2,32,256]{4,3,2,1,0:T(8,128)(2,1)S(1)} all-to-all(bf16[4,8,2,32,256]{4,3,2,1,0:T(8,128)(2,1)S(1)} %copy.203), channel_id=1, replica_groups=mesh['req_hi'=4,'req_lo'=8,'tp'=8] {'req_hi'}, dimensions={0} | all-to-all | bytes 2097152 | tf_op jit(solution)/shard_map/all_to_all | solution.py:74
  137.5 1.1 copy.204
  138.7 0.2 reduce-scatter.2.cloned.1.call-start
  138.9 0.4 copy-done.3
  139.3 1.6 copy.237
  140.9 1.9 copy.238
  142.8 0.4 fusion.81
  143.2 2.2 convolution_convert_fusion.2
  145.4 41.1 %all-gather.2.cloned.1.call-done = bf16[8,32,2,32,256]{4,3,0,1,2:T(8,128)(2,1)} async-done(((bf16[1,32,2,32,256]{4,3,0,1,2:T(8,128)(2,1)}), bf16[8,32,2,32,256]{4,3,0,1,2:T(8,128)(2,1)}) %all-gather.2.cloned.1.call-update) | async-done | bytes 8388624 | tf_op jit(solution)/shard_map/all_gather | solution.py:175
  186.5 7.4 %fusion.13 = f32[2,32,32,176,1]{3,2,4,1,0:T(8,128)} fusion(bf16[8,32,2,32,256]{4,3,0,1,2:T(8,128)(2,1)} %all-gather.2.cloned.1.call-done, bf16[2,8,256,176,1]{2,1,3,0,4:T(8,128)(2,1)} %bitcast.136), kind=kOutput, calls=%fused_computation.26 | convolution fusion | flops 1476395008 | bytes 11272192 | tf_op jit(solution)/shard_map/toesc,etcf->eosf/dot_general | solution.py:178
  193.9 9.9 %convolution_convert_fusion = bf16[2,32,32,2048]{3,2,1,0:T(8,128)(2,1)} fusion(f32[2,32,32,176,1]{3,2,4,1,0:T(8,128)} %fusion.13, bf16[8,32,2,32,256]{4,3,0,1,2:T(8,128)(2,1)} %all-gather.2.cloned.1.call-done, bf16[2,176,2048]{2,1,0:T(8,128)(2,1)} %param.34, bf16[2,8,256,176,1]{2,1,3,0,4:T(8,128)(2,1)S(1)} %bitcast.135), kind=kOutput, calls=%fused_computation.5 | convolution fusion | flops 2959147008 | bytes 21102592 | tf_op jit(solution)/shard_map/eosf,efd->eosd/dot_general | solution.py:183
  203.8 7.4 %pad_maximum_fusion = bf16[2176,2048]{1,0:T(8,128)(2,1)} fusion(bf16[128,2048]{1,0:T(8,128)(2,1)S(1)} %convolution_convert_fusion.2, bf16[2048,2048]{1,0:T(8,128)(2,1)} %bitcast.127), kind=kLoop, calls=%fused_computation.1 | loop fusion | flops 17825792 | bytes 17825792 | tf_op jit(solution)/shard_map/concatenate | solution.py:191
  211.2 57.9 %reduce-scatter.2.cloned.1.call-done = bf16[2176,256]{1,0:T(8,128)(2,1)} async-done(((bf16[2176,2048]{1,0:T(8,128)(2,1)}), bf16[2176,256]{1,0:T(8,128)(2,1)}) %reduce-scatter.2.cloned.1.call-update) | async-done | bytes 1114128 | tf_op jit(solution)/shard_map/reduce_scatter | solution.py:194
  269.1 1.2 slice-done
  270.3 1.1 copy.208
  271.4 7.5 %all-to-all-start.3 = ((bf16[4,8,2,32,256]{4,3,2,0,1:T(8,128)(2,1)}), bf16[4,8,2,32,256]{4,3,2,0,1:T(8,128)(2,1)S(1)}, u32[]{:S(2)}, u32[]{:S(2)}) async-start(bf16[4,8,2,32,256]{4,3,2,0,1:T(8,128)(2,1)} %copy.208), calls=%async_computation.4 | async-start | bytes 2097152 | tf_op jit(solution)/shard_map/all_to_all | solution.py:73
  279.1 26.4 %all-to-all-done.3 = bf16[4,8,2,32,256]{4,3,2,0,1:T(8,128)(2,1)S(1)} async-done(((bf16[4,8,2,32,256]{4,3,2,0,1:T(8,128)(2,1)}), bf16[4,8,2,32,256]{4,3,2,0,1:T(8,128)(2,1)S(1)}, u32[]{:S(2)}, u32[]{:S(2)}) %all-to-all-start.3) | async-done | bytes 1048608 | tf_op jit(solution)/shard_map/all_to_all | solution.py:73
  305.6 1.1 copy.209
  306.7 4.2 %all-to-all-start.4 = ((bf16[4,8,2,32,256]{4,3,2,1,0:T(8,128)(2,1)}), bf16[4,8,2,32,256]{4,3,2,1,0:T(8,128)(2,1)S(1)}, u32[]{:S(2)}, u32[]{:S(2)}) async-start(bf16[4,8,2,32,256]{4,3,2,1,0:T(8,128)(2,1)} %copy.209), calls=%async_computation.5 | async-start | bytes 2097152 | tf_op jit(solution)/shard_map/all_to_all | solution.py:74
  311.0 0.3 fusion.33
  311.3 5.1 %gather_fusion = f32[768]{0:T(1024)S(1)} fusion(f32[128,64]{0,1:T(8,128)S(1)} %fusion.33, s32[768]{0:T(1024)S(1)} %reshape.242), kind=kCustom, calls=%fused_computation | custom fusion | bytes 12288 | tf_op jit(solution)/shard_map/jit(take_along_axis)/gather | solution.py:156
  316.7 1.8 select_reduce_fusion
  318.5 4.4 %all-to-all-done.4 = bf16[4,8,2,32,256]{4,3,2,1,0:T(8,128)(2,1)S(1)} async-done(((bf16[4,8,2,32,256]{4,3,2,1,0:T(8,128)(2,1)}), bf16[4,8,2,32,256]{4,3,2,1,0:T(8,128)(2,1)S(1)}, u32[]{:S(2)}, u32[]{:S(2)}) %all-to-all-start.4) | async-done | bytes 1048608 | tf_op jit(solution)/shard_map/all_to_all | solution.py:74
  322.9 2.9 fusion.26
  (78 shorter events, 3.5 us)
Async XLA Ops:
  7.2 30.4 %copy-start = (bf16[2048,384]{1,0:T(8,128)(2,1)S(1)}, bf16[2048,384]{1,0:T(8,128)(2,1)}, u32[]{:S(2)}) copy-start(bf16[2048,384]{1,0:T(8,128)(2,1)} %param.24) | copy-start | bytes 4718596
  7.2 29.1 %copy-start.13 = (bf16[512]{0:T(512)(128)(2,1)S(1)}, bf16[512]{0:T(512)(128)(2,1)}, u32[]{:S(2)}) copy-start(bf16[512]{0:T(512)(128)(2,1)} %param.26) | copy-start | bytes 3076
  7.2 29.1 %copy-start.12 = (s32[128]{0:T(128)S(1)}, s32[128]{0:T(128)}, u32[]{:S(2)}) copy-start(s32[128]{0:T(128)} %param.20) | copy-start | bytes 1540
  36.9 1.7 copy-start.8
  37.2 2.1 copy-start.6
  42.4 1.4 copy-start.2
  42.4 2.0 copy-start.4
  42.4 2.5 copy-start.14
  48.3 5.4 %copy-start.10 = (s32[128,6]{0,1:T(8,128)S(1)}, s32[128,6]{0,1:T(8,128)}, u32[]{:S(2)}) copy-start(s32[128,6]{0,1:T(8,128)} %param.21) | copy-start | bytes 9220
  48.3 5.8 %copy-start.11 = (bf16[2048]{0:T(1024)(128)(2,1)S(1)}, bf16[2048]{0:T(1024)(128)(2,1)}, u32[]{:S(2)}) copy-start(bf16[2048]{0:T(1024)(128)(2,1)} %param.30) | copy-start | bytes 12292
  49.8 19.9 %copy-start.9 = (bf16[128,256]{1,0:T(8,128)(2,1)S(1)}, bf16[128,256]{1,0:T(8,128)(2,1)}, u32[]{:S(2)}) copy-start(bf16[128,256]{1,0:T(8,128)(2,1)} %param.19) | copy-start | bytes 196612
  49.8 19.8 %all-to-all-start = ((f32[8,128,256]{2,1,0:T(8,128)}), f32[8,128,256]{2,1,0:T(8,128)S(1)}, u32[]{:S(2)}, u32[]{:S(2)}) async-start(f32[8,128,256]{2,1,0:T(8,128)} %convolution_bitcast_fusion), calls=%async_computation | async-start | bytes 2097152 | tf_op jit(solution)/shard_map/all_to_all | solution.py:146
  53.7 132.8 %all-gather.2.cloned.1.call-start = ((), (), s32[]{:S(2)}) async-start(), calls=%async_computation.6 | async-start | bytes 9437184 | tf_op jit(solution)/shard_map/all_gather | solution.py:175
  137.5 1.7 copy-start.3
  138.7 130.4 %reduce-scatter.2.cloned.1.call-start = ((), (), s32[]{:S(2)}) async-start(), calls=%async_computation.7 | async-start | bytes 10027008 | tf_op jit(solution)/shard_map/reduce_scatter | solution.py:194
  140.9 1.9 copy-start.5
  269.1 1.2 slice-start
  271.4 34.2 %all-to-all-start.3 = ((bf16[4,8,2,32,256]{4,3,2,0,1:T(8,128)(2,1)}), bf16[4,8,2,32,256]{4,3,2,0,1:T(8,128)(2,1)S(1)}, u32[]{:S(2)}, u32[]{:S(2)}) async-start(bf16[4,8,2,32,256]{4,3,2,0,1:T(8,128)(2,1)} %copy.208), calls=%async_computation.4 | async-start | bytes 2097152 | tf_op jit(solution)/shard_map/all_to_all | solution.py:73
  279.1 31.8 %copy-start.7 = (bf16[2048,64]{0,1:T(8,128)(2,1)S(1)}, bf16[2048,64]{0,1:T(8,128)(2,1)}, u32[]{:S(2)}) copy-start(bf16[2048,64]{0,1:T(8,128)(2,1)} %param.31) | copy-start | bytes 786436
  306.7 16.2 %all-to-all-start.4 = ((bf16[4,8,2,32,256]{4,3,2,1,0:T(8,128)(2,1)}), bf16[4,8,2,32,256]{4,3,2,1,0:T(8,128)(2,1)S(1)}, u32[]{:S(2)}, u32[]{:S(2)}) async-start(bf16[4,8,2,32,256]{4,3,2,1,0:T(8,128)(2,1)} %copy.209), calls=%async_computation.5 | async-start | bytes 2097152 | tf_op jit(solution)/shard_map/all_to_all | solution.py:74
  311.3 14.5 %copy-start.1 = (bf16[2048,384]{1,0:T(8,128)(2,1)S(1)}, bf16[2048,384]{1,0:T(8,128)(2,1)}, u32[]{:S(2)}) copy-start(bf16[2048,384]{1,0:T(8,128)(2,1)} %param.24) | copy-start | bytes 4718596
Sparse Core Ops, SparseCore 0:
  138.8 47.6 all-gather.1
  211.3 57.7 reduce-scatter.1

commit v5 on v3

--- a/solution.py
+++ b/solution.py
@@ -61,6 +61,13 @@
         :, None, :latent_width
     ].astype(jnp.float32)
     return summed.astype(jnp.bfloat16)
+
+
+def gather_columns(values):
+    parts = lax.axis_size("tp")
+    copies = jnp.broadcast_to(values[None], (parts,) + values.shape)
+    received = lax.all_to_all(copies, "tp", split_axis=0, concat_axis=0, tiled=True)
+    return jnp.concatenate(list(received), axis=-1)
 
 
 def shards(
@@ -91,7 +98,7 @@
     heads_here = key_absorb.shape[0]
     nope_width = key_absorb.shape[1]
     latent_width = key_absorb.shape[2]
-    whole = lax.all_gather(hidden, "tp", axis=1, tiled=True)
+    whole = gather_columns(hidden)
     normed = rms_norm(whole, attention_gain).astype(jnp.bfloat16)
     projected = jnp.dot(normed, query_weight, preferred_element_type=jnp.float32).reshape(
         token_count, heads_here, -1
@@ -106,7 +113,7 @@
     latent_part = jnp.dot(normed, latent_weight, preferred_element_type=jnp.float32).astype(
         jnp.bfloat16
     )
-    latent_raw = lax.all_gather(latent_part, "tp", axis=1, tiled=True)
+    latent_raw = gather_columns(latent_part)
     latent_new = rms_norm(latent_raw[:, :latent_width], latent_gain)
     key_new = rotate(latent_raw[:, latent_width:].astype(jnp.float32), positions)
     new_rows = jnp.concatenate([latent_new, key_new], axis=-1).astype(jnp.bfloat16)
@@ -125,7 +132,7 @@
     attention_blocks = lax.all_to_all(attention_blocks, "tp", split_axis=0, concat_axis=0, tiled=True)
     attention_columns = jnp.sum(attention_blocks, axis=0)
     mixed_columns = (hidden.astype(jnp.float32) + attention_columns).astype(jnp.bfloat16)
-    mixed = lax.all_gather(mixed_columns, "tp", axis=1, tiled=True)
+    mixed = gather_columns(mixed_columns)
     expert_in = rms_norm(mixed, feedforward_gain).astype(jnp.bfloat16)
     logits = jnp.dot(expert_in, router_weight, preferred_element_type=jnp.float32)
     expert_count = router_weight.shape[1]

time: 296 us -> 314 us (1.061)
  blocking collectives: 79.7 us -> 39.3 us
  local copies, waits for them, and re-layouts: 15.8 us -> 39.3 us
  waiting for transfers between devices: 131 us -> 148 us
  starting transfers between devices: 14.2 us -> 26 us
  other arithmetic: 13.3 us -> 16.9 us
    all_gather x3 -> x0, blocking collectives: 40 us -> none  [the longest x1 14 us: shards(): whole = lax.all_gather(hidden, 'tp', axis=1, tiled=True)]
    all_to_all x0 -> x3, waiting for transfers between devices: none -> 15.3 us  [gather_columns(): lax.all_to_all(copies, 'tp', split_axis=0, concat_axis=0, tiled=True)]
    unnamed x48 -> x65, local copies, waits for them, and re-layouts: 5.26 us -> 20.4 us
    all_to_all x0 -> x3, starting transfers between devices: none -> 12 us  [gather_columns(): lax.all_to_all(copies, 'tp', split_axis=0, concat_axis=0, tiled=True)]
    broadcast_in_dim x0 -> x3, local copies, waits for them, and re-layouts: none -> 3.31 us  [gather_columns(): copies = jnp.broadcast_to(values[None], (parts,) + values.shape)]
  transfers between devices with their start and end apart: 4 -> 7, of which waited for: 4 -> 7; matrix products, arithmetic and copies ran while one was open for 6% -> 9% of each run, Pallas kernels for 0% -> 0%
where the time goes in v5:
time: 314 us; the launch traced here: 312 us
  waiting for transfers between devices  148 us (47%)
  local copies, waits for them, and re-layouts  39.3 us (13%)
  blocking collectives  39.3 us (13%)
  matrix products  28 us (9%)
  starting transfers between devices  26 us (8%)
  other arithmetic  16.9 us (5%)
  between operations  14.6 us (5%)
    reduce_scatter x1, waiting for transfers between devices, shards(): lax.psum_scatter(both_parts, 'tp', scatter_dimension=1, tiled=True)  57.9 us
    all_gather x1, waiting for transfers between devices, shards(): slab = lax.all_gather(slab_columns, 'tp', axis=0, tiled=False)  41.1 us
    all_to_all x1, blocking collectives, shards(): lax.all_to_all(outgoing, 'req', split_axis=0, concat_axis=0, tiled=True)  39.3 us
    unnamed x65, local copies, waits for them, and re-layouts  20.4 us
    all_to_all x1, waiting for transfers between devices, shards(): lax.all_to_all(results, 'req', split_axis=0, concat_axis=0, tiled=True)  20.2 us
    all_to_all x3, waiting for transfers between devices, gather_columns(): lax.all_to_all(copies, 'tp', split_axis=0, concat_axis=0, tiled=True)  15.3 us
    all_to_all x1, waiting for transfers between devices, shards(): lax.all_to_all(attention_blocks, 'tp', split_axis=0, concat_axis=0, tiled...  13.3 us
    all_to_all x3, starting transfers between devices, gather_columns(): lax.all_to_all(copies, 'tp', split_axis=0, concat_axis=0, tiled=True)  12 us
  transfers between devices with their start and end apart: 7, of which 7 were waited for; matrix products, arithmetic and copies ran while one was open for 9% of the time, Pallas kernels for 0%

profile of v5, /device:TPU:32, one launch (start us, length us, event | category | flops | bytes accessed | tf_op | source)
XLA Modules:
  0.0 311.9 jit_solution(17065126474094691752)
XLA Ops:
  7.2 1.8 broadcast_in_dim.36
  9.0 4.5 %all-to-all-start = ((bf16[8,128,256]{2,1,0:T(8,128)(2,1)}), bf16[8,128,256]{2,1,0:T(8,128)(2,1)}, u32[]{:S(2)}, u32[]{:S(2)}) async-start(bf16[8,128,256]{2,1,0:T(8,128)(2,1)} %broadcast_in_dim.36), calls=%async_computation | async-start | bytes 1048576 | tf_op jit(solution)/shard_map/all_to_all | solution.py:69
  16.6 1.5 copy.157
  18.6 5.3 %all-to-all-done = bf16[8,128,256]{2,1,0:T(8,128)(2,1)} async-done(((bf16[8,128,256]{2,1,0:T(8,128)(2,1)}), bf16[8,128,256]{2,1,0:T(8,128)(2,1)}, u32[]{:S(2)}, u32[]{:S(2)}) %all-to-all-start) | async-done | bytes 524320 | tf_op jit(solution)/shard_map/all_to_all | solution.py:69
  23.9 0.8 fusion.85
  24.7 0.8 fusion.84
  25.6 0.8 fusion.83
  26.4 0.8 fusion.82
  27.3 0.8 fusion.81
  28.1 0.8 fusion.80
  29.0 0.8 fusion.79
  29.8 0.8 fusion.78
  30.8 1.3 convolution_convert_fusion.4
  32.9 4.0 %all-to-all-start.1 = ((bf16[8,128,72]{1,2,0:T(8,128)(2,1)}), bf16[8,128,72]{1,2,0:T(8,128)(2,1)}, u32[]{:S(2)}, u32[]{:S(2)}) async-start(bf16[8,128,72]{1,2,0:T(8,128)(2,1)} %broadcast_in_dim.38), calls=%async_computation.1 | async-start | bytes 294912 | tf_op jit(solution)/shard_map/all_to_all | solution.py:69
  39.9 1.3 fusion.26
  41.2 2.0 all-to-all-done.1
  50.0 0.8 copy.126
  52.2 1.0 copy.165
  53.3 0.8 copy.121
  54.8 1.0 subtract_convert_fusion
  56.0 2.9 select_reduce_fusion.1
  58.9 1.3 copy-done.1
  60.8 3.4 %fusion.29 = bf16[2,128,128]{1,2,0:T(8,128)(2,1)S(1)} fusion(bf16[2,512,128]{2,1,0:T(8,128)(2,1)S(1)} %copy-done.18, bf16[2048,576]{0,1:T(8,128)(2,1)} %param.22, f32[128,2,2048]{2,0,1:T(8,128)} %copy-done.1, f32[128,2]{0,1:T(2,128)S(1)} %get-tuple-element.9, f32[128,2]{0,1:T(2,128)S(1)} %multiply_maximum_fusion, pred[128,2048]{1,0:T(8,128)(4,1)S(1)} %fusion.49, ...), kind=kOutput, calls=%fused_computation.44 | convolution fusion | flops 572948480 | bytes 5049344 | tf_op jit(solution)/shard_map/thl,hlv->thv/dot_general | solution.py:124
  64.2 1.5 convolution_bitcast_fusion
  65.7 3.7 %all-to-all-start.2 = ((f32[8,128,256]{2,1,0:T(8,128)}), f32[8,128,256]{2,1,0:T(8,128)S(1)}, u32[]{:S(2)}, u32[]{:S(2)}) async-start(f32[8,128,256]{2,1,0:T(8,128)} %convolution_bitcast_fusion), calls=%async_computation.2 | async-start | bytes 2097152 | tf_op jit(solution)/shard_map/all_to_all | solution.py:132
  69.8 1.8 reduce-window.19
  71.9 13.3 %all-to-all-done.2 = f32[8,128,256]{2,1,0:T(8,128)S(1)} async-done(((f32[8,128,256]{2,1,0:T(8,128)}), f32[8,128,256]{2,1,0:T(8,128)S(1)}, u32[]{:S(2)}, u32[]{:S(2)}) %all-to-all-start.2) | async-done | bytes 1048608 | tf_op jit(solution)/shard_map/all_to_all | solution.py:132
  86.0 0.8 broadcast_in_dim.41
  86.8 3.5 %all-to-all-start.3 = ((bf16[8,128,256]{2,1,0:T(8,128)(2,1)}), bf16[8,128,256]{2,1,0:T(8,128)(2,1)S(1)}, u32[]{:S(2)}, u32[]{:S(2)}) async-start(bf16[8,128,256]{2,1,0:T(8,128)(2,1)} %broadcast_in_dim.41), calls=%async_computation.3 | async-start | bytes 1048576 | tf_op jit(solution)/shard_map/all_to_all | solution.py:69
  90.7 1.9 fusion.4
  92.6 8.0 %all-to-all-done.3 = bf16[8,128,256]{2,1,0:T(8,128)(2,1)S(1)} async-done(((bf16[8,128,256]{2,1,0:T(8,128)(2,1)}), bf16[8,128,256]{2,1,0:T(8,128)(2,1)S(1)}, u32[]{:S(2)}, u32[]{:S(2)}) %all-to-all-start.3) | async-done | bytes 524320 | tf_op jit(solution)/shard_map/all_to_all | solution.py:69
  101.9 39.3 %all_to_all.30 = bf16[32,2,32,256]{3,2,1,0:T(8,128)(2,1)} all-to-all(bf16[32,2,32,256]{3,2,1,0:T(8,128)(2,1)S(1)} %bitcast.222), channel_id=1, replica_groups=mesh['req'=32,'tp'=8] {'req'}, dimensions={0} | all-to-all | bytes 2097152 | tf_op jit(solution)/shard_map/all_to_all | solution.py:160
  141.5 1.6 copy.168
  143.2 1.5 copy.167
  145.1 2.0 convolution_convert_fusion.2
  147.1 41.1 %all-gather.3.cloned.1.call-done = bf16[256,2,32,256]{3,2,1,0:T(8,128)(2,1)} async-done(((bf16[32,2,32,256]{3,2,1,0:T(8,128)(2,1)}), bf16[256,2,32,256]{3,2,1,0:T(8,128)(2,1)}) %all-gather.3.cloned.1.call-update) | async-done | bytes 8388624 | tf_op jit(solution)/shard_map/all_gather | solution.py:161
  188.2 6.2 %fusion = f32[2,32,32,176,1]{3,2,1,0,4:T(8,128)S(1)} fusion(bf16[8,32,2,32,256]{4,3,2,1,0:T(8,128)(2,1)} %bitcast.234, bf16[2,8,256,176,1]{2,1,3,0,4:T(8,128)(2,1)} %bitcast.227), kind=kOutput, calls=%fused_computation.2 | convolution fusion | flops 1476395008 | bytes 11272192 | tf_op jit(solution)/shard_map/toesc,etcf->eosf/dot_general | solution.py:167
  194.9 2.3 fusion.2
  197.2 2.4 convolution_convert_fusion
  199.6 4.3 %pad_maximum_fusion = bf16[2176,2048]{1,0:T(8,128)(2,1)} fusion(bf16[128,2048]{1,0:T(8,128)(2,1)S(1)} %convolution_convert_fusion.2, bf16[2048,2048]{1,0:T(8,128)(2,1)S(1)} %bitcast.218), kind=kLoop, calls=%fused_computation.1 | loop fusion | flops 17825792 | bytes 17825792 | tf_op jit(solution)/shard_map/concatenate | solution.py:177
  203.9 57.9 %reduce-scatter.2.cloned.1.call-done = bf16[2176,256]{1,0:T(8,128)(2,1)} async-done(((bf16[2176,2048]{1,0:T(8,128)(2,1)}), bf16[2176,256]{1,0:T(8,128)(2,1)}) %reduce-scatter.2.cloned.1.call-update) | async-done | bytes 1114128 | tf_op jit(solution)/shard_map/reduce_scatter | solution.py:180
  261.8 1.2 slice-done
  263.0 1.1 copy.187
  264.2 10.0 %all-to-all-start.5 = ((bf16[32,2,32,256]{3,2,1,0:T(8,128)(2,1)}), bf16[32,2,32,256]{3,2,1,0:T(8,128)(2,1)S(1)}, u32[]{:S(2)}, u32[]{:S(2)}) async-start(bf16[32,2,32,256]{3,2,1,0:T(8,128)(2,1)} %bitcast.221), calls=%async_computation.6 | async-start | bytes 2097152 | tf_op jit(solution)/shard_map/all_to_all | solution.py:187
  274.8 5.1 %gather_fusion = f32[768]{0:T(1024)S(1)} fusion(f32[128,64]{0,1:T(8,128)S(1)} %fusion.35, s32[768]{0:T(1024)S(1)} %reshape.249), kind=kCustom, calls=%fused_computation | custom fusion | bytes 12288 | tf_op jit(solution)/shard_map/jit(take_along_axis)/gather | solution.py:142
  280.2 1.8 select_reduce_fusion
  282.0 20.2 %all-to-all-done.5 = bf16[32,2,32,256]{3,2,1,0:T(8,128)(2,1)S(1)} async-done(((bf16[32,2,32,256]{3,2,1,0:T(8,128)(2,1)}), bf16[32,2,32,256]{3,2,1,0:T(8,128)(2,1)S(1)}, u32[]{:S(2)}, u32[]{:S(2)}) %all-to-all-start.5) | async-done | bytes 1048608 | tf_op jit(solution)/shard_map/all_to_all | solution.py:187
  302.2 2.9 fusion.28
  (111 shorter events, 22.1 us)
Async XLA Ops:
  7.2 29.7 %copy-start = (bf16[2048,384]{1,0:T(8,128)(2,1)S(1)}, bf16[2048,384]{1,0:T(8,128)(2,1)}, u32[]{:S(2)}) copy-start(bf16[2048,384]{1,0:T(8,128)(2,1)} %param.24) | copy-start | bytes 4718596
  9.0 14.9 %all-to-all-start = ((bf16[8,128,256]{2,1,0:T(8,128)(2,1)}), bf16[8,128,256]{2,1,0:T(8,128)(2,1)}, u32[]{:S(2)}, u32[]{:S(2)}) async-start(bf16[8,128,256]{2,1,0:T(8,128)(2,1)} %broadcast_in_dim.36), calls=%async_computation | async-start | bytes 1048576 | tf_op jit(solution)/shard_map/all_to_all | solution.py:69
  32.9 10.3 %all-to-all-start.1 = ((bf16[8,128,72]{1,2,0:T(8,128)(2,1)}), bf16[8,128,72]{1,2,0:T(8,128)(2,1)}, u32[]{:S(2)}, u32[]{:S(2)}) async-start(bf16[8,128,72]{1,2,0:T(8,128)(2,1)} %broadcast_in_dim.38), calls=%async_computation.1 | async-start | bytes 294912 | tf_op jit(solution)/shard_map/all_to_all | solution.py:69
  37.7 0.7 copy-start.6
  58.9 1.4 copy-start.1
  58.9 1.9 copy-start.12
  58.9 1.9 copy-start.18
  64.2 5.2 %copy-start.14 = (s32[128,6]{0,1:T(8,128)S(1)}, s32[128,6]{0,1:T(8,128)}, u32[]{:S(2)}) copy-start(s32[128,6]{0,1:T(8,128)} %param.21) | copy-start | bytes 9220
  65.7 19.6 %copy-start.13 = (bf16[128,256]{1,0:T(8,128)(2,1)S(1)}, bf16[128,256]{1,0:T(8,128)(2,1)}, u32[]{:S(2)}) copy-start(bf16[128,256]{1,0:T(8,128)(2,1)} %param.19) | copy-start | bytes 196612
  65.7 19.6 %all-to-all-start.2 = ((f32[8,128,256]{2,1,0:T(8,128)}), f32[8,128,256]{2,1,0:T(8,128)S(1)}, u32[]{:S(2)}, u32[]{:S(2)}) async-start(f32[8,128,256]{2,1,0:T(8,128)} %convolution_bitcast_fusion), calls=%async_computation.2 | async-start | bytes 2097152 | tf_op jit(solution)/shard_map/all_to_all | solution.py:132
  69.6 20.8 %copy-start.15 = (bf16[2048]{0:T(1024)(128)(2,1)S(1)}, bf16[2048]{0:T(1024)(128)(2,1)}, u32[]{:S(2)}) copy-start(bf16[2048]{0:T(1024)(128)(2,1)} %param.30) | copy-start | bytes 12292
  85.3 0.6 copy-start.9
  86.8 13.7 %all-to-all-start.3 = ((bf16[8,128,256]{2,1,0:T(8,128)(2,1)}), bf16[8,128,256]{2,1,0:T(8,128)(2,1)S(1)}, u32[]{:S(2)}, u32[]{:S(2)}) async-start(bf16[8,128,256]{2,1,0:T(8,128)(2,1)} %broadcast_in_dim.41), calls=%async_computation.3 | async-start | bytes 1048576 | tf_op jit(solution)/shard_map/all_to_all | solution.py:69
  90.3 97.9 %all-gather.3.cloned.1.call-start = ((), (), s32[]{:S(2)}) async-start(), calls=%async_computation.8 | async-start | bytes 9437184 | tf_op jit(solution)/shard_map/all_gather | solution.py:161
  100.5 1.0 copy-start.5
  101.5 40.0 %copy-start.2 = (bf16[2,2048,176]{1,2,0:T(8,128)(2,1)S(1)}, bf16[2,2048,176]{1,2,0:T(8,128)(2,1)}, u32[]{:S(2)}) copy-start(bf16[2,2048,176]{1,2,0:T(8,128)(2,1)} %param.33) | copy-start | bytes 4325380
  141.3 120.5 %reduce-scatter.2.cloned.1.call-start = ((), (), s32[]{:S(2)}) async-start(), calls=%async_computation.7 | async-start | bytes 10027008 | tf_op jit(solution)/shard_map/reduce_scatter | solution.py:180
  141.5 1.7 copy-start.3
  143.2 1.5 copy-start.7
  143.2 1.9 copy-start.8
  188.2 6.3 %copy-start.4 = (bf16[44,8,8,256]{3,2,1,0:T(8,128)(2,1)S(1)}, bf16[44,8,8,256]{3,2,1,0:T(8,128)(2,1)}, u32[]{:S(2)}) copy-start(bf16[44,8,8,256]{3,2,1,0:T(8,128)(2,1)} %copy.167) | copy-start | bytes 4325380
  188.2 6.6 %copy-start.16 = (bf16[256,2,32,256]{3,2,1,0:T(8,128)(2,1)S(1)}, bf16[256,2,32,256]{3,2,1,0:T(8,128)(2,1)}, u32[]{:S(2)}) copy-start(bf16[256,2,32,256]{3,2,1,0:T(8,128)(2,1)} %all-gather.3.cloned.1.call-done) | copy-start | bytes 25165828
  194.9 2.3 copy-start.17
  261.8 1.2 slice-start
  263.0 11.4 %copy-start.11 = (bf16[2048,64]{0,1:T(8,128)(2,1)S(1)}, bf16[2048,64]{0,1:T(8,128)(2,1)}, u32[]{:S(2)}) copy-start(bf16[2048,64]{0,1:T(8,128)(2,1)} %param.31) | copy-start | bytes 786436
  264.2 38.0 %all-to-all-start.5 = ((bf16[32,2,32,256]{3,2,1,0:T(8,128)(2,1)}), bf16[32,2,32,256]{3,2,1,0:T(8,128)(2,1)S(1)}, u32[]{:S(2)}, u32[]{:S(2)}) async-start(bf16[32,2,32,256]{3,2,1,0:T(8,128)(2,1)} %bitcast.221), calls=%async_computation.6 | async-start | bytes 2097152 | tf_op jit(solution)/shard_map/all_to_all | solution.py:187
  274.8 27.4 %copy-start.10 = (bf16[128,256]{1,0:T(8,128)(2,1)S(1)}, bf16[128,256]{1,0:T(8,128)(2,1)}, u32[]{:S(2)}) copy-start(bf16[128,256]{1,0:T(8,128)(2,1)} %copy-done.9) | copy-start | bytes 196612
Sparse Core Ops, SparseCore 0:
  141.4 46.7 all-gather.2
  204.1 57.7 reduce-scatter.1

commit v6 on v3

--- a/solution.py
+++ b/solution.py
@@ -127,6 +127,12 @@
     mixed_columns = (hidden.astype(jnp.float32) + attention_columns).astype(jnp.bfloat16)
     mixed = lax.all_gather(mixed_columns, "tp", axis=1, tiled=True)
     expert_in = rms_norm(mixed, feedforward_gain).astype(jnp.bfloat16)
+    shared_inner = (
+        jax.nn.silu(jnp.dot(expert_in, shared_gate, preferred_element_type=jnp.float32))
+        * jnp.dot(expert_in, shared_up, preferred_element_type=jnp.float32)
+    ).astype(jnp.bfloat16)
+    shared_part = jnp.dot(shared_inner, shared_down, preferred_element_type=jnp.float32)
+    shared_columns = lax.psum_scatter(shared_part, "tp", scatter_dimension=1, tiled=True)
     logits = jnp.dot(expert_in, router_weight, preferred_element_type=jnp.float32)
     expert_count = router_weight.shape[1]
     top_count = routes.shape[1]
@@ -162,21 +168,15 @@
     partial_out = jnp.einsum(
         "eosf,efd->eosd", inner_units, expert_down, preferred_element_type=jnp.float32
     )
-    shared_inner = (
-        jax.nn.silu(jnp.dot(expert_in, shared_gate, preferred_element_type=jnp.float32))
-        * jnp.dot(expert_in, shared_up, preferred_element_type=jnp.float32)
-    ).astype(jnp.bfloat16)
-    shared_part = jnp.dot(shared_inner, shared_down, preferred_element_type=jnp.float32)
-    both_parts = jnp.concatenate(
-        [partial_out.reshape(slot_total, -1), shared_part], axis=0
-    ).astype(jnp.bfloat16)
-    both_columns = lax.psum_scatter(both_parts, "tp", scatter_dimension=1, tiled=True)
-    expert_sums = both_columns[:slot_total]
-    shared_sums = both_columns[slot_total:]
+    expert_sums = lax.psum_scatter(
+        partial_out.reshape(slot_total, -1).astype(jnp.bfloat16),
+        "tp",
+        scatter_dimension=1,
+        tiled=True,
+    )
     results = expert_sums.reshape(per_owner, owner_count, slot_count, column_width).transpose(
         1, 0, 2, 3
     )
-    shared_columns = shared_sums.astype(jnp.float32)
     returned = lax.all_to_all(results, "req", split_axis=0, concat_axis=0, tiled=True)
     routed = jnp.dot(
         combine_matrix,

time: 296 us -> 296 us (level)
  matrix products: 27 us -> 31.5 us
  waiting for transfers between devices: 131 us -> 127 us
  local copies, waits for them, and re-layouts: 15.8 us -> 19.1 us
  other arithmetic: 13.3 us -> 10.1 us
    all_to_all x1, waiting for transfers between devices: 20.2 us -> 2.78 us  [shards(): lax.all_to_all(results, 'req', split_axis=0, concat_axis=0, tiled=True)]
    reduce_scatter x1 -> x2, waiting for transfers between devices: 57.8 us -> 67.7 us  [the longest x1 50.3 us: shards(): lax.psum_scatter(partial_out.reshape(slot_total, -1).astype(jnp.bfloat16)...]
    concatenate x1 -> x0, other arithmetic: 4.3 us -> none  [shards(): jnp.concatenate([partial_out.reshape(slot_total, -1), shared_part], axis=0)]
    all_gather x1, waiting for transfers between devices: 41.8 us -> 45.3 us  [shards(): slab = lax.all_gather(slab_columns, 'tp', axis=0, tiled=False)]
    dot_general x1, matrix products: 2.39 us -> 5.62 us  [shards(): jnp.einsum('eosf,efd->eosd', inner_units, expert_down, preferred_element_...]
    unnamed x48 -> x50, local copies, waits for them, and re-layouts: 5.26 us -> 7.11 us
  transfers between devices with their start and end apart: 4 -> 5, of which waited for: 4 -> 5; matrix products, arithmetic and copies ran while one was open for 6% -> 7% of each run, Pallas kernels for 0% -> 0%
where the time goes in v6:
time: 296 us
  waiting for transfers between devices  127 us (43%)
  blocking collectives  79.6 us (27%)
  matrix products  31.5 us (11%)
  local copies, waits for them, and re-layouts  19.1 us (6%)
  between operations  14.3 us (5%)
  starting transfers between devices  14.2 us (5%)
  other arithmetic  10.1 us (3%)
    reduce_scatter x1, waiting for transfers between devices, shards(): lax.psum_scatter(partial_out.reshape(slot_total, -1).astype(jnp.bfloat16)...  50.3 us
    all_gather x1, waiting for transfers between devices, shards(): slab = lax.all_gather(slab_columns, 'tp', axis=0, tiled=False)  45.3 us
    all_to_all x1, blocking collectives, shards(): lax.all_to_all(outgoing, 'req', split_axis=0, concat_axis=0, tiled=True)  39.7 us
    reduce_scatter x1, waiting for transfers between devices, shards(): lax.psum_scatter(shared_part, 'tp', scatter_dimension=1, tiled=True)  17.4 us
    all_gather x1, blocking collectives, shards(): whole = lax.all_gather(hidden, 'tp', axis=1, tiled=True)  13.8 us
    all_gather x1, blocking collectives, shards(): mixed = lax.all_gather(mixed_columns, 'tp', axis=1, tiled=True)  13.2 us
    all_gather x1, blocking collectives, shards(): latent_raw = lax.all_gather(latent_part, 'tp', axis=1, tiled=True)  12.8 us
    all_to_all x1, waiting for transfers between devices, shards(): lax.all_to_all(attention_blocks, 'tp', split_axis=0, concat_axis=0, tiled...  11.1 us
  transfers between devices with their start and end apart: 5, of which 5 were waited for; matrix products, arithmetic and copies ran while one was open for 7% of the time, Pallas kernels for 0%

profile of v6, /device:TPU:32, one launch (start us, length us, event | category | flops | bytes accessed | tf_op | source)
XLA Modules:
  0.0 295.7 jit_solution(2839923760064517350)
XLA Ops:
  7.2 0.8 convert_element_type.102
  8.0 13.8 %all_gather.15 = bf16[128,2048]{1,0:T(8,128)(2,1)S(1)} all-gather(bf16[128,256]{1,0:T(8,128)(2,1)} %param.19), channel_id=1, replica_groups=mesh['req'=32,'tp'=8] {'tp'}, dimensions={1}, use_global_device_ids=true | all-gather | bytes 589824 | tf_op jit(solution)/shard_map/all_gather | solution.py:94
  22.0 1.4 convolution_convert_fusion.3
  23.4 12.8 %all_gather.16 = bf16[128,576]{0,1:T(8,128)(2,1)S(1)} all-gather(bf16[128,72]{0,1:T(8,128)(2,1)S(1)} %convolution_convert_fusion.3), channel_id=1, replica_groups=mesh['req'=32,'tp'=8] {'tp'}, dimensions={1}, use_global_device_ids=true | all-gather | bytes 165888 | tf_op jit(solution)/shard_map/all_gather | solution.py:109
  36.7 0.5 fusion.49
  37.2 0.8 fusion.63
  38.0 0.3 fusion.24
  38.3 0.7 copy.190
  39.3 0.7 copy.147
  40.2 0.8 copy.152
  41.0 0.8 copy.191
  41.9 0.5 copy-done.10
  42.4 1.5 copy.185
  43.9 1.0 subtract_convert_fusion
  45.1 2.9 select_reduce_fusion.1
  48.0 1.3 copy-done.1
  49.3 0.6 fusion.9
  49.9 3.3 %fusion.27 = bf16[2,128,128]{1,2,0:T(8,128)(2,1)S(1)} fusion(bf16[2,512,128]{2,1,0:T(8,128)(2,1)S(1)} %copy-done.21, bf16[2048,576]{0,1:T(8,128)(2,1)} %param.22, f32[128,2,2048]{2,0,1:T(8,128)} %copy-done.1, f32[128,2]{0,1:T(2,128)S(1)} %get-tuple-element.9, f32[128,2]{0,1:T(2,128)S(1)} %multiply_maximum_fusion, pred[128,2048]{1,0:T(8,128)(4,1)S(1)} %fusion.49, ...), kind=kOutput, calls=%fused_computation.40 | convolution fusion | flops 572948480 | bytes 5049344 | tf_op jit(solution)/shard_map/thl,hlv->thv/dot_general | solution.py:117
  53.3 1.5 convolution_bitcast_fusion
  54.8 3.9 %all-to-all-start = ((f32[8,128,256]{2,1,0:T(8,128)}), f32[8,128,256]{2,1,0:T(8,128)S(1)}, u32[]{:S(2)}, u32[]{:S(2)}) async-start(f32[8,128,256]{2,1,0:T(8,128)} %convolution_bitcast_fusion), calls=%async_computation | async-start | bytes 2097152 | tf_op jit(solution)/shard_map/all_to_all | solution.py:125
  59.2 1.8 reduce-window.19
  61.0 0.3 slice_reduce_fusion
  61.6 1.9 fusion
  63.5 11.1 %all-to-all-done = f32[8,128,256]{2,1,0:T(8,128)S(1)} async-done(((f32[8,128,256]{2,1,0:T(8,128)}), f32[8,128,256]{2,1,0:T(8,128)S(1)}, u32[]{:S(2)}, u32[]{:S(2)}) %all-to-all-start) | async-done | bytes 1048608 | tf_op jit(solution)/shard_map/all_to_all | solution.py:125
  74.7 13.2 %all_gather.17 = bf16[128,2048]{1,0:T(8,128)(2,1)S(1)} all-gather(bf16[128,256]{1,0:T(8,128)(2,1)S(1)} %add_convert_fusion), channel_id=1, replica_groups=mesh['req'=32,'tp'=8] {'tp'}, dimensions={1}, use_global_device_ids=true | all-gather | bytes 589824 | tf_op jit(solution)/shard_map/all_gather | solution.py:128
  88.2 0.2 fusion.40
  88.4 0.4 convolution_convert_fusion.1
  88.8 39.7 %all_to_all.15 = bf16[32,2,32,256]{3,2,1,0:T(8,128)(2,1)} all-to-all(bf16[32,2,32,256]{3,2,1,0:T(8,128)(2,1)S(1)} %bitcast.124), channel_id=1, replica_groups=mesh['req'=32,'tp'=8] {'req'}, dimensions={0} | all-to-all | bytes 2097152 | tf_op jit(solution)/shard_map/all_to_all | solution.py:159
  128.6 0.2 reduce-scatter.3.cloned.1.call-start
  128.8 1.6 copy.195
  130.5 0.4 copy.196
  130.9 45.3 %all-gather.3.cloned.1.call-done = bf16[256,2,32,256]{3,2,1,0:T(8,128)(2,1)} async-done(((bf16[32,2,32,256]{3,2,1,0:T(8,128)(2,1)}), bf16[256,2,32,256]{3,2,1,0:T(8,128)(2,1)}) %all-gather.3.cloned.1.call-update) | async-done | bytes 8388624 | tf_op jit(solution)/shard_map/all_gather | solution.py:160
  176.3 5.9 %fusion.11 = f32[2,32,32,176,1]{3,2,0,1,4:T(8,128)S(1)} fusion(bf16[8,32,2,32,256]{4,3,2,1,0:T(8,128)(2,1)} %bitcast.136, bf16[2,8,256,176,1]{2,1,3,0,4:T(8,128)(2,1)S(1)} %bitcast.128), kind=kOutput, calls=%fused_computation.23 | convolution fusion | flops 1476395008 | bytes 11272192 | tf_op jit(solution)/shard_map/toesc,etcf->eosf/dot_general | solution.py:166
  182.1 0.3 copy-done.19
  182.5 2.3 fusion.13
  184.8 5.6 %convolution_convert_fusion = bf16[2,32,32,2048]{3,2,1,0:T(8,128)(2,1)} fusion(bf16[2,176,2048]{2,1,0:T(8,128)(2,1)S(1)} %copy-done.20, f32[2,32,32,176,1]{3,2,0,1,4:T(8,128)S(1)} %fusion.11, f32[2,32,32,176,1]{3,2,0,1,4:T(8,128)S(1)} %fusion.13), kind=kOutput, calls=%fused_computation.4 | convolution fusion | flops 1482752000 | bytes 12713984 | tf_op jit(solution)/shard_map/eosf,efd->eosd/dot_general | solution.py:168
  190.5 1.0 copy-done.6
  191.6 1.0 fusion.83
  192.5 3.0 %fusion.31 = f32[128,2048]{1,0:T(8,128)} fusion(bf16[176,2048]{1,0:T(8,128)(2,1)S(1)} %copy-done.7, bf16[128,2048]{1,0:T(8,128)(2,1)S(1)} %fusion.40, bf16[2048,176]{0,1:T(8,128)(2,1)} %param.36, f32[128,176]{0,1:T(8,128)} %fusion.83), kind=kOutput, calls=%fused_computation.43 | convolution fusion | flops 184684544 | bytes 3104768 | tf_op jit(solution)/shard_map/dot_general | solution.py:134
  195.6 50.3 %reduce-scatter.3.cloned.1.call-done = bf16[2048,256]{1,0:T(8,128)(2,1)} async-done(((bf16[2048,2048]{1,0:T(8,128)(2,1)}), bf16[2048,256]{1,0:T(8,128)(2,1)}) %reduce-scatter.3.cloned.1.call-update) | async-done | bytes 1048592 | tf_op jit(solution)/shard_map/reduce_scatter | solution.py:171
  245.9 2.4 copy.166
  248.3 10.1 %all-to-all-start.2 = ((bf16[32,2,32,256]{3,2,1,0:T(8,128)(2,1)}), bf16[32,2,32,256]{3,2,1,0:T(8,128)(2,1)S(1)}, u32[]{:S(2)}, u32[]{:S(2)}) async-start(bf16[32,2,32,256]{3,2,1,0:T(8,128)(2,1)} %copy.166), calls=%async_computation.3 | async-start | bytes 2097152 | tf_op jit(solution)/shard_map/all_to_all | solution.py:180
  258.6 0.3 fusion.34
  258.9 5.1 %gather_fusion = f32[768]{0:T(1024)S(1)} fusion(f32[128,64]{0,1:T(8,128)S(1)} %fusion.34, s32[768]{0:T(1024)S(1)} %reshape.243), kind=kCustom, calls=%fused_computation | custom fusion | bytes 12288 | tf_op jit(solution)/shard_map/jit(take_along_axis)/gather | solution.py:141
  264.3 1.8 select_reduce_fusion
  266.1 17.4 %reduce-scatter.5.cloned.1.call-done = f32[128,256]{1,0:T(8,128)} async-done(((f32[128,2048]{1,0:T(8,128)}), f32[128,256]{1,0:T(8,128)}) %reduce-scatter.5.cloned.1.call-update) | async-done | bytes 131088 | tf_op jit(solution)/shard_map/reduce_scatter | solution.py:135
  283.5 2.8 all-to-all-done.2
  286.3 2.9 fusion.26
  (86 shorter events, 3.2 us)
Async XLA Ops:
  7.2 30.0 %copy-start = (bf16[2048,384]{1,0:T(8,128)(2,1)S(1)}, bf16[2048,384]{1,0:T(8,128)(2,1)}, u32[]{:S(2)}) copy-start(bf16[2048,384]{1,0:T(8,128)(2,1)} %param.24) | copy-start | bytes 4718596
  7.2 29.1 %copy-start.18 = (bf16[512]{0:T(512)(128)(2,1)S(1)}, bf16[512]{0:T(512)(128)(2,1)}, u32[]{:S(2)}) copy-start(bf16[512]{0:T(512)(128)(2,1)} %param.26) | copy-start | bytes 3076
  7.2 29.1 %copy-start.17 = (s32[128]{0:T(128)S(1)}, s32[128]{0:T(128)}, u32[]{:S(2)}) copy-start(s32[128]{0:T(128)} %param.20) | copy-start | bytes 1540
  22.0 16.0 %copy-start.13 = (bf16[2,128,512]{2,1,0:T(8,128)(2,1)S(1)}, bf16[2,128,512]{2,1,0:T(8,128)(2,1)}, u32[]{:S(2)}) copy-start(bf16[2,128,512]{2,1,0:T(8,128)(2,1)} %param.27) | copy-start | bytes 786436
  41.8 0.7 copy-start.10
  48.0 1.4 copy-start.1
  48.0 1.9 copy-start.12
  48.0 1.9 copy-start.21
  53.3 5.4 %copy-start.15 = (s32[128,6]{0,1:T(8,128)S(1)}, s32[128,6]{0,1:T(8,128)}, u32[]{:S(2)}) copy-start(s32[128,6]{0,1:T(8,128)} %param.21) | copy-start | bytes 9220
  53.3 5.8 %copy-start.16 = (bf16[2048]{0:T(1024)(128)(2,1)S(1)}, bf16[2048]{0:T(1024)(128)(2,1)}, u32[]{:S(2)}) copy-start(bf16[2048]{0:T(1024)(128)(2,1)} %param.30) | copy-start | bytes 12292
  54.8 19.9 %copy-start.14 = (bf16[128,256]{1,0:T(8,128)(2,1)S(1)}, bf16[128,256]{1,0:T(8,128)(2,1)}, u32[]{:S(2)}) copy-start(bf16[128,256]{1,0:T(8,128)(2,1)} %param.19) | copy-start | bytes 196612
  54.8 19.8 %all-to-all-start = ((f32[8,128,256]{2,1,0:T(8,128)}), f32[8,128,256]{2,1,0:T(8,128)S(1)}, u32[]{:S(2)}, u32[]{:S(2)}) async-start(f32[8,128,256]{2,1,0:T(8,128)} %convolution_bitcast_fusion), calls=%async_computation | async-start | bytes 2097152 | tf_op jit(solution)/shard_map/all_to_all | solution.py:125
  58.7 117.6 %all-gather.3.cloned.1.call-start = ((), (), s32[]{:S(2)}) async-start(), calls=%async_computation.7 | async-start | bytes 9437184 | tf_op jit(solution)/shard_map/all_gather | solution.py:160
  74.7 13.7 %copy-start.5 = (pred[2048,128]{1,0:T(8,128)(4,1)S(1)}, pred[2048,128]{1,0:T(8,128)(4,1)}, u32[]{:S(2)}) copy-start(pred[2048,128]{1,0:T(8,128)(4,1)} %fusion) | copy-start | bytes 786436
  74.7 13.5 %copy-start.8 = (bf16[128,256]{1,0:T(8,128)(2,1)}, bf16[128,256]{1,0:T(8,128)(2,1)S(1)}, u32[]{:S(2)}) copy-start(bf16[128,256]{1,0:T(8,128)(2,1)S(1)} %add_convert_fusion) | copy-start | bytes 196612
  88.4 40.4 %copy-start.2 = (bf16[2,2048,176]{1,2,0:T(8,128)(2,1)S(1)}, bf16[2,2048,176]{1,2,0:T(8,128)(2,1)}, u32[]{:S(2)}) copy-start(bf16[2,2048,176]{1,2,0:T(8,128)(2,1)} %param.32) | copy-start | bytes 4325380
  128.6 117.3 %reduce-scatter.3.cloned.1.call-start = ((), (), s32[]{:S(2)}) async-start(), calls=%async_computation.5 | async-start | bytes 9437184 | tf_op jit(solution)/shard_map/reduce_scatter | solution.py:171
  128.8 1.7 copy-start.3
  176.3 5.9 %copy-start.4 = (bf16[44,8,8,256]{3,2,1,0:T(8,128)(2,1)S(1)}, bf16[44,8,8,256]{3,2,1,0:T(8,128)(2,1)}, u32[]{:S(2)}) copy-start(bf16[44,8,8,256]{3,2,1,0:T(8,128)(2,1)} %copy.195) | copy-start | bytes 4325380
  176.3 6.2 %copy-start.19 = (bf16[256,2,32,256]{3,2,1,0:T(8,128)(2,1)S(1)}, bf16[256,2,32,256]{3,2,1,0:T(8,128)(2,1)}, u32[]{:S(2)}) copy-start(bf16[256,2,32,256]{3,2,1,0:T(8,128)(2,1)} %all-gather.3.cloned.1.call-done) | copy-start | bytes 25165828
  182.5 2.3 copy-start.20
  190.4 1.1 copy-start.6
  190.5 2.1 copy-start.7
  190.5 93.0 %reduce-scatter.5.cloned.1.call-start = ((), (), s32[]{:S(2)}) async-start(), calls=%async_computation.6 | async-start | bytes 1179648 | tf_op jit(solution)/shard_map/reduce_scatter | solution.py:135
  245.9 12.7 %copy-start.11 = (bf16[2048,64]{0,1:T(8,128)(2,1)S(1)}, bf16[2048,64]{0,1:T(8,128)(2,1)}, u32[]{:S(2)}) copy-start(bf16[2048,64]{0,1:T(8,128)(2,1)} %param.31) | copy-start | bytes 786436
  248.3 38.0 %all-to-all-start.2 = ((bf16[32,2,32,256]{3,2,1,0:T(8,128)(2,1)}), bf16[32,2,32,256]{3,2,1,0:T(8,128)(2,1)S(1)}, u32[]{:S(2)}, u32[]{:S(2)}) async-start(bf16[32,2,32,256]{3,2,1,0:T(8,128)(2,1)} %copy.166), calls=%async_computation.3 | async-start | bytes 2097152 | tf_op jit(solution)/shard_map/all_to_all | solution.py:180
  258.9 27.3 %copy-start.9 = (bf16[128,256]{1,0:T(8,128)(2,1)S(1)}, bf16[128,256]{1,0:T(8,128)(2,1)}, u32[]{:S(2)}) copy-start(bf16[128,256]{1,0:T(8,128)(2,1)} %copy-done.8) | copy-start | bytes 196612
Sparse Core Ops, SparseCore 0:
  128.7 47.4 all-gather.2
  190.6 55.2 reduce-scatter.2
  248.4 35.0 reduce-scatter.4

commit v7 on v6

--- a/solution.py
+++ b/solution.py
@@ -157,6 +157,7 @@
     )
     outgoing = outgoing.reshape(owner_count, per_owner, slot_count, column_width)
     slab_columns = lax.all_to_all(outgoing, "req", split_axis=0, concat_axis=0, tiled=True)
+    slab_columns, shared_columns = lax.optimization_barrier((slab_columns, shared_columns))
     slab = lax.all_gather(slab_columns, "tp", axis=0, tiled=False)
     gate_blocks = expert_gate.reshape(per_owner, tp_count, column_width, -1)
     up_blocks = expert_up.reshape(per_owner, tp_count, column_width, -1)

time: 296 us -> 304 us (1.027)
  other arithmetic: 10.1 us -> 13.6 us
    all_to_all x1, waiting for transfers between devices: 2.78 us -> 20.2 us  [shards(): lax.all_to_all(results, 'req', split_axis=0, concat_axis=0, tiled=True)]
    reduce_scatter x1, waiting for transfers between devices: 17.4 us -> 0.01 us  [shards(): lax.psum_scatter(shared_part, 'tp', scatter_dimension=1, tiled=True)]
    reduce_scatter x1, waiting for transfers between devices: 50.3 us -> 55.4 us  [shards(): lax.psum_scatter(partial_out.reshape(slot_total, -1).astype(jnp.bfloat16)...]
    unnamed x50 -> x48, local copies, waits for them, and re-layouts: 7.11 us -> 6.69 us
  transfers between devices with their start and end apart: 5 -> 5, of which waited for: 5 -> 4; matrix products, arithmetic and copies ran while one was open for 7% -> 6% of each run, Pallas kernels for 0% -> 0%
where the time goes in v7:
time: 304 us
  waiting for transfers between devices  130 us (43%)
  blocking collectives  79.3 us (26%)
  matrix products  32.6 us (11%)
  local copies, waits for them, and re-layouts  19.3 us (6%)
  between operations  14.2 us (5%)
  starting transfers between devices  14.1 us (5%)
  other arithmetic  13.6 us (4%)
    reduce_scatter x1, waiting for transfers between devices, shards(): lax.psum_scatter(partial_out.reshape(slot_total, -1).astype(jnp.bfloat16)...  55.4 us
    all_gather x1, waiting for transfers between devices, shards(): slab = lax.all_gather(slab_columns, 'tp', axis=0, tiled=False)  46.4 us
    all_to_all x1, blocking collectives, shards(): lax.all_to_all(outgoing, 'req', split_axis=0, concat_axis=0, tiled=True)  39.6 us
    all_to_all x1, waiting for transfers between devices, shards(): lax.all_to_all(results, 'req', split_axis=0, concat_axis=0, tiled=True)  20.2 us
    all_gather x1, blocking collectives, shards(): whole = lax.all_gather(hidden, 'tp', axis=1, tiled=True)  13.8 us
    all_gather x1, blocking collectives, shards(): mixed = lax.all_gather(mixed_columns, 'tp', axis=1, tiled=True)  13.1 us
    all_gather x1, blocking collectives, shards(): latent_raw = lax.all_gather(latent_part, 'tp', axis=1, tiled=True)  12.8 us
    all_to_all x1, starting transfers between devices, shards(): lax.all_to_all(results, 'req', split_axis=0, concat_axis=0, tiled=True)  10.1 us
  transfers between devices with their start and end apart: 5, of which 4 were waited for; matrix products, arithmetic and copies ran while one was open for 6% of the time, Pallas kernels for 0%

profile of v7, /device:TPU:32, one launch (start us, length us, event | category | flops | bytes accessed | tf_op | source)
XLA Modules:
  0.0 303.7 jit_solution(6982705115922020251)
XLA Ops:
  7.2 0.8 convert_element_type.102
  8.0 13.8 %all_gather.15 = bf16[128,2048]{1,0:T(8,128)(2,1)S(1)} all-gather(bf16[128,256]{1,0:T(8,128)(2,1)} %param.19), channel_id=1, replica_groups=mesh['req'=32,'tp'=8] {'tp'}, dimensions={1}, use_global_device_ids=true | all-gather | bytes 589824 | tf_op jit(solution)/shard_map/all_gather | solution.py:94
  22.0 1.4 convolution_convert_fusion.3
  23.4 12.8 %all_gather.16 = bf16[128,576]{0,1:T(8,128)(2,1)S(1)} all-gather(bf16[128,72]{0,1:T(8,128)(2,1)S(1)} %convolution_convert_fusion.3), channel_id=1, replica_groups=mesh['req'=32,'tp'=8] {'tp'}, dimensions={1}, use_global_device_ids=true | all-gather | bytes 165888 | tf_op jit(solution)/shard_map/all_gather | solution.py:109
  36.7 0.5 fusion.49
  37.2 0.8 fusion.63
  38.3 0.7 copy.190
  39.3 0.7 copy.147
  40.2 0.8 copy.152
  41.0 0.8 copy.191
  41.9 0.5 copy-done.9
  42.4 1.5 copy.185
  43.9 1.0 subtract_convert_fusion
  45.1 2.9 select_reduce_fusion.1
  48.0 1.3 copy-done.1
  49.3 0.6 fusion.9
  49.9 3.3 %fusion.27 = bf16[2,128,128]{1,2,0:T(8,128)(2,1)S(1)} fusion(bf16[2,512,128]{2,1,0:T(8,128)(2,1)S(1)} %copy-done.20, bf16[2048,576]{0,1:T(8,128)(2,1)} %param.22, f32[128,2,2048]{2,0,1:T(8,128)} %copy-done.1, f32[128,2]{0,1:T(2,128)S(1)} %get-tuple-element.13, f32[128,2]{0,1:T(2,128)S(1)} %multiply_maximum_fusion, pred[128,2048]{1,0:T(8,128)(4,1)S(1)} %fusion.49, ...), kind=kOutput, calls=%fused_computation.40 | convolution fusion | flops 572948480 | bytes 5049344 | tf_op jit(solution)/shard_map/thl,hlv->thv/dot_general | solution.py:117
  53.3 1.5 convolution_bitcast_fusion
  54.8 3.8 %all-to-all-start = ((f32[8,128,256]{2,1,0:T(8,128)}), f32[8,128,256]{2,1,0:T(8,128)S(1)}, u32[]{:S(2)}, u32[]{:S(2)}) async-start(f32[8,128,256]{2,1,0:T(8,128)} %convolution_bitcast_fusion), calls=%async_computation | async-start | bytes 2097152 | tf_op jit(solution)/shard_map/all_to_all | solution.py:125
  59.0 1.8 reduce-window.19
  61.1 0.6 reduce-window.20
  61.7 1.5 fusion.60
  63.2 0.8 reduce_sum.79
  64.1 1.9 fusion
  66.0 8.5 %all-to-all-done = f32[8,128,256]{2,1,0:T(8,128)S(1)} async-done(((f32[8,128,256]{2,1,0:T(8,128)}), f32[8,128,256]{2,1,0:T(8,128)S(1)}, u32[]{:S(2)}, u32[]{:S(2)}) %all-to-all-start) | async-done | bytes 1048608 | tf_op jit(solution)/shard_map/all_to_all | solution.py:125
  74.5 0.7 reduce_sum.77
  75.2 1.0 add_convert_fusion
  76.2 0.6 copy-done.7
  76.8 13.1 %all_gather.17 = bf16[128,2048]{1,0:T(8,128)(2,1)S(1)} all-gather(bf16[128,256]{1,0:T(8,128)(2,1)S(1)} %add_convert_fusion), channel_id=1, replica_groups=mesh['req'=32,'tp'=8] {'tp'}, dimensions={1}, use_global_device_ids=true | all-gather | bytes 589824 | tf_op jit(solution)/shard_map/all_gather | solution.py:128
  90.3 1.0 fusion.83
  91.3 3.0 fusion.31
  94.4 1.5 convolution_convert_fusion.1
  95.9 39.6 %all_to_all.15 = bf16[32,2,32,256]{3,2,1,0:T(8,128)(2,1)} all-to-all(bf16[32,2,32,256]{3,2,1,0:T(8,128)(2,1)S(1)} %bitcast.124), channel_id=1, replica_groups=mesh['req'=32,'tp'=8] {'req'}, dimensions={0} | all-to-all | bytes 2097152 | tf_op jit(solution)/shard_map/all_to_all | solution.py:159
  135.8 1.6 copy.195
  137.4 0.4 copy.196
  137.9 46.4 %all-gather.3.cloned.1.call-done = bf16[256,2,32,256]{3,2,1,0:T(8,128)(2,1)} async-done(((bf16[32,2,32,256]{3,2,1,0:T(8,128)(2,1)}), bf16[256,2,32,256]{3,2,1,0:T(8,128)(2,1)}) %all-gather.3.cloned.1.call-update) | async-done | bytes 8388624 | tf_op jit(solution)/shard_map/all_gather | solution.py:161
  184.3 5.9 %fusion.11 = f32[2,32,32,176,1]{3,2,0,1,4:T(8,128)S(1)} fusion(bf16[8,32,2,32,256]{4,3,2,1,0:T(8,128)(2,1)} %bitcast.136, bf16[2,8,256,176,1]{2,1,3,0,4:T(8,128)(2,1)S(1)} %bitcast.128), kind=kOutput, calls=%fused_computation.23 | convolution fusion | flops 1476395008 | bytes 11272192 | tf_op jit(solution)/shard_map/toesc,etcf->eosf/dot_general | solution.py:167
  190.1 0.3 copy-done.18
  190.5 2.3 fusion.13
  192.8 5.6 %convolution_convert_fusion = bf16[2,32,32,2048]{3,2,1,0:T(8,128)(2,1)} fusion(bf16[2,176,2048]{2,1,0:T(8,128)(2,1)S(1)} %copy-done.19, f32[2,32,32,176,1]{3,2,0,1,4:T(8,128)S(1)} %fusion.11, f32[2,32,32,176,1]{3,2,0,1,4:T(8,128)S(1)} %fusion.13), kind=kOutput, calls=%fused_computation.4 | convolution fusion | flops 1482752000 | bytes 12713984 | tf_op jit(solution)/shard_map/eosf,efd->eosd/dot_general | solution.py:169
  198.5 55.4 %reduce-scatter.5.cloned.1.call-done = bf16[2048,256]{1,0:T(8,128)(2,1)} async-done(((bf16[2048,2048]{1,0:T(8,128)(2,1)}), bf16[2048,256]{1,0:T(8,128)(2,1)}) %reduce-scatter.5.cloned.1.call-update) | async-done | bytes 1048592 | tf_op jit(solution)/shard_map/reduce_scatter | solution.py:172
  253.9 2.4 copy.166
  256.3 10.1 %all-to-all-start.2 = ((bf16[32,2,32,256]{3,2,1,0:T(8,128)(2,1)}), bf16[32,2,32,256]{3,2,1,0:T(8,128)(2,1)S(1)}, u32[]{:S(2)}, u32[]{:S(2)}) async-start(bf16[32,2,32,256]{3,2,1,0:T(8,128)(2,1)} %copy.166), calls=%async_computation.4 | async-start | bytes 2097152 | tf_op jit(solution)/shard_map/all_to_all | solution.py:181
  266.6 0.3 fusion.34
  267.0 5.1 %gather_fusion = f32[768]{0:T(1024)S(1)} fusion(f32[128,64]{0,1:T(8,128)S(1)} %fusion.34, s32[768]{0:T(1024)S(1)} %reshape.243), kind=kCustom, calls=%fused_computation | custom fusion | bytes 12288 | tf_op jit(solution)/shard_map/jit(take_along_axis)/gather | solution.py:141
  272.3 1.8 select_reduce_fusion
  274.1 20.2 %all-to-all-done.2 = bf16[32,2,32,256]{3,2,1,0:T(8,128)(2,1)S(1)} async-done(((bf16[32,2,32,256]{3,2,1,0:T(8,128)(2,1)}), bf16[32,2,32,256]{3,2,1,0:T(8,128)(2,1)S(1)}, u32[]{:S(2)}, u32[]{:S(2)}) %all-to-all-start.2) | async-done | bytes 1048608 | tf_op jit(solution)/shard_map/all_to_all | solution.py:181
  294.3 2.9 fusion.26
  (84 shorter events, 3.8 us)
Async XLA Ops:
  7.2 30.0 %copy-start = (bf16[2048,384]{1,0:T(8,128)(2,1)S(1)}, bf16[2048,384]{1,0:T(8,128)(2,1)}, u32[]{:S(2)}) copy-start(bf16[2048,384]{1,0:T(8,128)(2,1)} %param.24) | copy-start | bytes 4718596
  7.2 29.1 %copy-start.17 = (bf16[512]{0:T(512)(128)(2,1)S(1)}, bf16[512]{0:T(512)(128)(2,1)}, u32[]{:S(2)}) copy-start(bf16[512]{0:T(512)(128)(2,1)} %param.26) | copy-start | bytes 3076
  7.2 29.1 %copy-start.16 = (s32[128]{0:T(128)S(1)}, s32[128]{0:T(128)}, u32[]{:S(2)}) copy-start(s32[128]{0:T(128)} %param.20) | copy-start | bytes 1540
  22.0 16.0 %copy-start.12 = (bf16[2,128,512]{2,1,0:T(8,128)(2,1)S(1)}, bf16[2,128,512]{2,1,0:T(8,128)(2,1)}, u32[]{:S(2)}) copy-start(bf16[2,128,512]{2,1,0:T(8,128)(2,1)} %param.27) | copy-start | bytes 786436
  41.8 0.7 copy-start.9
  48.0 1.4 copy-start.1
  48.0 1.9 copy-start.11
  48.0 1.9 copy-start.20
  53.3 5.3 %copy-start.14 = (s32[128,6]{0,1:T(8,128)S(1)}, s32[128,6]{0,1:T(8,128)}, u32[]{:S(2)}) copy-start(s32[128,6]{0,1:T(8,128)} %param.21) | copy-start | bytes 9220
  53.3 5.7 %copy-start.15 = (bf16[2048]{0:T(1024)(128)(2,1)S(1)}, bf16[2048]{0:T(1024)(128)(2,1)}, u32[]{:S(2)}) copy-start(bf16[2048]{0:T(1024)(128)(2,1)} %param.30) | copy-start | bytes 12292
  54.8 19.7 %all-to-all-start = ((f32[8,128,256]{2,1,0:T(8,128)}), f32[8,128,256]{2,1,0:T(8,128)S(1)}, u32[]{:S(2)}, u32[]{:S(2)}) async-start(f32[8,128,256]{2,1,0:T(8,128)} %convolution_bitcast_fusion), calls=%async_computation | async-start | bytes 2097152 | tf_op jit(solution)/shard_map/all_to_all | solution.py:125
  58.5 77.0 %reduce-scatter.3.cloned.1.call-start = ((), (), s32[]{:S(2)}) async-start(), calls=%async_computation.5 | async-start | bytes 1179648 | tf_op jit(solution)/shard_map/reduce_scatter | solution.py:135
  61.7 28.6 %copy-start.5 = (bf16[2048,176]{0,1:T(8,128)(2,1)S(1)}, bf16[2048,176]{0,1:T(8,128)(2,1)}, u32[]{:S(2)}) copy-start(bf16[2048,176]{0,1:T(8,128)(2,1)} %param.35) | copy-start | bytes 2162692
  75.2 16.1 %copy-start.6 = (bf16[176,2048]{1,0:T(8,128)(2,1)S(1)}, bf16[176,2048]{1,0:T(8,128)(2,1)}, u32[]{:S(2)}) copy-start(bf16[176,2048]{1,0:T(8,128)(2,1)} %param.37) | copy-start | bytes 2162692
  76.2 0.6 copy-start.7
  94.3 41.4 %copy-start.2 = (bf16[2,2048,176]{1,2,0:T(8,128)(2,1)S(1)}, bf16[2,2048,176]{1,2,0:T(8,128)(2,1)}, u32[]{:S(2)}) copy-start(bf16[2,2048,176]{1,2,0:T(8,128)(2,1)} %param.32) | copy-start | bytes 4325380
  94.4 89.9 %all-gather.3.cloned.1.call-start = ((), (), s32[]{:S(2)}) async-start(), calls=%async_computation.7 | async-start | bytes 9437184 | tf_op jit(solution)/shard_map/all_gather | solution.py:161
  135.5 118.3 %reduce-scatter.5.cloned.1.call-start = ((), (), s32[]{:S(2)}) async-start(), calls=%async_computation.6 | async-start | bytes 9437184 | tf_op jit(solution)/shard_map/reduce_scatter | solution.py:172
  135.7 1.7 copy-start.3
  184.2 5.9 %copy-start.4 = (bf16[44,8,8,256]{3,2,1,0:T(8,128)(2,1)S(1)}, bf16[44,8,8,256]{3,2,1,0:T(8,128)(2,1)}, u32[]{:S(2)}) copy-start(bf16[44,8,8,256]{3,2,1,0:T(8,128)(2,1)} %copy.195) | copy-start | bytes 4325380
  184.3 6.2 %copy-start.18 = (bf16[256,2,32,256]{3,2,1,0:T(8,128)(2,1)S(1)}, bf16[256,2,32,256]{3,2,1,0:T(8,128)(2,1)}, u32[]{:S(2)}) copy-start(bf16[256,2,32,256]{3,2,1,0:T(8,128)(2,1)} %all-gather.3.cloned.1.call-done) | copy-start | bytes 25165828
  190.5 2.4 copy-start.19
  253.9 12.7 %copy-start.10 = (bf16[2048,64]{0,1:T(8,128)(2,1)S(1)}, bf16[2048,64]{0,1:T(8,128)(2,1)}, u32[]{:S(2)}) copy-start(bf16[2048,64]{0,1:T(8,128)(2,1)} %param.31) | copy-start | bytes 786436
  256.3 38.0 %all-to-all-start.2 = ((bf16[32,2,32,256]{3,2,1,0:T(8,128)(2,1)}), bf16[32,2,32,256]{3,2,1,0:T(8,128)(2,1)S(1)}, u32[]{:S(2)}, u32[]{:S(2)}) async-start(bf16[32,2,32,256]{3,2,1,0:T(8,128)(2,1)} %copy.166), calls=%async_computation.4 | async-start | bytes 2097152 | tf_op jit(solution)/shard_map/all_to_all | solution.py:181
  266.9 27.4 %copy-start.8 = (bf16[128,256]{1,0:T(8,128)(2,1)S(1)}, bf16[128,256]{1,0:T(8,128)(2,1)}, u32[]{:S(2)}) copy-start(bf16[128,256]{1,0:T(8,128)(2,1)} %copy-done.7) | copy-start | bytes 196612
  266.9 27.3 %copy-start.13 = (f32[128,256]{1,0:T(8,128)S(1)}, f32[128,256]{1,0:T(8,128)}, u32[]{:S(2)}) copy-start(f32[128,256]{1,0:T(8,128)} %reduce-scatter.3.cloned.1.call-done) | copy-start | bytes 393220
Sparse Core Ops, SparseCore 0:
  94.5 36.5 reduce-scatter.2
  135.6 48.5 all-gather.2
  198.6 55.2 reduce-scatter.4

commit v8 on v3

--- a/solution.py
+++ b/solution.py
@@ -103,10 +103,10 @@
     query_latent = jnp.einsum(
         "thn,hnl->thl", query_nope, key_absorb, preferred_element_type=jnp.float32
     ).astype(jnp.bfloat16)
-    latent_part = jnp.dot(normed, latent_weight, preferred_element_type=jnp.float32).astype(
+    latent_full = lax.all_gather(latent_weight, "tp", axis=1, tiled=True)
+    latent_raw = jnp.dot(normed, latent_full, preferred_element_type=jnp.float32).astype(
         jnp.bfloat16
     )
-    latent_raw = lax.all_gather(latent_part, "tp", axis=1, tiled=True)
     latent_new = rms_norm(latent_raw[:, :latent_width], latent_gain)
     key_new = rotate(latent_raw[:, latent_width:].astype(jnp.float32), positions)
     new_rows = jnp.concatenate([latent_new, key_new], axis=-1).astype(jnp.bfloat16)

time: 296 us -> 302 us (1.020)
  blocking collectives: 79.7 us -> 65.7 us
  waiting for transfers between devices: 131 us -> 141 us
  other arithmetic: 13.3 us -> 17.4 us
  local copies, waits for them, and re-layouts: 15.8 us -> 19.9 us
    all_gather x1 -> x0, blocking collectives: 12.8 us -> none  [shards(): latent_raw = lax.all_gather(latent_part, 'tp', axis=1, tiled=True)]
    all_gather x0 -> x1, waiting for transfers between devices: none -> 8.87 us  [shards(): latent_full = lax.all_gather(latent_weight, 'tp', axis=1, tiled=True)]
    unnamed x48 -> x50, local copies, waits for them, and re-layouts: 5.26 us -> 6.73 us
  transfers between devices with their start and end apart: 4 -> 5, of which waited for: 4 -> 5; matrix products, arithmetic and copies ran while one was open for 6% -> 9% of each run, Pallas kernels for 0% -> 0%
where the time goes in v8:
time: 302 us; the launch traced here: 301 us
  waiting for transfers between devices  141 us (47%)
  blocking collectives  65.7 us (22%)
  matrix products  29.3 us (10%)
  local copies, waits for them, and re-layouts  19.9 us (7%)
  other arithmetic  17.4 us (6%)
  between operations  14.2 us (5%)
  starting transfers between devices  14.1 us (5%)
    reduce_scatter x1, waiting for transfers between devices, shards(): lax.psum_scatter(both_parts, 'tp', scatter_dimension=1, tiled=True)  57.9 us
    all_gather x1, waiting for transfers between devices, shards(): slab = lax.all_gather(slab_columns, 'tp', axis=0, tiled=False)  41.8 us
    all_to_all x1, blocking collectives, shards(): lax.all_to_all(outgoing, 'req', split_axis=0, concat_axis=0, tiled=True)  38.6 us
    all_to_all x1, waiting for transfers between devices, shards(): lax.all_to_all(results, 'req', split_axis=0, concat_axis=0, tiled=True)  20.2 us
    all_gather x1, blocking collectives, shards(): whole = lax.all_gather(hidden, 'tp', axis=1, tiled=True)  13.8 us
    all_gather x1, blocking collectives, shards(): mixed = lax.all_gather(mixed_columns, 'tp', axis=1, tiled=True)  13.2 us
    all_to_all x1, waiting for transfers between devices, shards(): lax.all_to_all(attention_blocks, 'tp', split_axis=0, concat_axis=0, tiled...  11.1 us
    all_to_all x1, starting transfers between devices, shards(): lax.all_to_all(results, 'req', split_axis=0, concat_axis=0, tiled=True)  10.1 us
  transfers between devices with their start and end apart: 5, of which 5 were waited for; matrix products, arithmetic and copies ran while one was open for 9% of the time, Pallas kernels for 0%

profile of v8, /device:TPU:32, one launch (start us, length us, event | category | flops | bytes accessed | tf_op | source)
XLA Modules:
  0.0 301.0 jit_solution(16166487934097803946)
XLA Ops:
  7.2 0.7 all-gather.4.cloned.1.call-update
  7.9 0.7 convert_element_type.100
  8.6 0.7 convert_element_type.107
  9.3 0.8 copy.117
  10.3 13.8 %all_gather.15 = bf16[128,2048]{1,0:T(8,128)(2,1)S(1)} all-gather(bf16[128,256]{1,0:T(8,128)(2,1)} %param.19), channel_id=1, replica_groups=mesh['req'=32,'tp'=8] {'tp'}, dimensions={1}, use_global_device_ids=true | all-gather | bytes 589824 | tf_op jit(solution)/shard_map/all_gather | solution.py:94
  24.4 0.8 fusion.63
  25.2 0.7 copy-done.7
  26.0 0.7 copy.163
  26.7 1.5 copy.157
  28.2 0.6 negate_power_fusion
  28.8 0.5 fusion.81
  29.3 1.3 fusion.26
  30.6 1.2 fusion.49
  31.8 8.9 %all-gather.4.cloned.1.call-done = bf16[2048,576]{0,1:T(8,128)(2,1)} async-done(((bf16[2048,72]{0,1:T(8,128)(2,1)}), bf16[2048,576]{0,1:T(8,128)(2,1)}) %all-gather.4.cloned.1.call-update) | async-done | bytes 2359312 | tf_op jit(solution)/shard_map/all_gather | solution.py:106
  40.6 2.5 convolution_convert_fusion.4
  43.4 0.8 copy.126
  44.2 0.8 subtract_convert_fusion.1
  45.2 0.7 copy.121
  46.0 0.7 copy.123
  46.7 1.0 subtract_convert_fusion
  47.9 2.9 select_reduce_fusion.1
  50.8 1.3 copy-done.1
  52.1 0.6 fusion.13
  52.7 3.4 %fusion.29 = bf16[2,128,128]{1,2,0:T(8,128)(2,1)S(1)} fusion(bf16[2,512,128]{2,1,0:T(8,128)(2,1)} %param.28, bf16[2048,576]{0,1:T(8,128)(2,1)} %param.22, f32[128,2,2048]{2,0,1:T(8,128)} %copy-done.1, f32[128,2]{0,1:T(2,128)S(1)} %get-tuple-element.9, f32[128,2]{0,1:T(2,128)S(1)} %multiply_maximum_fusion, pred[128,2048]{1,0:T(8,128)(4,1)S(1)} %copy-done.6, ...), kind=kOutput, calls=%fused_computation.45 | convolution fusion | flops 572948480 | bytes 5049344 | tf_op jit(solution)/shard_map/thl,hlv->thv/dot_general | solution.py:117
  56.1 1.5 convolution_bitcast_fusion
  57.6 3.7 %all-to-all-start = ((f32[8,128,256]{2,1,0:T(8,128)}), f32[8,128,256]{2,1,0:T(8,128)S(1)}, u32[]{:S(2)}, u32[]{:S(2)}) async-start(f32[8,128,256]{2,1,0:T(8,128)} %convolution_bitcast_fusion), calls=%async_computation | async-start | bytes 2097152 | tf_op jit(solution)/shard_map/all_to_all | solution.py:125
  61.8 1.8 reduce-window.19
  64.2 1.9 fusion.4
  66.1 11.1 %all-to-all-done = f32[8,128,256]{2,1,0:T(8,128)S(1)} async-done(((f32[8,128,256]{2,1,0:T(8,128)}), f32[8,128,256]{2,1,0:T(8,128)S(1)}, u32[]{:S(2)}, u32[]{:S(2)}) %all-to-all-start) | async-done | bytes 1048608 | tf_op jit(solution)/shard_map/all_to_all | solution.py:125
  77.3 13.2 %all_gather.17 = bf16[128,2048]{1,0:T(8,128)(2,1)S(1)} all-gather(bf16[128,256]{1,0:T(8,128)(2,1)S(1)} %add_convert_fusion), channel_id=1, replica_groups=mesh['req'=32,'tp'=8] {'tp'}, dimensions={1}, use_global_device_ids=true | all-gather | bytes 589824 | tf_op jit(solution)/shard_map/all_gather | solution.py:128
  91.0 0.4 convolution_convert_fusion.1
  91.4 38.6 %all_to_all.15 = bf16[32,2,32,256]{3,2,1,0:T(8,128)(2,1)} all-to-all(bf16[32,2,32,256]{3,2,1,0:T(8,128)(2,1)S(1)} %bitcast.126), channel_id=1, replica_groups=mesh['req'=32,'tp'=8] {'req'}, dimensions={0} | all-to-all | bytes 2097152 | tf_op jit(solution)/shard_map/all_to_all | solution.py:153
  130.3 1.6 copy.168
  131.9 1.5 copy.167
  133.9 2.0 convolution_convert_fusion.2
  135.9 41.8 %all-gather.6.cloned.1.call-done = bf16[256,2,32,256]{3,2,1,0:T(8,128)(2,1)} async-done(((bf16[32,2,32,256]{3,2,1,0:T(8,128)(2,1)}), bf16[256,2,32,256]{3,2,1,0:T(8,128)(2,1)}) %all-gather.6.cloned.1.call-update) | async-done | bytes 8388624 | tf_op jit(solution)/shard_map/all_gather | solution.py:154
  177.7 6.2 %fusion = f32[2,32,32,176,1]{3,2,1,0,4:T(8,128)S(1)} fusion(bf16[8,32,2,32,256]{4,3,2,1,0:T(8,128)(2,1)} %bitcast.138, bf16[2,8,256,176,1]{2,1,3,0,4:T(8,128)(2,1)} %bitcast.131), kind=kOutput, calls=%fused_computation.2 | convolution fusion | flops 1476395008 | bytes 11272192 | tf_op jit(solution)/shard_map/toesc,etcf->eosf/dot_general | solution.py:160
  184.3 2.3 fusion.2
  186.7 2.4 convolution_convert_fusion
  189.1 4.3 %pad_maximum_fusion = bf16[2176,2048]{1,0:T(8,128)(2,1)} fusion(bf16[128,2048]{1,0:T(8,128)(2,1)S(1)} %convolution_convert_fusion.2, bf16[2048,2048]{1,0:T(8,128)(2,1)S(1)} %bitcast.122), kind=kLoop, calls=%fused_computation.1 | loop fusion | flops 17825792 | bytes 17825792 | tf_op jit(solution)/shard_map/concatenate | solution.py:170
  193.4 57.9 %reduce-scatter.2.cloned.1.call-done = bf16[2176,256]{1,0:T(8,128)(2,1)} async-done(((bf16[2176,2048]{1,0:T(8,128)(2,1)}), bf16[2176,256]{1,0:T(8,128)(2,1)}) %reduce-scatter.2.cloned.1.call-update) | async-done | bytes 1114128 | tf_op jit(solution)/shard_map/reduce_scatter | solution.py:173
  251.3 1.2 slice-done
  252.5 1.1 copy.187
  253.6 10.1 %all-to-all-start.2 = ((bf16[32,2,32,256]{3,2,1,0:T(8,128)(2,1)}), bf16[32,2,32,256]{3,2,1,0:T(8,128)(2,1)S(1)}, u32[]{:S(2)}, u32[]{:S(2)}) async-start(bf16[32,2,32,256]{3,2,1,0:T(8,128)(2,1)} %bitcast.125), calls=%async_computation.3 | async-start | bytes 2097152 | tf_op jit(solution)/shard_map/all_to_all | solution.py:180
  264.3 5.1 %gather_fusion = f32[768]{0:T(1024)S(1)} fusion(f32[128,64]{0,1:T(8,128)S(1)} %fusion.35, s32[768]{0:T(1024)S(1)} %reshape.246), kind=kCustom, calls=%fused_computation | custom fusion | bytes 12288 | tf_op jit(solution)/shard_map/jit(take_along_axis)/gather | solution.py:135
  269.7 1.8 select_reduce_fusion
  271.5 20.2 %all-to-all-done.2 = bf16[32,2,32,256]{3,2,1,0:T(8,128)(2,1)S(1)} async-done(((bf16[32,2,32,256]{3,2,1,0:T(8,128)(2,1)}), bf16[32,2,32,256]{3,2,1,0:T(8,128)(2,1)S(1)}, u32[]{:S(2)}, u32[]{:S(2)}) %all-to-all-start.2) | async-done | bytes 1048608 | tf_op jit(solution)/shard_map/all_to_all | solution.py:180
  291.7 2.9 fusion.28
  (88 shorter events, 4.6 us)
Async XLA Ops:
  7.2 17.2 %copy-start = (bf16[2048,384]{1,0:T(8,128)(2,1)S(1)}, bf16[2048,384]{1,0:T(8,128)(2,1)}, u32[]{:S(2)}) copy-start(bf16[2048,384]{1,0:T(8,128)(2,1)} %param.24) | copy-start | bytes 4718596
  7.2 33.4 %all-gather.4.cloned.1.call-start = ((), (), s32[]{:S(2)}) async-start(), calls=%async_computation.4 | async-start | bytes 2654208 | tf_op jit(solution)/shard_map/all_gather | solution.py:106
  24.4 0.8 copy-start.19
  24.4 4.4 %copy-start.18 = (s32[128]{0:T(128)S(1)}, s32[128]{0:T(128)}, u32[]{:S(2)}) copy-start(s32[128]{0:T(128)} %param.20) | copy-start | bytes 1540
  25.2 0.7 copy-start.7
  45.1 5.7 %copy-start.12 = (bf16[128,576]{0,1:T(8,128)(2,1)}, bf16[128,576]{0,1:T(8,128)(2,1)S(1)}, u32[]{:S(2)}) copy-start(bf16[128,576]{0,1:T(8,128)(2,1)S(1)} %pad_maximum_fusion.2) | copy-start | bytes 442372
  47.9 4.3 %copy-start.6 = (pred[128,2048]{1,0:T(8,128)(4,1)S(1)}, pred[128,2048]{1,0:T(8,128)(4,1)}, u32[]{:S(2)}) copy-start(pred[128,2048]{1,0:T(8,128)(4,1)} %fusion.49) | copy-start | bytes 786436
  50.8 1.4 copy-start.1
  50.8 1.9 copy-start.14
  56.1 5.2 %copy-start.16 = (s32[128,6]{0,1:T(8,128)S(1)}, s32[128,6]{0,1:T(8,128)}, u32[]{:S(2)}) copy-start(s32[128,6]{0,1:T(8,128)} %param.21) | copy-start | bytes 9220
  56.1 5.6 %copy-start.17 = (bf16[2048]{0:T(1024)(128)(2,1)S(1)}, bf16[2048]{0:T(1024)(128)(2,1)}, u32[]{:S(2)}) copy-start(bf16[2048]{0:T(1024)(128)(2,1)} %param.30) | copy-start | bytes 12292
  57.6 19.7 %copy-start.15 = (bf16[128,256]{1,0:T(8,128)(2,1)S(1)}, bf16[128,256]{1,0:T(8,128)(2,1)}, u32[]{:S(2)}) copy-start(bf16[128,256]{1,0:T(8,128)(2,1)} %param.19) | copy-start | bytes 196612
  57.6 19.6 %all-to-all-start = ((f32[8,128,256]{2,1,0:T(8,128)}), f32[8,128,256]{2,1,0:T(8,128)S(1)}, u32[]{:S(2)}, u32[]{:S(2)}) async-start(f32[8,128,256]{2,1,0:T(8,128)} %convolution_bitcast_fusion), calls=%async_computation | async-start | bytes 2097152 | tf_op jit(solution)/shard_map/all_to_all | solution.py:125
  61.3 116.4 %all-gather.6.cloned.1.call-start = ((), (), s32[]{:S(2)}) async-start(), calls=%async_computation.6 | async-start | bytes 9437184 | tf_op jit(solution)/shard_map/all_gather | solution.py:154
  77.3 13.7 %copy-start.5 = (pred[2048,128]{1,0:T(8,128)(4,1)S(1)}, pred[2048,128]{1,0:T(8,128)(4,1)}, u32[]{:S(2)}) copy-start(pred[2048,128]{1,0:T(8,128)(4,1)} %fusion.4) | copy-start | bytes 786436
  77.3 13.5 %copy-start.10 = (bf16[128,256]{1,0:T(8,128)(2,1)}, bf16[128,256]{1,0:T(8,128)(2,1)S(1)}, u32[]{:S(2)}) copy-start(bf16[128,256]{1,0:T(8,128)(2,1)S(1)} %add_convert_fusion) | copy-start | bytes 196612
  91.0 39.3 %copy-start.2 = (bf16[2,2048,176]{1,2,0:T(8,128)(2,1)S(1)}, bf16[2,2048,176]{1,2,0:T(8,128)(2,1)}, u32[]{:S(2)}) copy-start(bf16[2,2048,176]{1,2,0:T(8,128)(2,1)} %param.33) | copy-start | bytes 4325380
  130.0 121.2 %reduce-scatter.2.cloned.1.call-start = ((), (), s32[]{:S(2)}) async-start(), calls=%async_computation.5 | async-start | bytes 10027008 | tf_op jit(solution)/shard_map/reduce_scatter | solution.py:173
  130.3 1.7 copy-start.3
  131.9 1.5 copy-start.8
  131.9 1.9 copy-start.9
  177.7 6.3 %copy-start.4 = (bf16[44,8,8,256]{3,2,1,0:T(8,128)(2,1)S(1)}, bf16[44,8,8,256]{3,2,1,0:T(8,128)(2,1)}, u32[]{:S(2)}) copy-start(bf16[44,8,8,256]{3,2,1,0:T(8,128)(2,1)} %copy.167) | copy-start | bytes 4325380
  177.7 6.6 %copy-start.20 = (bf16[256,2,32,256]{3,2,1,0:T(8,128)(2,1)S(1)}, bf16[256,2,32,256]{3,2,1,0:T(8,128)(2,1)}, u32[]{:S(2)}) copy-start(bf16[256,2,32,256]{3,2,1,0:T(8,128)(2,1)} %all-gather.6.cloned.1.call-done) | copy-start | bytes 25165828
  184.3 2.4 copy-start.21
  251.3 1.2 slice-start
  252.5 11.5 %copy-start.13 = (bf16[2048,64]{0,1:T(8,128)(2,1)S(1)}, bf16[2048,64]{0,1:T(8,128)(2,1)}, u32[]{:S(2)}) copy-start(bf16[2048,64]{0,1:T(8,128)(2,1)} %param.31) | copy-start | bytes 786436
  253.6 38.0 %all-to-all-start.2 = ((bf16[32,2,32,256]{3,2,1,0:T(8,128)(2,1)}), bf16[32,2,32,256]{3,2,1,0:T(8,128)(2,1)S(1)}, u32[]{:S(2)}, u32[]{:S(2)}) async-start(bf16[32,2,32,256]{3,2,1,0:T(8,128)(2,1)} %bitcast.125), calls=%async_computation.3 | async-start | bytes 2097152 | tf_op jit(solution)/shard_map/all_to_all | solution.py:180
  264.3 27.3 %copy-start.11 = (bf16[128,256]{1,0:T(8,128)(2,1)S(1)}, bf16[128,256]{1,0:T(8,128)(2,1)}, u32[]{:S(2)}) copy-start(bf16[128,256]{1,0:T(8,128)(2,1)} %copy-done.10) | copy-start | bytes 196612
Sparse Core Ops, SparseCore 0:
  9.8 30.7 all-gather.3
  130.2 47.4 all-gather.5
  193.5 57.7 reduce-scatter.1

commit v9 on v3

--- a/solution.py
+++ b/solution.py
@@ -121,9 +121,11 @@
         head_values.reshape(token_count, -1), output_weight, preferred_element_type=jnp.float32
     )
     tp_count = lax.axis_size("tp")
-    attention_blocks = attention.reshape(token_count, tp_count, column_width).transpose(1, 0, 2)
+    attention_blocks = (
+        attention.reshape(token_count, tp_count, column_width).transpose(1, 0, 2).astype(jnp.bfloat16)
+    )
     attention_blocks = lax.all_to_all(attention_blocks, "tp", split_axis=0, concat_axis=0, tiled=True)
-    attention_columns = jnp.sum(attention_blocks, axis=0)
+    attention_columns = jnp.sum(attention_blocks.astype(jnp.float32), axis=0)
     mixed_columns = (hidden.astype(jnp.float32) + attention_columns).astype(jnp.bfloat16)
     mixed = lax.all_gather(mixed_columns, "tp", axis=1, tiled=True)
     expert_in = rms_norm(mixed, feedforward_gain).astype(jnp.bfloat16)

time: 296 us -> 290 us (0.980)
  waiting for transfers between devices: 131 us -> 125 us
    all_to_all x1, waiting for transfers between devices: 11.1 us -> 5.51 us  [shards(): lax.all_to_all(attention_blocks, 'tp', split_axis=0, concat_axis=0, tiled...]
where the time goes in v9:
time: 290 us
  waiting for transfers between devices  125 us (43%)
  blocking collectives  79.6 us (27%)
  matrix products  26.8 us (9%)
  local copies, waits for them, and re-layouts  15.8 us (5%)
  between operations  14.6 us (5%)
  starting transfers between devices  14.1 us (5%)
  other arithmetic  13.3 us (5%)
    reduce_scatter x1, waiting for transfers between devices, shards(): lax.psum_scatter(both_parts, 'tp', scatter_dimension=1, tiled=True)  57.9 us
    all_gather x1, waiting for transfers between devices, shards(): slab = lax.all_gather(slab_columns, 'tp', axis=0, tiled=False)  41.8 us
    all_to_all x1, blocking collectives, shards(): lax.all_to_all(outgoing, 'req', split_axis=0, concat_axis=0, tiled=True)  39.7 us
    all_to_all x1, waiting for transfers between devices, shards(): lax.all_to_all(results, 'req', split_axis=0, concat_axis=0, tiled=True)  20.2 us
    all_gather x1, blocking collectives, shards(): whole = lax.all_gather(hidden, 'tp', axis=1, tiled=True)  14 us
    all_gather x1, blocking collectives, shards(): mixed = lax.all_gather(mixed_columns, 'tp', axis=1, tiled=True)  13.1 us
    all_gather x1, blocking collectives, shards(): latent_raw = lax.all_gather(latent_part, 'tp', axis=1, tiled=True)  12.8 us
    all_to_all x1, starting transfers between devices, shards(): lax.all_to_all(results, 'req', split_axis=0, concat_axis=0, tiled=True)  10.1 us
  transfers between devices with their start and end apart: 4, of which 4 were waited for; matrix products, arithmetic and copies ran while one was open for 6% of the time, Pallas kernels for 0%

profile of v9, /device:TPU:32, one launch (start us, length us, event | category | flops | bytes accessed | tf_op | source)
XLA Modules:
  0.0 289.5 jit_solution(10051229672015895156)
XLA Ops:
  7.2 14.0 %all_gather.15 = bf16[128,2048]{1,0:T(8,128)(2,1)S(1)} all-gather(bf16[128,256]{1,0:T(8,128)(2,1)} %param.19), channel_id=1, replica_groups=mesh['req'=32,'tp'=8] {'tp'}, dimensions={1}, use_global_device_ids=true | all-gather | bytes 589824 | tf_op jit(solution)/shard_map/all_gather | solution.py:94
  21.2 0.2 fusion.37
  21.4 0.7 convert_element_type.109
  22.1 1.3 convolution_convert_fusion.5
  23.4 12.8 %all_gather.16 = bf16[128,576]{0,1:T(8,128)(2,1)S(1)} all-gather(bf16[128,72]{0,1:T(8,128)(2,1)S(1)} %convolution_convert_fusion.5), channel_id=1, replica_groups=mesh['req'=32,'tp'=8] {'tp'}, dimensions={1}, use_global_device_ids=true | all-gather | bytes 165888 | tf_op jit(solution)/shard_map/all_gather | solution.py:109
  36.4 0.2 reduce-window.18
  37.0 0.1 subtract_convert_fusion.1
  37.4 0.4 copy-done.10
  37.9 0.8 fusion.64
  38.9 0.3 fusion.27
  39.2 0.5 fusion.50
  39.7 0.2 multiply_reduce_fusion
  39.9 2.9 select_reduce_fusion.1
  42.8 0.6 fusion.13
  43.4 0.8 copy-done.1
  44.2 1.5 copy.157
  45.7 3.3 %fusion.30 = bf16[2,128,128]{1,2,0:T(8,128)(2,1)S(1)} fusion(bf16[2,512,128]{2,1,0:T(8,128)(2,1)S(1)} %copy-done.20, bf16[2048,576]{0,1:T(8,128)(2,1)} %param.22, f32[128,2,2048]{2,0,1:T(8,128)} %copy-done.1, f32[128,2]{0,1:T(2,128)S(1)} %get-tuple-element.9, f32[128,2]{0,1:T(2,128)S(1)} %multiply_maximum_fusion, pred[128,2048]{1,0:T(8,128)(4,1)S(1)} %fusion.50, ...), kind=kOutput, calls=%fused_computation.45 | convolution fusion | flops 572948480 | bytes 5049344 | tf_op jit(solution)/shard_map/thl,hlv->thv/dot_general | solution.py:117
  49.0 1.3 fusion.20
  50.3 3.8 %all-to-all-start = ((bf16[8,128,256]{2,1,0:T(8,128)(2,1)}), bf16[8,128,256]{2,1,0:T(8,128)(2,1)S(1)}, u32[]{:S(2)}, u32[]{:S(2)}) async-start(bf16[8,128,256]{2,1,0:T(8,128)(2,1)} %fusion.20), calls=%async_computation | async-start | bytes 1048576 | tf_op jit(solution)/shard_map/all_to_all | solution.py:127
  54.6 1.8 reduce-window.19
  56.4 0.3 slice_reduce_fusion
  57.0 1.9 fusion.4
  58.9 5.5 %all-to-all-done = bf16[8,128,256]{2,1,0:T(8,128)(2,1)S(1)} async-done(((bf16[8,128,256]{2,1,0:T(8,128)(2,1)}), bf16[8,128,256]{2,1,0:T(8,128)(2,1)S(1)}, u32[]{:S(2)}, u32[]{:S(2)}) %all-to-all-start) | async-done | bytes 524320 | tf_op jit(solution)/shard_map/all_to_all | solution.py:127
  64.5 13.1 %all_gather.17 = bf16[128,2048]{1,0:T(8,128)(2,1)S(1)} all-gather(bf16[128,256]{1,0:T(8,128)(2,1)S(1)} %add_convert_fusion), channel_id=1, replica_groups=mesh['req'=32,'tp'=8] {'tp'}, dimensions={1}, use_global_device_ids=true | all-gather | bytes 589824 | tf_op jit(solution)/shard_map/all_gather | solution.py:130
  77.6 0.2 fusion.40
  77.8 0.2 fusion.42
  78.1 0.4 convolution_convert_fusion.1
  78.5 39.7 %all_to_all.15 = bf16[32,2,32,256]{3,2,1,0:T(8,128)(2,1)} all-to-all(bf16[32,2,32,256]{3,2,1,0:T(8,128)(2,1)S(1)} %bitcast.126), channel_id=1, replica_groups=mesh['req'=32,'tp'=8] {'req'}, dimensions={0} | all-to-all | bytes 2097152 | tf_op jit(solution)/shard_map/all_to_all | solution.py:155
  118.2 0.2 reduce-scatter.2.cloned.1.call-start
  118.5 1.6 copy.168
  120.1 1.5 copy.167
  121.7 0.3 fusion.83
  122.0 2.0 convolution_convert_fusion.2
  124.1 41.8 %all-gather.3.cloned.1.call-done = bf16[256,2,32,256]{3,2,1,0:T(8,128)(2,1)} async-done(((bf16[32,2,32,256]{3,2,1,0:T(8,128)(2,1)}), bf16[256,2,32,256]{3,2,1,0:T(8,128)(2,1)}) %all-gather.3.cloned.1.call-update) | async-done | bytes 8388624 | tf_op jit(solution)/shard_map/all_gather | solution.py:156
  165.9 6.2 %fusion = f32[2,32,32,176,1]{3,2,1,0,4:T(8,128)S(1)} fusion(bf16[8,32,2,32,256]{4,3,2,1,0:T(8,128)(2,1)} %bitcast.138, bf16[2,8,256,176,1]{2,1,3,0,4:T(8,128)(2,1)} %bitcast.131), kind=kOutput, calls=%fused_computation.2 | convolution fusion | flops 1476395008 | bytes 11272192 | tf_op jit(solution)/shard_map/toesc,etcf->eosf/dot_general | solution.py:162
  172.2 0.4 copy-done.18
  172.5 2.3 fusion.2
  174.9 2.4 convolution_convert_fusion
  177.3 4.3 %pad_maximum_fusion = bf16[2176,2048]{1,0:T(8,128)(2,1)} fusion(bf16[128,2048]{1,0:T(8,128)(2,1)S(1)} %convolution_convert_fusion.2, bf16[2048,2048]{1,0:T(8,128)(2,1)S(1)} %bitcast.122), kind=kLoop, calls=%fused_computation.1 | loop fusion | flops 17825792 | bytes 17825792 | tf_op jit(solution)/shard_map/concatenate | solution.py:172
  181.6 57.9 %reduce-scatter.2.cloned.1.call-done = bf16[2176,256]{1,0:T(8,128)(2,1)} async-done(((bf16[2176,2048]{1,0:T(8,128)(2,1)}), bf16[2176,256]{1,0:T(8,128)(2,1)}) %reduce-scatter.2.cloned.1.call-update) | async-done | bytes 1114128 | tf_op jit(solution)/shard_map/reduce_scatter | solution.py:175
  239.5 1.2 slice-done
  240.7 1.1 copy.187
  241.8 10.1 %all-to-all-start.2 = ((bf16[32,2,32,256]{3,2,1,0:T(8,128)(2,1)}), bf16[32,2,32,256]{3,2,1,0:T(8,128)(2,1)S(1)}, u32[]{:S(2)}, u32[]{:S(2)}) async-start(bf16[32,2,32,256]{3,2,1,0:T(8,128)(2,1)} %bitcast.124), calls=%async_computation.3 | async-start | bytes 2097152 | tf_op jit(solution)/shard_map/all_to_all | solution.py:182
  252.2 0.3 fusion.36
  252.5 5.1 %gather_fusion = f32[768]{0:T(1024)S(1)} fusion(f32[128,64]{0,1:T(8,128)S(1)} %fusion.36, s32[768]{0:T(1024)S(1)} %reshape.246), kind=kCustom, calls=%fused_computation | custom fusion | bytes 12288 | tf_op jit(solution)/shard_map/jit(take_along_axis)/gather | solution.py:137
  257.9 1.8 select_reduce_fusion
  259.7 20.2 %all-to-all-done.2 = bf16[32,2,32,256]{3,2,1,0:T(8,128)(2,1)S(1)} async-done(((bf16[32,2,32,256]{3,2,1,0:T(8,128)(2,1)}), bf16[32,2,32,256]{3,2,1,0:T(8,128)(2,1)S(1)}, u32[]{:S(2)}, u32[]{:S(2)}) %all-to-all-start.2) | async-done | bytes 1048608 | tf_op jit(solution)/shard_map/all_to_all | solution.py:182
  279.8 2.9 fusion.29
  (84 shorter events, 2.7 us)
Async XLA Ops:
  7.2 30.8 %copy-start = (bf16[2048,384]{1,0:T(8,128)(2,1)S(1)}, bf16[2048,384]{1,0:T(8,128)(2,1)}, u32[]{:S(2)}) copy-start(bf16[2048,384]{1,0:T(8,128)(2,1)} %param.24) | copy-start | bytes 4718596
  7.2 29.1 %copy-start.17 = (bf16[512]{0:T(512)(128)(2,1)S(1)}, bf16[512]{0:T(512)(128)(2,1)}, u32[]{:S(2)}) copy-start(bf16[512]{0:T(512)(128)(2,1)} %param.26) | copy-start | bytes 3076
  7.2 29.1 %copy-start.16 = (s32[128]{0:T(128)S(1)}, s32[128]{0:T(128)}, u32[]{:S(2)}) copy-start(s32[128]{0:T(128)} %param.20) | copy-start | bytes 1540
  36.9 2.1 copy-start.12
  37.2 0.7 copy-start.10
  42.8 1.4 copy-start.1
  42.8 2.8 copy-start.20
  49.0 5.1 %copy-start.14 = (s32[128,6]{0,1:T(8,128)S(1)}, s32[128,6]{0,1:T(8,128)}, u32[]{:S(2)}) copy-start(s32[128,6]{0,1:T(8,128)} %param.21) | copy-start | bytes 9220
  49.0 7.8 %copy-start.15 = (bf16[2048]{0:T(1024)(128)(2,1)S(1)}, bf16[2048]{0:T(1024)(128)(2,1)}, u32[]{:S(2)}) copy-start(bf16[2048]{0:T(1024)(128)(2,1)} %param.30) | copy-start | bytes 12292
  49.0 15.4 %copy-start.13 = (bf16[128,256]{1,0:T(8,128)(2,1)S(1)}, bf16[128,256]{1,0:T(8,128)(2,1)}, u32[]{:S(2)}) copy-start(bf16[128,256]{1,0:T(8,128)(2,1)} %param.19) | copy-start | bytes 196612
  50.3 14.1 %all-to-all-start = ((bf16[8,128,256]{2,1,0:T(8,128)(2,1)}), bf16[8,128,256]{2,1,0:T(8,128)(2,1)S(1)}, u32[]{:S(2)}, u32[]{:S(2)}) async-start(bf16[8,128,256]{2,1,0:T(8,128)(2,1)} %fusion.20), calls=%async_computation | async-start | bytes 1048576 | tf_op jit(solution)/shard_map/all_to_all | solution.py:127
  54.1 111.8 %all-gather.3.cloned.1.call-start = ((), (), s32[]{:S(2)}) async-start(), calls=%async_computation.5 | async-start | bytes 9437184 | tf_op jit(solution)/shard_map/all_gather | solution.py:156
  64.4 13.6 %copy-start.5 = (pred[2048,128]{1,0:T(8,128)(4,1)S(1)}, pred[2048,128]{1,0:T(8,128)(4,1)}, u32[]{:S(2)}) copy-start(pred[2048,128]{1,0:T(8,128)(4,1)} %fusion.4) | copy-start | bytes 786436
  64.5 13.3 %copy-start.8 = (bf16[128,256]{1,0:T(8,128)(2,1)}, bf16[128,256]{1,0:T(8,128)(2,1)S(1)}, u32[]{:S(2)}) copy-start(bf16[128,256]{1,0:T(8,128)(2,1)S(1)} %add_convert_fusion) | copy-start | bytes 196612
  78.0 40.4 %copy-start.2 = (bf16[2,2048,176]{1,2,0:T(8,128)(2,1)S(1)}, bf16[2,2048,176]{1,2,0:T(8,128)(2,1)}, u32[]{:S(2)}) copy-start(bf16[2,2048,176]{1,2,0:T(8,128)(2,1)} %param.33) | copy-start | bytes 4325380
  118.2 121.2 %reduce-scatter.2.cloned.1.call-start = ((), (), s32[]{:S(2)}) async-start(), calls=%async_computation.4 | async-start | bytes 10027008 | tf_op jit(solution)/shard_map/reduce_scatter | solution.py:175
  118.5 1.7 copy-start.3
  120.1 1.5 copy-start.6
  120.1 1.9 copy-start.7
  165.9 6.3 %copy-start.4 = (bf16[44,8,8,256]{3,2,1,0:T(8,128)(2,1)S(1)}, bf16[44,8,8,256]{3,2,1,0:T(8,128)(2,1)}, u32[]{:S(2)}) copy-start(bf16[44,8,8,256]{3,2,1,0:T(8,128)(2,1)} %copy.167) | copy-start | bytes 4325380
  165.9 6.6 %copy-start.18 = (bf16[256,2,32,256]{3,2,1,0:T(8,128)(2,1)S(1)}, bf16[256,2,32,256]{3,2,1,0:T(8,128)(2,1)}, u32[]{:S(2)}) copy-start(bf16[256,2,32,256]{3,2,1,0:T(8,128)(2,1)} %all-gather.3.cloned.1.call-done) | copy-start | bytes 25165828
  172.5 2.4 copy-start.19
  239.5 1.2 slice-start
  240.7 11.5 %copy-start.11 = (bf16[2048,64]{0,1:T(8,128)(2,1)S(1)}, bf16[2048,64]{0,1:T(8,128)(2,1)}, u32[]{:S(2)}) copy-start(bf16[2048,64]{0,1:T(8,128)(2,1)} %param.31) | copy-start | bytes 786436
  241.8 38.0 %all-to-all-start.2 = ((bf16[32,2,32,256]{3,2,1,0:T(8,128)(2,1)}), bf16[32,2,32,256]{3,2,1,0:T(8,128)(2,1)S(1)}, u32[]{:S(2)}, u32[]{:S(2)}) async-start(bf16[32,2,32,256]{3,2,1,0:T(8,128)(2,1)} %bitcast.124), calls=%async_computation.3 | async-start | bytes 2097152 | tf_op jit(solution)/shard_map/all_to_all | solution.py:182
  252.5 27.3 %copy-start.9 = (bf16[128,256]{1,0:T(8,128)(2,1)S(1)}, bf16[128,256]{1,0:T(8,128)(2,1)}, u32[]{:S(2)}) copy-start(bf16[128,256]{1,0:T(8,128)(2,1)} %copy-done.8) | copy-start | bytes 196612
Sparse Core Ops, SparseCore 0:
  118.3 47.4 all-gather.2
  181.7 57.7 reduce-scatter.1
